TPU v7x, 256 devices: a whole 4x4x8 slice. The times are simulated.
256 devices in a mesh: ctx: 32 (over y, z), tp: 8 (over x, core).
Axes of the slice: x: 4, y: 4, z: 8, core: 2. Of those that a mesh axis runs over, the one named last changes fastest.
Arguments:
- queries: bfloat16 [32768, 4096], P('ctx', 'tp'), may hold values from -6 to 6
- keys: bfloat16 [32768, 4096], P('ctx', 'tp'), may hold values from -6 to 6
- values: bfloat16 [32768, 4096], P('ctx', 'tp'), may hold values from -128 to 128
- gates: bfloat16 [32768, 4096], P('ctx', 'tp'), may hold values from -6 to 6
- log_decay: float32 [32, 32768], P('tp', 'ctx'), may hold values from -1 to 0, as said below
- norm_gain: float32 [4096], P('tp'), may hold values from 0.1 to 1.9
- out_weight: bfloat16 [4096, 6144], P('tp'), may hold values from -0.09375 to 0.09375
Outputs:
- attended: bfloat16 [32768, 6144], P(('ctx', 'tp'))
Inputs may be any that keep to these rules, and one draw needn't show every extreme that they name: log_decay is negative everywhere.
All inputs are finite; a program needn't handle non-finite values.
Results may differ from a plain program's by a relative error of at most 0.017.
Values may be sent and summed in bfloat16 or wider, within the bound.
No kernel may reach another device: no remote copies, remote signals or barrier semaphores. Data moves between devices by JAX's collectives and lax.ppermute only.
A program may use at most 64 MiB of HBM per device.

v0:
```python
import jax
import jax.numpy as jnp
from jax import lax
from jax.sharding import PartitionSpec as P


def prefix(x, axis, join, neutral):
    place = lax.axis_index(axis)
    gathered = jax.tree.map(
        lambda a, kind: lax.all_gather(a.astype(kind), axis), x, (jnp.bfloat16, jnp.bfloat16)
    )
    state = jax.tree.map(lambda a, e: jnp.zeros_like(a) + jnp.asarray(e, a.dtype), x, neutral)

    def one(lap, state):
        return join(
            state,
            jax.tree.map(
                lambda a, own: lax.dynamic_index_in_dim(a, lap, 0, False).astype(own.dtype),
                gathered,
                x,
            ),
        )

    return lax.fori_loop(0, place, one, state)


def block_step(carry_state, block_inputs):
    query_blk, key_blk, value_blk, block_decay_factor = block_inputs
    block_cum = jnp.cumsum(block_decay_factor, axis=1)
    width_blk = block_decay_factor.shape[1]
    lower = jnp.arange(width_blk)[:, None] >= jnp.arange(width_blk)[None, :]
    spread = block_cum[:, :, None] - block_cum[:, None, :]
    factor = jnp.exp(jnp.where(lower[None], spread, -jnp.inf))
    scores = jnp.einsum("thd,shd->hts", query_blk, key_blk, preferred_element_type=jnp.float32)
    weighted = (scores * factor).astype(jnp.bfloat16)
    inside = jnp.einsum("hts,shd->thd", weighted, value_blk, preferred_element_type=jnp.float32)
    carried = jnp.exp(block_cum).T[:, :, None] * jnp.einsum(
        "thd,hde->the", query_blk.astype(jnp.float32), carry_state, precision=lax.Precision.HIGHEST
    )
    tail = jnp.exp(block_cum[:, -1:] - block_cum)
    key_decayed = key_blk.astype(jnp.float32) * tail.T[:, :, None]
    new_state = jnp.exp(block_cum[:, -1])[:, None, None] * carry_state + jnp.einsum(
        "shd,she->hde", key_decayed, value_blk.astype(jnp.float32), precision=lax.Precision.HIGHEST
    )
    return (new_state, inside + carried)


def chain_join(earlier, later):
    return (jnp.exp(later[1])[:, None, None] * earlier[0] + later[0], earlier[1] + later[1])


def on_device(queries, keys, values, gates, log_decay, norm_gain, out_weight):
    local_rows = queries.shape[0]
    head_count = log_decay.shape[0]
    head_width = queries.shape[1] // head_count
    width_blk = min(local_rows, 512)
    blocks = local_rows // width_blk
    query_third_block = queries.reshape(local_rows, head_count, head_width)
    query_r = queries.reshape(blocks, width_blk, head_count, head_width)
    key_r = keys.reshape(blocks, width_blk, head_count, head_width)
    value_r = values.reshape(blocks, width_blk, head_count, head_width)
    decay_r = log_decay.reshape(head_count, blocks, width_blk).transpose(1, 0, 2)
    zero_state = jnp.zeros((head_count, head_width, head_width), jnp.float32)
    local_state, attn = lax.scan(block_step, zero_state, (query_r, key_r, value_r, decay_r))
    attn = attn.reshape(local_rows, head_count, head_width)
    device_cum = jnp.cumsum(log_decay, axis=1)
    own_total = device_cum[:, -1]
    incoming, unused_total = prefix(
        (local_state, own_total), "ctx", chain_join, (zero_state, jnp.zeros_like(own_total))
    )
    from_before = jnp.exp(device_cum).T[:, :, None] * jnp.einsum(
        "thd,hde->the",
        query_third_block.astype(jnp.float32),
        incoming,
        precision=lax.Precision.HIGHEST,
    )
    attn = attn + from_before
    meansq = jnp.mean(attn * attn, axis=-1, keepdims=True)
    entire_gating_vector = jax.nn.sigmoid(
        gates.reshape(local_rows, head_count, head_width).astype(jnp.float32)
    )
    normed = (
        attn
        * lax.rsqrt(meansq + 1e-06)
        * norm_gain.reshape(head_count, head_width)
        * entire_gating_vector
    )
    normed = normed.astype(jnp.bfloat16).reshape(local_rows, head_count * head_width)
    return lax.psum_scatter(
        jnp.dot(normed, out_weight, preferred_element_type=jnp.float32).astype(jnp.bfloat16),
        "tp",
        scatter_dimension=0,
        tiled=True,
    )


def solution(mesh):
    placed = (
        P("ctx", "tp"),
        P("ctx", "tp"),
        P("ctx", "tp"),
        P("ctx", "tp"),
        P("tp", "ctx"),
        P("tp"),
        P("tp", None),
    )
    return jax.shard_map(
        on_device, mesh=mesh, in_specs=placed, out_specs=P(("ctx", "tp"), None), check_vma=False
    )
```

profile of v0, /device:TPU:1, one launch (start us, length us, event | category | flops | bytes accessed | tf_op | source)
XLA Modules:
  0.0 268.5 jit_solution(14431095850278082684)
XLA Ops:
  6.5 2.3 reshape.123
  8.8 1.1 reshape.124
  9.9 1.2 reshape.125
  11.1 41.7 %while.26 = (s32[]{:T(128)}, f32[4,128,128]{2,1,0:T(8,128)S(1)}, f32[2,512,4,128]{1,0,3,2:T(2,128)}, f32[2,4,512]{2,1,0:T(4,128)S(1)}, bf16[2,512,4,128]{3,2,1,0...) while((s32[]{:T(128)}, f32[4,128,128]{2,1,0:T(8,128)S(1)}, ...), condition=%wide.region_3.4_spmd.clone, body=%wide.region_0.3_spmd.clone.sunk | while | flops 1348208640 | bytes 31851160 | solution.py:64
  11.1 1.2 reduce-window.26
  12.4 0.2 slice_reduce_fusion.3
  12.5 0.2 reduce-window.27
  12.8 0.1 copy.104
  13.0 0.1 iota_compare_fusion.2
  13.1 1.2 constant_dynamic-slice_fusion.8
  14.4 1.6 constant_dynamic-slice_fusion.9
  15.9 1.9 fusion.26
  17.8 0.7 fusion.27
  18.5 1.3 convolution_add_fusion.2
  19.8 1.1 copy.105
  20.9 9.7 %dynamic_update_slice.6 = f32[2,512,4,128]{1,0,3,2:T(2,128)S(1)} dynamic-update-slice(f32[2,512,4,128]{1,0,3,2:T(2,128)S(1)} %copy-done.2, f32[1,512,4,128]{1,0,3,2:T(1,128)S(1)} %copy.105, s32[]{:T(128)S(6)} %copy.110, s32[]{:T(128)} %constant.50.clone.1..sunk.1, s32[]{:T(128)} %constant.50.clone.1..sunk.1, s32[]{:T(128)} %constant.50.clone.1..sunk.1) | dynamic-update-slice | bytes 2097156 | tf_op jit(solution)/shard_map/while/body/jit(dynamic_update_index_in_dim)/dynamic_update_slice | solution.py:64
  30.6 1.3 copy-done.3
  32.0 1.2 reduce-window.26
  33.2 0.2 slice_reduce_fusion.3
  33.3 0.2 reduce-window.27
  33.7 0.1 copy.104
  33.9 0.1 iota_compare_fusion.2
  34.0 1.2 constant_dynamic-slice_fusion.8
  35.2 1.6 constant_dynamic-slice_fusion.9
  36.8 1.9 fusion.26
  38.6 0.7 fusion.27
  39.3 1.3 convolution_add_fusion.2
  40.7 1.1 copy.105
  41.8 9.7 %dynamic_update_slice.6 = f32[2,512,4,128]{1,0,3,2:T(2,128)S(1)} dynamic-update-slice(f32[2,512,4,128]{1,0,3,2:T(2,128)S(1)} %copy-done.2, f32[1,512,4,128]{1,0,3,2:T(1,128)S(1)} %copy.105, s32[]{:T(128)S(6)} %copy.110, s32[]{:T(128)} %constant.50.clone.1..sunk.1, s32[]{:T(128)} %constant.50.clone.1..sunk.1, s32[]{:T(128)} %constant.50.clone.1..sunk.1) | dynamic-update-slice | bytes 2097156 | tf_op jit(solution)/shard_map/while/body/jit(dynamic_update_index_in_dim)/dynamic_update_slice | solution.py:64
  51.5 1.3 copy-done.3
  52.8 0.7 convert_element_type.50
  53.6 1.1 reduce-window.16
  54.7 0.2 slice_reduce_fusion.1
  54.9 0.2 reduce-window.17
  55.1 0.2 copy.43
  55.4 0.6 dynamic-slice
  56.6 0.2 dynamic-update-slice
  56.9 65.0 %all-reduce = bf16[128]{0:T(256)(128)(2,1)S(1)} all-reduce(bf16[128]{0:T(256)(128)(2,1)S(1)} %dynamic-update-slice), channel_id=2, replica_groups=mesh['ctx'=32,'tp'=8] {'ctx'}, use_global_device_ids=true, to_apply=%add | all-reduce | flops 128 | bytes 512
  121.9 0.1 reshape.136
  122.0 3.2 %add_divide_fusion = f32[1024,512]{1,0:T(8,128)} fusion(bf16[1024,512]{1,0:T(8,128)(2,1)} %param.14), kind=kLoop, calls=%fused_computation.36 | loop fusion | flops 2097152 | bytes 3145728 | tf_op jit(solution)/shard_map/div | solution.py:79
  125.2 1.9 copy.38
  127.1 4.2 %reshape.126 = f32[1024,4,128]{0,2,1:T(8,128)} reshape(f32[2,512,4,128]{1,0,3,2:T(2,128)} %get-tuple-element.87) | data formatting | bytes 4194304 | tf_op jit(solution)/shard_map/reshape | solution.py:65
  131.3 4.5 %all-gather.4.cloned.1.call-done = bf16[128,128,128]{2,1,0:T(8,128)(2,1)} async-done(((bf16[4,128,128]{2,1,0:T(8,128)(2,1)}), bf16[128,128,128]{2,1,0:T(8,128)(2,1)}) %all-gather.4.cloned.1.call-update) | async-done | bytes 4194320 | tf_op jit(solution)/shard_map/all_gather | solution.py:10
  135.8 0.2 while.25
  136.0 2.9 %multiply_reduce_fusion = (f32[1024,4]{0,1:T(4,128)S(1)}, f32[1024,4,128]{0,2,1:T(8,128)S(1)}) fusion(f32[1024,4,128]{0,2,1:T(8,128)} %reshape.126, f32[4,128,128]{2,1,0:T(8,128)S(1)} %get-tuple-element.89, f32[1024,4]{0,1:T(4,128)S(1)} %bitcast.136, bf16[1024,512]{1,0:T(8,128)(2,1)S(1)} %copy-done.1), kind=kOutput, calls=%fused_computation.37 | convolution fusion | flops 807399424 | bytes 5537792 | tf_op jit(solution)/shard_map/thd,hde->the/dot_general | solution.py:71
  139.0 0.4 multiply_convert_fusion.1
  139.3 12.5 %convolution_convert_fusion = bf16[1024,6144]{1,0:T(8,128)(2,1)} fusion(bf16[1024,512]{0,1:T(8,128)(2,1)S(1)} %bitcast.128, bf16[512,6144]{1,0:T(8,128)(2,1)} %param.17), kind=kOutput, calls=%fused_computation.32 | convolution fusion | flops 6448742400 | bytes 19922944 | tf_op jit(solution)/shard_map/dot_general | solution.py:90
  151.8 109.8 %reduce-scatter.2.cloned.1.call-done = bf16[128,6144]{1,0:T(8,128)(2,1)} async-done(((bf16[1024,6144]{1,0:T(8,128)(2,1)}), bf16[128,6144]{1,0:T(8,128)(2,1)}) %reduce-scatter.2.cloned.1.call-update) | async-done | bytes 1572880 | tf_op jit(solution)/shard_map/reduce_scatter | solution.py:89
  (45 shorter events, 0.8 us)
Async XLA Ops:
  6.5 2.3 copy-start.4
  6.5 129.3 %all-gather.4.cloned.1.call-start = ((), (), s32[]{:S(2)}) async-start(), calls=%async_computation.2 | async-start | bytes 4325376 | tf_op jit(solution)/shard_map/all_gather | solution.py:10
  6.5 3.4 %copy-start = (bf16[1024,512]{1,0:T(8,128)(2,1)S(1)}, bf16[1024,512]{1,0:T(8,128)(2,1)}, u32[]{:S(2)}) copy-start(bf16[1024,512]{1,0:T(8,128)(2,1)} %param.11) | copy-start | bytes 3145732
  8.8 2.3 copy-start.5
  11.1 44.2 %copy-start.7 = (u32[256]{0:T(256)S(1)}, u32[256]{0:T(256)}, u32[]{:S(2)}) copy-start(u32[256]{0:T(256)} %constant.60) | copy-start | bytes 3076
  18.5 2.5 copy-start.2
  30.6 1.3 copy-start.3
  39.3 2.5 copy-start.2
  51.4 1.3 copy-start.3
  53.5 208.2 %reduce-scatter.2.cloned.1.call-start = ((), (), s32[]{:S(2)}) async-start(), calls=%async_computation.1 | async-start | bytes 14155776 | tf_op jit(solution)/shard_map/reduce_scatter | solution.py:89
  127.1 8.9 %copy-start.1 = (bf16[1024,512]{1,0:T(8,128)(2,1)S(1)}, bf16[1024,512]{1,0:T(8,128)(2,1)}, u32[]{:S(2)}) copy-start(bf16[1024,512]{1,0:T(8,128)(2,1)} %param.11) | copy-start | bytes 3145732
  136.0 2.9 %copy-start.6 = (f32[512]{0:T(512)S(1)}, f32[512]{0:T(512)}, u32[]{:S(2)}) copy-start(f32[512]{0:T(512)} %param.16) | copy-start | bytes 6148
Sparse Core Ops, SparseCore 0:
  53.6 82.1 all-gather.3
  151.9 109.6 reduce-scatter.1
where the time goes:
time: 269 us
  waiting for transfers between devices  114 us (42%)
  blocking collectives  65 us (24%)
  local copies, waits for them, and re-layouts  42.5 us (16%)
  matrix products  23.1 us (9%)
  between operations  14.1 us (5%)
  other arithmetic  8.89 us (3%)
    reduce_scatter x1, waiting for transfers between devices, on_device(): lax.psum_scatter(jnp.dot(normed, out_weight, preferred_element_type=jnp.f...  110 us
    unnamed x1, blocking collectives  65 us
    dynamic_update_slice x4, local copies, waits for them, and re-layouts, on_device(): lax.scan(block_step, zero_state, (query_r, key_r, value_r, decay_r))  21.5 us
    dot_general x1, matrix products, on_device(): jnp.dot(normed, out_weight, preferred_element_type=jnp.float32)  12.5 us
    dynamic_slice x6, local copies, waits for them, and re-layouts, on_device(): lax.scan(block_step, zero_state, (query_r, key_r, value_r, decay_r))  5.6 us
  transfers between devices with their start and end apart: 2, of which 2 were waited for; matrix products, arithmetic and copies ran while one was open for 4% of the time, Pallas kernels for 0%

commit v1 on v0

v1 whole, which is shorter than its diff:
```python
import jax
import jax.numpy as jnp
from jax import lax
from jax.sharding import PartitionSpec as P


def chain_join(earlier, later):
    return (jnp.exp(later[1])[:, None, None] * earlier[0] + later[0], earlier[1] + later[1])


def exclusive_prefix(state, total, axis):
    n = lax.axis_size(axis)

    def shifted(x, s):
        return lax.ppermute(x, axis, [(i, i + s) for i in range(n - s)])

    acc = (shifted(state, 1), shifted(total, 1))
    s = 1
    while s < n:
        got = (shifted(acc[0], s), shifted(acc[1], s))
        acc = chain_join(got, acc)
        s *= 2
    return acc[0]


def on_device(queries, keys, values, gates, log_decay, norm_gain, out_weight):
    local_rows = queries.shape[0]
    head_count = log_decay.shape[0]
    head_width = queries.shape[1] // head_count
    width_blk = min(local_rows, 512)
    blocks = local_rows // width_blk
    hp = lax.Precision.HIGHEST

    q = queries.reshape(blocks, width_blk, head_count, head_width)
    k = keys.reshape(blocks, width_blk, head_count, head_width)
    v = values.reshape(blocks, width_blk, head_count, head_width)
    decay = log_decay.reshape(head_count, blocks, width_blk).transpose(1, 0, 2)
    cum = jnp.cumsum(decay, axis=2)
    last = cum[:, :, -1]

    tail = jnp.exp(last[:, :, None] - cum)
    key_decayed = k.astype(jnp.float32) * tail.transpose(0, 2, 1)[:, :, :, None]
    block_state = jnp.einsum(
        "bshd,bshe->bhde", key_decayed, v.astype(jnp.float32), precision=hp
    )

    carries = []
    run = jnp.zeros((head_count, head_width, head_width), jnp.float32)
    before = jnp.zeros((head_count,), jnp.float32)
    offsets = []
    for b in range(blocks):
        carries.append(run)
        offsets.append(before)
        run = jnp.exp(last[b])[:, None, None] * run + block_state[b]
        before = before + last[b]
    local_state = run
    own_total = before

    incoming = exclusive_prefix(local_state, own_total, "ctx")

    lower = jnp.arange(width_blk)[:, None] >= jnp.arange(width_blk)[None, :]
    spread = cum[:, :, :, None] - cum[:, :, None, :]
    factor = jnp.exp(jnp.where(lower[None, None], spread, -jnp.inf))
    scores = jnp.einsum("bthd,bshd->bhts", q, k, preferred_element_type=jnp.float32)
    weighted = (scores * factor).astype(jnp.bfloat16)
    inside = jnp.einsum("bhts,bshd->bthd", weighted, v, preferred_element_type=jnp.float32)

    carry_all = jnp.stack(
        [carries[b] + jnp.exp(offsets[b])[:, None, None] * incoming for b in range(blocks)]
    )
    carried = jnp.exp(cum).transpose(0, 2, 1)[:, :, :, None] * jnp.einsum(
        "bthd,bhde->bthe", q.astype(jnp.float32), carry_all, precision=hp
    )
    attn = (inside + carried).reshape(local_rows, head_count, head_width)

    meansq = jnp.mean(attn * attn, axis=-1, keepdims=True)
    gate = jax.nn.sigmoid(gates.reshape(local_rows, head_count, head_width).astype(jnp.float32))
    normed = attn * lax.rsqrt(meansq + 1e-06) * norm_gain.reshape(head_count, head_width) * gate
    normed = normed.astype(jnp.bfloat16).reshape(local_rows, head_count * head_width)
    return lax.psum_scatter(
        jnp.dot(normed, out_weight, preferred_element_type=jnp.float32).astype(jnp.bfloat16),
        "tp",
        scatter_dimension=0,
        tiled=True,
    )


def solution(mesh):
    placed = (
        P("ctx", "tp"),
        P("ctx", "tp"),
        P("ctx", "tp"),
        P("ctx", "tp"),
        P("tp", "ctx"),
        P("tp"),
        P("tp", None),
    )
    return jax.shard_map(
        on_device, mesh=mesh, in_specs=placed, out_specs=P(("ctx", "tp"), None), check_vma=False
    )
```

time: 269 us -> 207 us (0.77)
  blocking collectives: 65 us -> 0 us
  starting transfers between devices: 0.04 us -> 64.2 us
  local copies, waits for them, and re-layouts: 42.5 us -> 8.51 us
  waiting for transfers between devices: 114 us -> 92.8 us
  other arithmetic: 8.89 us -> 3.68 us
    unnamed x1 -> x0, blocking collectives: 65 us -> none
    ppermute x0 -> x11, starting transfers between devices: none -> 64.2 us  [shifted(): return lax.ppermute(x, axis, [(i, i + s) for i in range(n - s)])]
    reduce_scatter x1, waiting for transfers between devices: 110 us -> 72.2 us  [on_device(): lax.psum_scatter(jnp.dot(normed, out_weight, preferred_element_type=jnp.f...]
    dynamic_update_slice x4 -> x0, local copies, waits for them, and re-layouts: 21.5 us -> none  [on_device(): lax.scan(block_step, zero_state, (query_r, key_r, value_r, decay_r))]
    ppermute x0 -> x11, waiting for transfers between devices: none -> 20.6 us  [shifted(): return lax.ppermute(x, axis, [(i, i + s) for i in range(n - s)])]
    dynamic_slice x6 -> x0, local copies, waits for them, and re-layouts: 5.6 us -> none  [on_device(): lax.scan(block_step, zero_state, (query_r, key_r, value_r, decay_r))]
    all_gather x1 -> x0, waiting for transfers between devices: 4.52 us -> none  [prefix(): lax.all_gather(a.astype(kind), axis)]
    reshape x6 -> x7, local copies, waits for them, and re-layouts: 8.75 us -> 4.24 us  [the longest x2 1.74 us: on_device(): k = keys.reshape(blocks, width_blk, head_count, head_width)]
  transfers between devices with their start and end apart: 2 -> 12, of which waited for: 2 -> 9; matrix products, arithmetic and copies ran while one was open for 4% -> 3% of each run, Pallas kernels for 0% -> 0%
where the time goes in v1:
time: 207 us
  waiting for transfers between devices  92.8 us (45%)
  starting transfers between devices  64.2 us (31%)
  matrix products  23.7 us (11%)
  between operations  13.6 us (7%)
  local copies, waits for them, and re-layouts  8.51 us (4%)
  other arithmetic  3.68 us (2%)
    reduce_scatter x1, waiting for transfers between devices, on_device(): lax.psum_scatter(jnp.dot(normed, out_weight, preferred_element_type=jnp.f...  72.2 us
    ppermute x11, starting transfers between devices, shifted(): return lax.ppermute(x, axis, [(i, i + s) for i in range(n - s)])  64.2 us
    ppermute x11, waiting for transfers between devices, shifted(): return lax.ppermute(x, axis, [(i, i + s) for i in range(n - s)])  20.6 us
    dot_general x1, matrix products, on_device(): jnp.dot(normed, out_weight, preferred_element_type=jnp.float32)  11.9 us
    dot_general x1, matrix products, on_device(): jnp.einsum('bhts,bshd->bthd', weighted, v, preferred_element_type=jnp.flo...  6.41 us
  transfers between devices with their start and end apart: 12, of which 9 were waited for; matrix products, arithmetic and copies ran while one was open for 3% of the time, Pallas kernels for 0%

profile of v1, /device:TPU:1, one launch (start us, length us, event | category | flops | bytes accessed | tf_op | source)
XLA Modules:
  0.0 206.5 jit_solution(9075946358202262627)
XLA Ops:
  6.5 0.8 reshape.111
  7.4 2.4 %reduce-window.6 = f32[2,4,4,128]{3,2,1,0:T(4,128)S(1)} reduce-window(f32[2,4,4,128]{3,2,1,0:T(4,128)S(1)} %copy.53, f32[]{:T(128)} %constant.5.clone.1), window={size=1x1x1x128 pad=0_0x0_0x0_0x127_0}, to_apply=%region_0.0 | reduce-window | flops 520192 | bytes 32772 | tf_op jit(solution)/shard_map/reduce-window
  9.8 0.2 slice_reduce_fusion
  10.0 0.4 reduce-window.9
  10.4 0.1 broadcast_add_fusion
  10.6 0.1 copy.56
  10.7 0.1 copy.55
  10.8 0.1 copy.54
  10.9 0.1 exponential_bitcast_fusion
  11.0 1.3 reshape.114
  12.4 0.3 reshape.110
  12.7 1.5 copy.45
  14.1 2.5 %fusion.11 = f32[2,4,128,128]{3,2,1,0:T(8,128)S(1)} fusion(bf16[2,512,4,128]{1,3,2,0:T(8,128)(2,1)} %copy.45, f32[2,512,4]{1,2,0:T(4,128)S(1)} %get-tuple-element.15, bf16[2,512,4,128]{3,2,1,0:T(4,128)(2,1)S(1)} %reshape.114), kind=kOutput, calls=%fused_computation.15 | convolution fusion | flops 806354944 | bytes 2637824 | tf_op jit(solution)/shard_map/bshd,bshe->bhde/dot_general | solution.py:43
  16.7 0.1 fusion.26
  16.8 4.5 %collective-permute-start.5 = (f32[4,128,128]{2,1,0:T(8,128)S(1)}, f32[4,128,128]{2,1,0:T(8,128)S(1)}, u32[]{:S(2)}, u32[]{:S(2)}) collective-permute-start(f32[4,128,128]{2,1,0:T(8,128)S(1)} %fusion.26), channel_id=1, source_target_pairs={{0,8},{8,16},{16,24},{24,32},{32,40},{40,48},{48,56},{56,64},{64,7... | collective-permute-start | bytes 786440 | tf_op jit(solution)/shard_map/ppermute | solution.py:15
  21.3 5.0 %collective-permute-done.5 = f32[4,128,128]{2,1,0:T(8,128)S(1)} collective-permute-done((f32[4,128,128]{2,1,0:T(8,128)S(1)}, f32[4,128,128]{2,1,0:T(8,128)S(1)}, u32[]{:S(2)}, u32[]{:S(2)}) %collective-permute-start.5) | collective-permute-done | bytes 262176 | tf_op jit(solution)/shard_map/ppermute | solution.py:15
  26.3 4.1 %collective-permute-start.6 = (f32[4,128,128]{2,1,0:T(8,128)S(1)}, f32[4,128,128]{2,1,0:T(8,128)S(1)}, u32[]{:S(2)}, u32[]{:S(2)}) collective-permute-start(f32[4,128,128]{2,1,0:T(8,128)S(1)} %collective-permute-done.5), channel_id=1, source_target_pairs={{0,8},{8,16},{16,24},{24,32},{32,40},{40,48},{48,56},{56,64},{64,7... | collective-permute-start | bytes 786440 | tf_op jit(solution)/shard_map/ppermute | solution.py:15
  30.4 3.5 %collective-permute-start = (f32[4]{0:T(128)S(1)}, f32[4]{0:T(128)S(1)}, u32[]{:S(2)}, u32[]{:S(2)}) collective-permute-start(f32[4]{0:T(128)S(1)} %get-tuple-element.18), channel_id=1, source_target_pairs={{0,8},{8,16},{16,24},{24,32},{32,40},{40,48},{48,56},{56,64},{64,7... | collective-permute-start | bytes 56 | tf_op jit(solution)/shard_map/ppermute | solution.py:15
  33.9 0.7 collective-permute-done
  34.6 4.2 %collective-permute-start.1 = (f32[4]{0:T(128)S(1)}, f32[4]{0:T(128)S(1)}, u32[]{:S(2)}, u32[]{:S(2)}) collective-permute-start(f32[4]{0:T(128)S(1)} %collective-permute-done), channel_id=1, source_target_pairs={{0,8},{8,16},{16,24},{24,32},{32,40},{40,48},{48,56},{56,64},{64,7... | collective-permute-start | bytes 56 | tf_op jit(solution)/shard_map/ppermute | solution.py:15
  38.8 0.7 collective-permute-done.1
  39.5 0.1 multiply_add_fusion.4
  39.6 7.0 %collective-permute-start.7 = (f32[4,128,128]{2,1,0:T(8,128)S(1)}, f32[4,128,128]{2,1,0:T(8,128)S(1)}, u32[]{:S(2)}, u32[]{:S(2)}) collective-permute-start(f32[4,128,128]{2,1,0:T(8,128)S(1)} %multiply_add_fusion.4), channel_id=1, source_target_pairs={{0,16},{8,24},{16,32},{24,40},{32,48},{40,56},{48,64},{56,72},{64,... | collective-permute-start | bytes 786440 | tf_op jit(solution)/shard_map/ppermute | solution.py:15
  46.7 3.3 %collective-permute-done.7 = f32[4,128,128]{2,1,0:T(8,128)S(1)} collective-permute-done((f32[4,128,128]{2,1,0:T(8,128)S(1)}, f32[4,128,128]{2,1,0:T(8,128)S(1)}, u32[]{:S(2)}, u32[]{:S(2)}) %collective-permute-start.7) | collective-permute-done | bytes 262176 | tf_op jit(solution)/shard_map/ppermute | solution.py:15
  50.0 0.1 multiply_add_fusion.3
  50.1 18.5 %collective-permute-start.8 = (f32[4,128,128]{2,1,0:T(8,128)S(1)}, f32[4,128,128]{2,1,0:T(8,128)S(1)}, u32[]{:S(2)}, u32[]{:S(2)}) collective-permute-start(f32[4,128,128]{2,1,0:T(8,128)S(1)} %multiply_add_fusion.3), channel_id=1, source_target_pairs={{0,32},{8,40},{16,48},{24,56},{32,64},{40,72},{48,80},{56,88},{64,... | collective-permute-start | bytes 786440 | tf_op jit(solution)/shard_map/ppermute | solution.py:15
  68.6 1.3 collective-permute-start.2
  69.9 8.7 %collective-permute-done.2 = f32[4]{0:T(128)S(1)} collective-permute-done((f32[4]{0:T(128)S(1)}, f32[4]{0:T(128)S(1)}, u32[]{:S(2)}, u32[]{:S(2)}) %collective-permute-start.2) | collective-permute-done | bytes 48 | tf_op jit(solution)/shard_map/ppermute | solution.py:15
  78.6 0.1 multiply_add_fusion.2
  78.7 7.0 %collective-permute-start.9 = (f32[4,128,128]{2,1,0:T(8,128)S(1)}, f32[4,128,128]{2,1,0:T(8,128)S(1)}, u32[]{:S(2)}, u32[]{:S(2)}) collective-permute-start(f32[4,128,128]{2,1,0:T(8,128)S(1)} %multiply_add_fusion.2), channel_id=1, source_target_pairs={{0,64},{8,72},{16,80},{24,88},{32,96},{40,104},{48,112},{56,120},{... | collective-permute-start | bytes 786440 | tf_op jit(solution)/shard_map/ppermute | solution.py:15
  85.7 0.1 iota_compare_fusion
  85.8 0.3 reshape.109
  86.1 2.4 %collective-permute-start.3 = (f32[4]{0:T(128)S(1)}, f32[4]{0:T(128)S(1)}, u32[]{:S(2)}, u32[]{:S(2)}) collective-permute-start(f32[4]{0:T(128)S(1)} %get-tuple-element.8), channel_id=1, source_target_pairs={{0,32},{8,40},{16,48},{24,56},{32,64},{40,72},{48,80},{56,88},{64,... | collective-permute-start | bytes 56 | tf_op jit(solution)/shard_map/ppermute | solution.py:15
  88.5 0.7 collective-permute-done.3
  89.2 0.8 collective-permute-done.9
  90.1 0.1 multiply_add_fusion.1
  90.1 10.3 %collective-permute-start.10 = (f32[4,128,128]{2,1,0:T(8,128)S(1)}, f32[4,128,128]{2,1,0:T(8,128)S(1)}, u32[]{:S(2)}, u32[]{:S(2)}) collective-permute-start(f32[4,128,128]{2,1,0:T(8,128)S(1)} %multiply_add_fusion.1), channel_id=1, source_target_pairs={{0,128},{8,136},{16,144},{24,152},{32,160},{40,168},{48,176},{56,1... | collective-permute-start | bytes 786440 | tf_op jit(solution)/shard_map/ppermute | solution.py:15
  100.5 6.4 %fusion = f32[2,4,512,128]{2,3,1,0:T(8,128)} fusion(f32[2,4,512]{2,1,0:T(4,128)S(1)} %reduce_window_sum.24, pred[512,512]{1,0:T(8,128)(4,1)S(1)} %iota_compare_fusion, bf16[2,512,4,128]{1,3,2,0:T(8,128)(2,1)} %copy.45, bf16[2,512,4,128]{3,2,1,0:T(4,128)(2,1)} %copy-done.3, bf16[2,512,4,128]{3,2,1,0:T(4,128)(2,1)S(1)} %reshape.109), kind=kOutput, calls=%fused_computation.2 | convolution fusion | flops 1082130432 | bytes 5521408 | tf_op jit(solution)/shard_map/bhts,bshd->bthd/dot_general | solution.py:66
  106.9 1.3 collective-permute-start.4
  108.2 0.7 collective-permute-done.4
  108.9 0.1 fusion.28
  109.0 2.9 %multiply_reduce_fusion = (f32[2,512,4]{1,2,0:T(4,128)S(1)}, f32[2,512,4,128]{1,3,2,0:T(8,128)S(1)}) fusion(bf16[2,512,4,128]{3,2,1,0:T(4,128)(2,1)S(1)} %reshape.109, f32[1,4,128,128]{3,2,1,0:T(8,128)S(1)} %get-tuple-element.12, f32[1,4,128,128]{3,2,1,0:T(8,128)S(1)} %get-tuple-element.11, f32[2,512,4]{1,2,0:T(4,128)S(1)} %get-tuple-element.16, ...), kind=kOutput, calls=%fused_computation.14 | convolution fusion | flops 807530496 | bytes 5799936 | tf_op jit(solution)/shard_map/bthd,bhde->bthe/dot_general | solution.py:71
  111.9 0.2 copy.51
  112.1 1.8 copy.50
  114.0 1.2 mul.134
  115.2 0.4 copy-done
  115.6 11.9 %convolution_convert_fusion = bf16[1024,6144]{1,0:T(8,128)(2,1)} fusion(bf16[512,6144]{1,0:T(8,128)(2,1)} %param.13, f32[128,8,4,128]{3,2,1,0:T(4,128)S(1)} %bitcast.57, f32[128,8,4,128]{3,2,1,0:T(4,128)S(1)} %bitcast.58, bf16[1024,512]{1,0:T(8,128)(2,1)} %param.10, f32[512]{0:T(512)S(1)} %copy-done.4), kind=kOutput, calls=%fused_computation | convolution fusion | flops 6452936704 | bytes 24119296 | tf_op jit(solution)/shard_map/dot_general | solution.py:81
  127.5 72.2 %reduce-scatter.2.cloned.1.call-done = bf16[128,6144]{1,0:T(8,128)(2,1)} async-done(((bf16[1024,6144]{1,0:T(8,128)(2,1)}), bf16[128,6144]{1,0:T(8,128)(2,1)}) %reduce-scatter.2.cloned.1.call-update) | async-done | bytes 1572880 | tf_op jit(solution)/shard_map/reduce_scatter | solution.py:80
  (26 shorter events, 0.3 us)
Async XLA Ops:
  6.5 5.8 %copy-start.1 = (bf16[1024,512]{1,0:T(8,128)(2,1)S(1)}, bf16[1024,512]{1,0:T(8,128)(2,1)}, u32[]{:S(2)}) copy-start(bf16[1024,512]{1,0:T(8,128)(2,1)} %param.8) | copy-start | bytes 3145732
  6.5 193.1 %reduce-scatter.2.cloned.1.call-start = ((), (), s32[]{:S(2)}) async-start(), calls=%async_computation.1 | async-start | bytes 14155776 | tf_op jit(solution)/shard_map/reduce_scatter | solution.py:80
  12.4 1.8 copy-start.3
  16.7 69.1 %copy-start.2 = (bf16[1024,512]{1,0:T(8,128)(2,1)S(1)}, bf16[1024,512]{1,0:T(8,128)(2,1)}, u32[]{:S(2)}) copy-start(bf16[1024,512]{1,0:T(8,128)(2,1)} %param.7) | copy-start | bytes 3145732
  16.8 9.5 %collective-permute-start.5 = (f32[4,128,128]{2,1,0:T(8,128)S(1)}, f32[4,128,128]{2,1,0:T(8,128)S(1)}, u32[]{:S(2)}, u32[]{:S(2)}) collective-permute-start(f32[4,128,128]{2,1,0:T(8,128)S(1)} %fusion.26), channel_id=1, source_target_pairs={{0,8},{8,16},{16,24},{24,32},{32,40},{40,48},{48,56},{56,64},{64,7... | collective-permute-start | bytes 786440 | tf_op jit(solution)/shard_map/ppermute | solution.py:15
  26.3 13.3 %collective-permute-start.6 = (f32[4,128,128]{2,1,0:T(8,128)S(1)}, f32[4,128,128]{2,1,0:T(8,128)S(1)}, u32[]{:S(2)}, u32[]{:S(2)}) collective-permute-start(f32[4,128,128]{2,1,0:T(8,128)S(1)} %collective-permute-done.5), channel_id=1, source_target_pairs={{0,8},{8,16},{16,24},{24,32},{32,40},{40,48},{48,56},{56,64},{64,7... | collective-permute-start | bytes 786440 | tf_op jit(solution)/shard_map/ppermute | solution.py:15
  30.4 4.2 %collective-permute-start = (f32[4]{0:T(128)S(1)}, f32[4]{0:T(128)S(1)}, u32[]{:S(2)}, u32[]{:S(2)}) collective-permute-start(f32[4]{0:T(128)S(1)} %get-tuple-element.18), channel_id=1, source_target_pairs={{0,8},{8,16},{16,24},{24,32},{32,40},{40,48},{48,56},{56,64},{64,7... | collective-permute-start | bytes 56 | tf_op jit(solution)/shard_map/ppermute | solution.py:15
  34.6 4.9 %collective-permute-start.1 = (f32[4]{0:T(128)S(1)}, f32[4]{0:T(128)S(1)}, u32[]{:S(2)}, u32[]{:S(2)}) collective-permute-start(f32[4]{0:T(128)S(1)} %collective-permute-done), channel_id=1, source_target_pairs={{0,8},{8,16},{16,24},{24,32},{32,40},{40,48},{48,56},{56,64},{64,7... | collective-permute-start | bytes 56 | tf_op jit(solution)/shard_map/ppermute | solution.py:15
  39.6 10.3 %collective-permute-start.7 = (f32[4,128,128]{2,1,0:T(8,128)S(1)}, f32[4,128,128]{2,1,0:T(8,128)S(1)}, u32[]{:S(2)}, u32[]{:S(2)}) collective-permute-start(f32[4,128,128]{2,1,0:T(8,128)S(1)} %multiply_add_fusion.4), channel_id=1, source_target_pairs={{0,16},{8,24},{16,32},{24,40},{32,48},{40,56},{48,64},{56,72},{64,... | collective-permute-start | bytes 786440 | tf_op jit(solution)/shard_map/ppermute | solution.py:15
  50.1 28.5 %collective-permute-start.8 = (f32[4,128,128]{2,1,0:T(8,128)S(1)}, f32[4,128,128]{2,1,0:T(8,128)S(1)}, u32[]{:S(2)}, u32[]{:S(2)}) collective-permute-start(f32[4,128,128]{2,1,0:T(8,128)S(1)} %multiply_add_fusion.3), channel_id=1, source_target_pairs={{0,32},{8,40},{16,48},{24,56},{32,64},{40,72},{48,80},{56,88},{64,... | collective-permute-start | bytes 786440 | tf_op jit(solution)/shard_map/ppermute | solution.py:15
  68.6 10.0 %collective-permute-start.2 = (f32[4]{0:T(128)S(1)}, f32[4]{0:T(128)S(1)}, u32[]{:S(2)}, u32[]{:S(2)}) collective-permute-start(f32[4]{0:T(128)S(1)} %get-tuple-element.10), channel_id=1, source_target_pairs={{0,16},{8,24},{16,32},{24,40},{32,48},{40,56},{48,64},{56,72},{64,... | collective-permute-start | bytes 56 | tf_op jit(solution)/shard_map/ppermute | solution.py:15
  78.7 11.4 %collective-permute-start.9 = (f32[4,128,128]{2,1,0:T(8,128)S(1)}, f32[4,128,128]{2,1,0:T(8,128)S(1)}, u32[]{:S(2)}, u32[]{:S(2)}) collective-permute-start(f32[4,128,128]{2,1,0:T(8,128)S(1)} %multiply_add_fusion.2), channel_id=1, source_target_pairs={{0,64},{8,72},{16,80},{24,88},{32,96},{40,104},{48,112},{56,120},{... | collective-permute-start | bytes 786440 | tf_op jit(solution)/shard_map/ppermute | solution.py:15
  86.1 3.2 %collective-permute-start.3 = (f32[4]{0:T(128)S(1)}, f32[4]{0:T(128)S(1)}, u32[]{:S(2)}, u32[]{:S(2)}) collective-permute-start(f32[4]{0:T(128)S(1)} %get-tuple-element.8), channel_id=1, source_target_pairs={{0,32},{8,40},{16,48},{24,56},{32,64},{40,72},{48,80},{56,88},{64,... | collective-permute-start | bytes 56 | tf_op jit(solution)/shard_map/ppermute | solution.py:15
  90.1 18.8 %collective-permute-start.10 = (f32[4,128,128]{2,1,0:T(8,128)S(1)}, f32[4,128,128]{2,1,0:T(8,128)S(1)}, u32[]{:S(2)}, u32[]{:S(2)}) collective-permute-start(f32[4,128,128]{2,1,0:T(8,128)S(1)} %multiply_add_fusion.1), channel_id=1, source_target_pairs={{0,128},{8,136},{16,144},{24,152},{32,160},{40,168},{48,176},{56,1... | collective-permute-start | bytes 786440 | tf_op jit(solution)/shard_map/ppermute | solution.py:15
  106.9 2.0 collective-permute-start.4
  114.0 1.6 copy-start
  114.0 1.6 copy-start.4
Sparse Core Ops, SparseCore 0:
  127.6 72.0 reduce-scatter.1

commit v2 on v1

--- a/solution.py
+++ b/solution.py
@@ -4,23 +4,26 @@
 from jax.sharding import PartitionSpec as P
 
 
-def chain_join(earlier, later):
-    return (jnp.exp(later[1])[:, None, None] * earlier[0] + later[0], earlier[1] + later[1])
-
-
 def exclusive_prefix(state, total, axis):
     n = lax.axis_size(axis)
+    heads, rows, cols = state.shape
+    pad = 8
+    packed = jnp.concatenate(
+        [state, jnp.broadcast_to(total[:, None, None], (heads, pad, cols))], axis=1
+    )
+    is_state = (jnp.arange(rows + pad) < rows)[None, :, None]
 
     def shifted(x, s):
         return lax.ppermute(x, axis, [(i, i + s) for i in range(n - s)])
 
-    acc = (shifted(state, 1), shifted(total, 1))
+    acc = shifted(packed, 1)
     s = 1
     while s < n:
-        got = (shifted(acc[0], s), shifted(acc[1], s))
-        acc = chain_join(got, acc)
+        got = shifted(acc, s)
+        scale = jnp.where(is_state, jnp.exp(acc[:, rows : rows + 1, 0:1]), 1.0)
+        acc = got * scale + acc
         s *= 2
-    return acc[0]
+    return acc[:, :rows, :]
 
 
 def on_device(queries, keys, values, gates, log_decay, norm_gain, out_weight):

time: 207 us -> 199 us (0.961)
  starting transfers between devices: 64.2 us -> 36.2 us
  waiting for transfers between devices: 92.8 us -> 113 us
    ppermute x11 -> x6, starting transfers between devices: 64.2 us -> 36.2 us  [shifted(): return lax.ppermute(x, axis, [(i, i + s) for i in range(n - s)])]
    ppermute x11 -> x6, waiting for transfers between devices: 20.6 us -> 36.4 us  [shifted(): return lax.ppermute(x, axis, [(i, i + s) for i in range(n - s)])]
    reduce_scatter x1, waiting for transfers between devices: 72.2 us -> 76.3 us  [on_device(): lax.psum_scatter(jnp.dot(normed, out_weight, preferred_element_type=jnp.f...]
  transfers between devices with their start and end apart: 12 -> 7, of which waited for: 9 -> 6; matrix products, arithmetic and copies ran while one was open for 3% -> 4% of each run, Pallas kernels for 0% -> 0%
where the time goes in v2:
time: 199 us
  waiting for transfers between devices  113 us (57%)
  starting transfers between devices  36.2 us (18%)
  matrix products  22.4 us (11%)
  between operations  13.6 us (7%)
  local copies, waits for them, and re-layouts  9.2 us (5%)
  other arithmetic  4.97 us (2%)
    reduce_scatter x1, waiting for transfers between devices, on_device(): lax.psum_scatter(jnp.dot(normed, out_weight, preferred_element_type=jnp.f...  76.3 us
    ppermute x6, waiting for transfers between devices, shifted(): return lax.ppermute(x, axis, [(i, i + s) for i in range(n - s)])  36.4 us
    ppermute x6, starting transfers between devices, shifted(): return lax.ppermute(x, axis, [(i, i + s) for i in range(n - s)])  36.2 us
    dot_general x1, matrix products, on_device(): jnp.dot(normed, out_weight, preferred_element_type=jnp.float32)  11.9 us
    dot_general x1, matrix products, on_device(): jnp.einsum('bhts,bshd->bthd', weighted, v, preferred_element_type=jnp.flo...  6.51 us
  transfers between devices with their start and end apart: 7, of which 6 were waited for; matrix products, arithmetic and copies ran while one was open for 4% of the time, Pallas kernels for 0%

profile of v2, /device:TPU:1, one launch (start us, length us, event | category | flops | bytes accessed | tf_op | source)
XLA Modules:
  0.0 199.1 jit_solution(14372433266621203286)
XLA Ops:
  6.5 0.8 reshape.286
  7.4 2.4 %reduce-window.6 = f32[2,4,4,128]{3,2,1,0:T(4,128)S(1)} reduce-window(f32[2,4,4,128]{3,2,1,0:T(4,128)S(1)} %copy.53, f32[]{:T(128)} %constant.6.clone.1), window={size=1x1x1x128 pad=0_0x0_0x0_0x127_0}, to_apply=%region_0.0 | reduce-window | flops 520192 | bytes 32772 | tf_op jit(solution)/shard_map/reduce-window
  9.8 0.2 slice_reduce_fusion
  10.0 0.4 reduce-window.9
  10.4 0.1 broadcast_add_fusion
  10.5 0.1 slice.62
  10.6 0.1 copy.56
  10.7 0.1 copy.54
  10.8 0.1 copy.55
  10.9 0.1 exponential_bitcast_fusion
  11.0 1.3 reshape.289
  12.4 0.3 reshape.285
  12.7 1.5 copy.45
  14.1 2.6 %fusion.11 = f32[2,4,128,128]{3,2,1,0:T(8,128)S(1)} fusion(bf16[2,512,4,128]{1,3,2,0:T(8,128)(2,1)} %copy.45, f32[2,512,4]{1,2,0:T(4,128)S(1)} %get-tuple-element.9, bf16[2,512,4,128]{3,2,1,0:T(4,128)(2,1)S(1)} %reshape.289), kind=kOutput, calls=%fused_computation.15 | convolution fusion | flops 806354944 | bytes 2637824 | tf_op jit(solution)/shard_map/bshd,bshe->bhde/dot_general | solution.py:46
  16.8 0.1 fusion.26
  17.0 4.4 %collective-permute-start = (f32[4,136,128]{2,1,0:T(8,128)S(1)}, f32[4,136,128]{2,1,0:T(8,128)S(1)}, u32[]{:S(2)}, u32[]{:S(2)}) collective-permute-start(f32[4,136,128]{2,1,0:T(8,128)S(1)} %pad_maximum_fusion), channel_id=1, source_target_pairs={{0,8},{8,16},{16,24},{24,32},{32,40},{40,48},{48,56},{56,64},{64,7... | collective-permute-start | bytes 835592 | tf_op jit(solution)/shard_map/ppermute | solution.py:17
  21.4 0.8 iota_compare_fusion
  22.2 0.3 reshape.284
  22.4 6.5 %fusion = f32[2,4,512,128]{2,3,1,0:T(8,128)} fusion(f32[2,4,512]{2,1,0:T(4,128)S(1)} %reduce_window_sum.24, pred[512,512]{1,0:T(8,128)(4,1)} %iota_compare_fusion, bf16[2,512,4,128]{1,3,2,0:T(8,128)(2,1)} %copy.45, bf16[2,512,4,128]{3,2,1,0:T(4,128)(2,1)} %copy-done.4, bf16[2,512,4,128]{3,2,1,0:T(4,128)(2,1)S(1)} %reshape.284), kind=kOutput, calls=%fused_computation.2 | convolution fusion | flops 1082130432 | bytes 5521408 | tf_op jit(solution)/shard_map/bhts,bshd->bthd/dot_general | solution.py:69
  29.0 3.5 %collective-permute-start.1 = (f32[4,136,128]{2,1,0:T(8,128)S(1)}, f32[4,136,128]{2,1,0:T(8,128)S(1)}, u32[]{:S(2)}, u32[]{:S(2)}) collective-permute-start(f32[4,136,128]{2,1,0:T(8,128)S(1)} %collective-permute-done), channel_id=1, source_target_pairs={{0,8},{8,16},{16,24},{24,32},{32,40},{40,48},{48,56},{56,64},{64,7... | collective-permute-start | bytes 835592 | tf_op jit(solution)/shard_map/ppermute | solution.py:17
  32.5 0.1 fusion.29
  32.6 0.1 broadcast_select_fusion.4
  32.7 4.8 %collective-permute-done.1 = f32[4,136,128]{2,1,0:T(8,128)S(1)} collective-permute-done((f32[4,136,128]{2,1,0:T(8,128)S(1)}, f32[4,136,128]{2,1,0:T(8,128)S(1)}, u32[]{:S(2)}, u32[]{:S(2)}) %collective-permute-start.1) | collective-permute-done | bytes 278560 | tf_op jit(solution)/shard_map/ppermute | solution.py:17
  37.5 0.1 multiply_add_fusion.3
  37.7 6.2 %collective-permute-start.2 = (f32[4,136,128]{2,1,0:T(8,128)S(1)}, f32[4,136,128]{2,1,0:T(8,128)S(1)}, u32[]{:S(2)}, u32[]{:S(2)}) collective-permute-start(f32[4,136,128]{2,1,0:T(8,128)S(1)} %multiply_add_fusion.3), channel_id=1, source_target_pairs={{0,16},{8,24},{16,32},{24,40},{32,48},{40,56},{48,64},{56,72},{64,... | collective-permute-start | bytes 835592 | tf_op jit(solution)/shard_map/ppermute | solution.py:17
  44.0 0.1 fusion.30
  44.1 0.1 broadcast_select_fusion.3
  44.1 9.9 %collective-permute-done.2 = f32[4,136,128]{2,1,0:T(8,128)S(1)} collective-permute-done((f32[4,136,128]{2,1,0:T(8,128)S(1)}, f32[4,136,128]{2,1,0:T(8,128)S(1)}, u32[]{:S(2)}, u32[]{:S(2)}) %collective-permute-start.2) | collective-permute-done | bytes 278560 | tf_op jit(solution)/shard_map/ppermute | solution.py:17
  54.1 0.1 multiply_add_fusion.2
  54.2 11.1 %collective-permute-start.3 = (f32[4,136,128]{2,1,0:T(8,128)S(1)}, f32[4,136,128]{2,1,0:T(8,128)S(1)}, u32[]{:S(2)}, u32[]{:S(2)}) collective-permute-start(f32[4,136,128]{2,1,0:T(8,128)S(1)} %multiply_add_fusion.2), channel_id=1, source_target_pairs={{0,32},{8,40},{16,48},{24,56},{32,64},{40,72},{48,80},{56,88},{64,... | collective-permute-start | bytes 835592 | tf_op jit(solution)/shard_map/ppermute | solution.py:17
  65.3 0.1 fusion.31
  65.5 12.1 %collective-permute-done.3 = f32[4,136,128]{2,1,0:T(8,128)S(1)} collective-permute-done((f32[4,136,128]{2,1,0:T(8,128)S(1)}, f32[4,136,128]{2,1,0:T(8,128)S(1)}, u32[]{:S(2)}, u32[]{:S(2)}) %collective-permute-start.3) | collective-permute-done | bytes 278560 | tf_op jit(solution)/shard_map/ppermute | solution.py:17
  77.6 0.1 multiply_add_fusion.1
  77.8 5.0 %collective-permute-start.4 = (f32[4,136,128]{2,1,0:T(8,128)S(1)}, f32[4,136,128]{2,1,0:T(8,128)S(1)}, u32[]{:S(2)}, u32[]{:S(2)}) collective-permute-start(f32[4,136,128]{2,1,0:T(8,128)S(1)} %multiply_add_fusion.1), channel_id=1, source_target_pairs={{0,64},{8,72},{16,80},{24,88},{32,96},{40,104},{48,112},{56,120},{... | collective-permute-start | bytes 835592 | tf_op jit(solution)/shard_map/ppermute | solution.py:17
  82.7 0.1 fusion.32
  82.9 5.3 %collective-permute-done.4 = f32[4,136,128]{2,1,0:T(8,128)S(1)} collective-permute-done((f32[4,136,128]{2,1,0:T(8,128)S(1)}, f32[4,136,128]{2,1,0:T(8,128)S(1)}, u32[]{:S(2)}, u32[]{:S(2)}) %collective-permute-start.4) | collective-permute-done | bytes 278560 | tf_op jit(solution)/shard_map/ppermute | solution.py:17
  88.2 0.1 multiply_add_fusion
  88.4 5.9 %collective-permute-start.5 = (f32[4,136,128]{2,1,0:T(8,128)S(1)}, f32[4,136,128]{2,1,0:T(8,128)S(1)}, u32[]{:S(2)}, u32[]{:S(2)}) collective-permute-start(f32[4,136,128]{2,1,0:T(8,128)S(1)} %multiply_add_fusion), channel_id=1, source_target_pairs={{0,128},{8,136},{16,144},{24,152},{32,160},{40,168},{48,176},{56,1... | collective-permute-start | bytes 835592 | tf_op jit(solution)/shard_map/ppermute | solution.py:17
  94.3 0.1 fusion.33
  94.5 4.3 %collective-permute-done.5 = f32[4,136,128]{2,1,0:T(8,128)S(1)} collective-permute-done((f32[4,136,128]{2,1,0:T(8,128)S(1)}, f32[4,136,128]{2,1,0:T(8,128)S(1)}, u32[]{:S(2)}, u32[]{:S(2)}) %collective-permute-start.5) | collective-permute-done | bytes 278560 | tf_op jit(solution)/shard_map/ppermute | solution.py:17
  98.7 0.1 fusion.28
  98.9 1.4 multiply_reduce_fusion
  100.3 0.2 copy.51
  100.5 1.9 copy.50
  102.4 1.2 mul.134
  103.6 0.4 copy-done
  104.0 11.9 %convolution_convert_fusion = bf16[1024,6144]{1,0:T(8,128)(2,1)} fusion(bf16[512,6144]{1,0:T(8,128)(2,1)} %param.13, f32[128,8,4,128]{3,2,1,0:T(4,128)S(1)} %bitcast.57, f32[128,8,4,128]{3,2,1,0:T(4,128)S(1)} %bitcast.58, bf16[1024,512]{1,0:T(8,128)(2,1)} %param.10, f32[512]{0:T(512)S(1)} %copy-done.5), kind=kOutput, calls=%fused_computation | convolution fusion | flops 6452936704 | bytes 24119296 | tf_op jit(solution)/shard_map/dot_general | solution.py:84
  115.9 76.3 %reduce-scatter.2.cloned.1.call-done = bf16[128,6144]{1,0:T(8,128)(2,1)} async-done(((bf16[1024,6144]{1,0:T(8,128)(2,1)}), bf16[128,6144]{1,0:T(8,128)(2,1)}) %reduce-scatter.2.cloned.1.call-update) | async-done | bytes 1572880 | tf_op jit(solution)/shard_map/reduce_scatter | solution.py:83
  (28 shorter events, 0.5 us)
Async XLA Ops:
  6.5 5.8 %copy-start.2 = (bf16[1024,512]{1,0:T(8,128)(2,1)S(1)}, bf16[1024,512]{1,0:T(8,128)(2,1)}, u32[]{:S(2)}) copy-start(bf16[1024,512]{1,0:T(8,128)(2,1)} %param.8) | copy-start | bytes 3145732
  6.5 185.7 %reduce-scatter.2.cloned.1.call-start = ((), (), s32[]{:S(2)}) async-start(), calls=%async_computation.1 | async-start | bytes 14155776 | tf_op jit(solution)/shard_map/reduce_scatter | solution.py:83
  12.4 9.0 %copy-start.4 = (bf16[2,512,4,128]{3,2,1,0:T(4,128)(2,1)}, bf16[2,512,4,128]{3,2,1,0:T(4,128)(2,1)S(1)}, u32[]{:S(2)}) copy-start(bf16[2,512,4,128]{3,2,1,0:T(4,128)(2,1)S(1)} %reshape.289) | copy-start | bytes 3145732
  14.1 8.0 %copy-start.3 = (bf16[1024,512]{1,0:T(8,128)(2,1)S(1)}, bf16[1024,512]{1,0:T(8,128)(2,1)}, u32[]{:S(2)}) copy-start(bf16[1024,512]{1,0:T(8,128)(2,1)} %param.7) | copy-start | bytes 3145732
  17.0 12.0 %collective-permute-start = (f32[4,136,128]{2,1,0:T(8,128)S(1)}, f32[4,136,128]{2,1,0:T(8,128)S(1)}, u32[]{:S(2)}, u32[]{:S(2)}) collective-permute-start(f32[4,136,128]{2,1,0:T(8,128)S(1)} %pad_maximum_fusion), channel_id=1, source_target_pairs={{0,8},{8,16},{16,24},{24,32},{32,40},{40,48},{48,56},{56,64},{64,7... | collective-permute-start | bytes 835592 | tf_op jit(solution)/shard_map/ppermute | solution.py:17
  29.0 8.6 %collective-permute-start.1 = (f32[4,136,128]{2,1,0:T(8,128)S(1)}, f32[4,136,128]{2,1,0:T(8,128)S(1)}, u32[]{:S(2)}, u32[]{:S(2)}) collective-permute-start(f32[4,136,128]{2,1,0:T(8,128)S(1)} %collective-permute-done), channel_id=1, source_target_pairs={{0,8},{8,16},{16,24},{24,32},{32,40},{40,48},{48,56},{56,64},{64,7... | collective-permute-start | bytes 835592 | tf_op jit(solution)/shard_map/ppermute | solution.py:17
  37.7 61.2 %copy-start.1 = (f32[2,4,512,128]{2,3,1,0:T(8,128)S(1)}, f32[2,4,512,128]{2,3,1,0:T(8,128)}, u32[]{:S(2)}) copy-start(f32[2,4,512,128]{2,3,1,0:T(8,128)} %fusion) | copy-start | bytes 6291460
  37.7 16.4 %collective-permute-start.2 = (f32[4,136,128]{2,1,0:T(8,128)S(1)}, f32[4,136,128]{2,1,0:T(8,128)S(1)}, u32[]{:S(2)}, u32[]{:S(2)}) collective-permute-start(f32[4,136,128]{2,1,0:T(8,128)S(1)} %multiply_add_fusion.3), channel_id=1, source_target_pairs={{0,16},{8,24},{16,32},{24,40},{32,48},{40,56},{48,64},{56,72},{64,... | collective-permute-start | bytes 835592 | tf_op jit(solution)/shard_map/ppermute | solution.py:17
  54.2 23.4 %collective-permute-start.3 = (f32[4,136,128]{2,1,0:T(8,128)S(1)}, f32[4,136,128]{2,1,0:T(8,128)S(1)}, u32[]{:S(2)}, u32[]{:S(2)}) collective-permute-start(f32[4,136,128]{2,1,0:T(8,128)S(1)} %multiply_add_fusion.2), channel_id=1, source_target_pairs={{0,32},{8,40},{16,48},{24,56},{32,64},{40,72},{48,80},{56,88},{64,... | collective-permute-start | bytes 835592 | tf_op jit(solution)/shard_map/ppermute | solution.py:17
  77.8 10.5 %collective-permute-start.4 = (f32[4,136,128]{2,1,0:T(8,128)S(1)}, f32[4,136,128]{2,1,0:T(8,128)S(1)}, u32[]{:S(2)}, u32[]{:S(2)}) collective-permute-start(f32[4,136,128]{2,1,0:T(8,128)S(1)} %multiply_add_fusion.1), channel_id=1, source_target_pairs={{0,64},{8,72},{16,80},{24,88},{32,96},{40,104},{48,112},{56,120},{... | collective-permute-start | bytes 835592 | tf_op jit(solution)/shard_map/ppermute | solution.py:17
  88.4 10.4 %collective-permute-start.5 = (f32[4,136,128]{2,1,0:T(8,128)S(1)}, f32[4,136,128]{2,1,0:T(8,128)S(1)}, u32[]{:S(2)}, u32[]{:S(2)}) collective-permute-start(f32[4,136,128]{2,1,0:T(8,128)S(1)} %multiply_add_fusion), channel_id=1, source_target_pairs={{0,128},{8,136},{16,144},{24,152},{32,160},{40,168},{48,176},{56,1... | collective-permute-start | bytes 835592 | tf_op jit(solution)/shard_map/ppermute | solution.py:17
  102.4 1.6 copy-start
  102.4 1.6 copy-start.5
Sparse Core Ops, SparseCore 0:
  116.0 76.1 reduce-scatter.1

commit v3 on v1

--- a/solution.py
+++ b/solution.py
@@ -4,23 +4,35 @@
 from jax.sharding import PartitionSpec as P
 
 
-def chain_join(earlier, later):
-    return (jnp.exp(later[1])[:, None, None] * earlier[0] + later[0], earlier[1] + later[1])
-
-
 def exclusive_prefix(state, total, axis):
     n = lax.axis_size(axis)
+    heads, rows, cols = state.shape
+    pad = 8
+
+    def pack(st, tot):
+        hi = tot.astype(jnp.bfloat16)
+        lo = (tot - hi.astype(jnp.float32)).astype(jnp.bfloat16)
+        parts = jnp.stack([hi, lo] + [jnp.zeros_like(hi)] * (pad - 2), axis=1)
+        return jnp.concatenate(
+            [st.astype(jnp.bfloat16), jnp.broadcast_to(parts[:, :, None], (heads, pad, cols))],
+            axis=1,
+        )
+
+    def unpack(x):
+        x = x.astype(jnp.float32)
+        return x[:, :rows, :], x[:, rows, 0] + x[:, rows + 1, 0]
 
     def shifted(x, s):
         return lax.ppermute(x, axis, [(i, i + s) for i in range(n - s)])
 
-    acc = (shifted(state, 1), shifted(total, 1))
+    st, tot = unpack(shifted(pack(state, total), 1))
     s = 1
     while s < n:
-        got = (shifted(acc[0], s), shifted(acc[1], s))
-        acc = chain_join(got, acc)
+        got_st, got_tot = unpack(shifted(pack(st, tot), s))
+        st = jnp.exp(tot)[:, None, None] * got_st + st
+        tot = got_tot + tot
         s *= 2
-    return acc[0]
+    return st
 
 
 def on_device(queries, keys, values, gates, log_decay, norm_gain, out_weight):

time: 207 us -> 180 us (0.87)
  starting transfers between devices: 64.2 us -> 40.6 us
  waiting for transfers between devices: 92.8 us -> 86 us
    ppermute x11 -> x6, starting transfers between devices: 64.2 us -> 40.6 us  [shifted(): return lax.ppermute(x, axis, [(i, i + s) for i in range(n - s)])]
    ppermute x11 -> x6, waiting for transfers between devices: 20.6 us -> 10 us  [shifted(): return lax.ppermute(x, axis, [(i, i + s) for i in range(n - s)])]
    reduce_scatter x1, waiting for transfers between devices: 72.2 us -> 76 us  [on_device(): lax.psum_scatter(jnp.dot(normed, out_weight, preferred_element_type=jnp.f...]
  transfers between devices with their start and end apart: 12 -> 7, of which waited for: 9 -> 6; matrix products, arithmetic and copies ran while one was open for 3% -> 4% of each run, Pallas kernels for 0% -> 0%
where the time goes in v3:
time: 180 us
  waiting for transfers between devices  86 us (48%)
  starting transfers between devices  40.6 us (23%)
  matrix products  23.7 us (13%)
  between operations  13.7 us (8%)
  local copies, waits for them, and re-layouts  10.4 us (6%)
  other arithmetic  5.17 us (3%)
    reduce_scatter x1, waiting for transfers between devices, on_device(): lax.psum_scatter(jnp.dot(normed, out_weight, preferred_element_type=jnp.f...  76 us
    ppermute x6, starting transfers between devices, shifted(): return lax.ppermute(x, axis, [(i, i + s) for i in range(n - s)])  40.6 us
    dot_general x1, matrix products, on_device(): jnp.dot(normed, out_weight, preferred_element_type=jnp.float32)  11.9 us
    ppermute x6, waiting for transfers between devices, shifted(): return lax.ppermute(x, axis, [(i, i + s) for i in range(n - s)])  10 us
    dot_general x1, matrix products, on_device(): jnp.einsum('bhts,bshd->bthd', weighted, v, preferred_element_type=jnp.flo...  6.43 us
  transfers between devices with their start and end apart: 7, of which 6 were waited for; matrix products, arithmetic and copies ran while one was open for 4% of the time, Pallas kernels for 0%

profile of v3, /device:TPU:1, one launch (start us, length us, event | category | flops | bytes accessed | tf_op | source)
XLA Modules:
  0.0 179.7 jit_solution(15059445112417960629)
XLA Ops:
  6.5 0.8 reshape.511
  7.4 2.4 %reduce-window.6 = f32[2,4,4,128]{3,2,1,0:T(4,128)S(1)} reduce-window(f32[2,4,4,128]{3,2,1,0:T(4,128)S(1)} %copy.101, f32[]{:T(128)} %constant.6.clone.1), window={size=1x1x1x128 pad=0_0x0_0x0_0x127_0}, to_apply=%region_0.0 | reduce-window | flops 520192 | bytes 32772 | tf_op jit(solution)/shard_map/reduce-window
  9.8 0.2 slice_reduce_fusion
  10.0 0.4 reduce-window.9
  11.1 0.1 copy.85
  11.2 0.1 copy.84
  11.4 1.3 reshape.514
  12.8 0.3 reshape.510
  13.1 1.5 copy.81
  14.5 2.5 %fusion.11 = f32[2,4,128,128]{3,2,1,0:T(8,128)S(1)} fusion(bf16[2,512,4,128]{1,3,2,0:T(8,128)(2,1)} %copy.81, f32[2,512,4]{1,2,0:T(4,128)S(1)} %get-tuple-element.33, bf16[2,512,4,128]{3,2,1,0:T(4,128)(2,1)S(1)} %reshape.514), kind=kOutput, calls=%fused_computation.15 | convolution fusion | flops 806354944 | bytes 2637824 | tf_op jit(solution)/shard_map/bshd,bshe->bhde/dot_general | solution.py:55
  17.1 0.1 fusion.31
  17.4 4.4 %collective-permute-start = (bf16[4,136,128]{2,1,0:T(8,128)(2,1)S(1)}, bf16[4,136,128]{2,1,0:T(8,128)(2,1)S(1)}, u32[]{:S(2)}, u32[]{:S(2)}) collective-permute-start(bf16[4,136,128]{2,1,0:T(8,128)(2,1)S(1)} %pad_maximum_fusion), channel_id=1, source_target_pairs={{0,8},{8,16},{16,24},{24,32},{32,40},{40,48},{48,56},{56,64},{64,7... | collective-permute-start | bytes 417800 | tf_op jit(solution)/shard_map/ppermute | solution.py:26
  21.7 2.3 %collective-permute-done = bf16[4,136,128]{2,1,0:T(8,128)(2,1)S(1)} collective-permute-done((bf16[4,136,128]{2,1,0:T(8,128)(2,1)S(1)}, bf16[4,136,128]{2,1,0:T(8,128)(2,1)S(1)}, u32[]{:S(2)}, u32[]{:S(2)}) %collective-permute-start) | collective-permute-done | bytes 139296 | tf_op jit(solution)/shard_map/ppermute | solution.py:26
  24.1 0.1 fusion.51
  24.2 0.1 copy.87
  24.3 0.1 copy.86
  24.6 4.1 %collective-permute-start.1 = (bf16[4,136,128]{2,1,0:T(8,128)(2,1)S(1)}, bf16[4,136,128]{2,1,0:T(8,128)(2,1)S(1)}, u32[]{:S(2)}, u32[]{:S(2)}) collective-permute-start(bf16[4,136,128]{2,1,0:T(8,128)(2,1)S(1)} %pad_maximum_fusion.1), channel_id=1, source_target_pairs={{0,8},{8,16},{16,24},{24,32},{32,40},{40,48},{48,56},{56,64},{64,7... | collective-permute-start | bytes 417800 | tf_op jit(solution)/shard_map/ppermute | solution.py:26
  28.7 2.0 %collective-permute-done.1 = bf16[4,136,128]{2,1,0:T(8,128)(2,1)S(1)} collective-permute-done((bf16[4,136,128]{2,1,0:T(8,128)(2,1)S(1)}, bf16[4,136,128]{2,1,0:T(8,128)(2,1)S(1)}, u32[]{:S(2)}, u32[]{:S(2)}) %collective-permute-start.1) | collective-permute-done | bytes 139296 | tf_op jit(solution)/shard_map/ppermute | solution.py:26
  30.8 0.1 exponential_reduce_fusion.2
  31.0 0.1 copy.88
  31.1 0.1 copy.89
  31.4 5.6 %collective-permute-start.2 = (bf16[4,136,128]{2,1,0:T(8,128)(2,1)S(1)}, bf16[4,136,128]{2,1,0:T(8,128)(2,1)S(1)}, u32[]{:S(2)}, u32[]{:S(2)}) collective-permute-start(bf16[4,136,128]{2,1,0:T(8,128)(2,1)S(1)} %pad_maximum_fusion.2), channel_id=1, source_target_pairs={{0,16},{8,24},{16,32},{24,40},{32,48},{40,56},{48,64},{56,72},{64,... | collective-permute-start | bytes 417800 | tf_op jit(solution)/shard_map/ppermute | solution.py:26
  37.0 2.0 %collective-permute-done.2 = bf16[4,136,128]{2,1,0:T(8,128)(2,1)S(1)} collective-permute-done((bf16[4,136,128]{2,1,0:T(8,128)(2,1)S(1)}, bf16[4,136,128]{2,1,0:T(8,128)(2,1)S(1)}, u32[]{:S(2)}, u32[]{:S(2)}) %collective-permute-start.2) | collective-permute-done | bytes 139296 | tf_op jit(solution)/shard_map/ppermute | solution.py:26
  39.0 0.1 exponential_reduce_fusion.3
  39.1 0.1 reduce.7
  39.3 0.1 copy.90
  39.8 15.0 %collective-permute-start.3 = (bf16[4,136,128]{2,1,0:T(8,128)(2,1)S(1)}, bf16[4,136,128]{2,1,0:T(8,128)(2,1)S(1)}, u32[]{:S(2)}, u32[]{:S(2)}) collective-permute-start(bf16[4,136,128]{2,1,0:T(8,128)(2,1)S(1)} %pad_maximum_fusion.3), channel_id=1, source_target_pairs={{0,32},{8,40},{16,48},{24,56},{32,64},{40,72},{48,80},{56,88},{64,... | collective-permute-start | bytes 417800 | tf_op jit(solution)/shard_map/ppermute | solution.py:26
  54.8 2.1 %collective-permute-done.3 = bf16[4,136,128]{2,1,0:T(8,128)(2,1)S(1)} collective-permute-done((bf16[4,136,128]{2,1,0:T(8,128)(2,1)S(1)}, bf16[4,136,128]{2,1,0:T(8,128)(2,1)S(1)}, u32[]{:S(2)}, u32[]{:S(2)}) %collective-permute-start.3) | collective-permute-done | bytes 139296 | tf_op jit(solution)/shard_map/ppermute | solution.py:26
  56.9 0.1 fusion.47
  57.0 0.1 fusion.44
  57.1 0.1 copy.92
  57.3 0.1 copy.93
  57.5 6.0 %collective-permute-start.4 = (bf16[4,136,128]{2,1,0:T(8,128)(2,1)S(1)}, bf16[4,136,128]{2,1,0:T(8,128)(2,1)S(1)}, u32[]{:S(2)}, u32[]{:S(2)}) collective-permute-start(bf16[4,136,128]{2,1,0:T(8,128)(2,1)S(1)} %pad_maximum_fusion.4), channel_id=1, source_target_pairs={{0,64},{8,72},{16,80},{24,88},{32,96},{40,104},{48,112},{56,120},{... | collective-permute-start | bytes 417800 | tf_op jit(solution)/shard_map/ppermute | solution.py:26
  63.6 0.3 reshape.509
  63.9 1.6 collective-permute-done.4
  65.6 0.1 exponential_reduce_fusion.1
  65.7 0.1 copy.94
  65.8 0.1 copy.95
  66.2 5.6 %collective-permute-start.5 = (bf16[4,136,128]{2,1,0:T(8,128)(2,1)S(1)}, bf16[4,136,128]{2,1,0:T(8,128)(2,1)S(1)}, u32[]{:S(2)}, u32[]{:S(2)}) collective-permute-start(bf16[4,136,128]{2,1,0:T(8,128)(2,1)S(1)} %pad_maximum_fusion.5), channel_id=1, source_target_pairs={{0,128},{8,136},{16,144},{24,152},{32,160},{40,168},{48,176},{56,1... | collective-permute-start | bytes 417800 | tf_op jit(solution)/shard_map/ppermute | solution.py:26
  71.8 6.4 %fusion = f32[2,4,512,128]{2,3,1,0:T(8,128)} fusion(f32[2,4,512]{2,1,0:T(4,128)S(1)} %reduce_window_sum.24, pred[512,512]{1,0:T(8,128)(4,1)S(1)} %iota_compare_fusion, bf16[2,512,4,128]{1,3,2,0:T(8,128)(2,1)} %copy.81, bf16[2,512,4,128]{3,2,1,0:T(4,128)(2,1)} %copy-done.3, bf16[2,512,4,128]{3,2,1,0:T(4,128)(2,1)S(1)} %reshape.509), kind=kOutput, calls=%fused_computation.2 | convolution fusion | flops 1082130432 | bytes 5521408 | tf_op jit(solution)/shard_map/bhts,bshd->bthd/dot_general | solution.py:78
  78.2 0.1 fusion.33
  78.4 2.9 %multiply_reduce_fusion = (f32[2,512,4]{1,2,0:T(4,128)S(1)}, f32[2,512,4,128]{1,3,2,0:T(8,128)S(1)}) fusion(bf16[2,512,4,128]{3,2,1,0:T(4,128)(2,1)S(1)} %reshape.509, f32[1,4,128,128]{3,2,1,0:T(8,128)S(1)} %get-tuple-element.30, f32[1,4,128,128]{3,2,1,0:T(8,128)S(1)} %get-tuple-element.29, f32[2,512,4]{1,2,0:T(4,128)S(1)} %get-tuple-element.34, ...), kind=kOutput, calls=%fused_computation.14 | convolution fusion | flops 807530496 | bytes 5799936 | tf_op jit(solution)/shard_map/bthd,bhde->bthe/dot_general | solution.py:83
  81.3 0.2 copy.99
  81.5 1.9 %copy.98 = f32[2,512,4,128]{3,2,1,0:T(4,128)} copy(f32[2,512,4,128]{1,3,2,0:T(8,128)S(1)} %get-tuple-element.43) | data formatting | bytes 4194304 | tf_op jit(solution)/shard_map/add | solution.py:86
  83.4 1.2 mul.149
  84.6 0.4 copy-done
  85.0 11.9 %convolution_convert_fusion = bf16[1024,6144]{1,0:T(8,128)(2,1)} fusion(bf16[512,6144]{1,0:T(8,128)(2,1)} %param.13, f32[128,8,4,128]{3,2,1,0:T(4,128)S(1)} %bitcast.96, f32[128,8,4,128]{3,2,1,0:T(4,128)S(1)} %bitcast.97, bf16[1024,512]{1,0:T(8,128)(2,1)} %param.10, f32[512]{0:T(512)S(1)} %copy-done.4), kind=kOutput, calls=%fused_computation | convolution fusion | flops 6452936704 | bytes 24119296 | tf_op jit(solution)/shard_map/dot_general | solution.py:93
  96.9 76.0 %reduce-scatter.2.cloned.1.call-done = bf16[128,6144]{1,0:T(8,128)(2,1)} async-done(((bf16[1024,6144]{1,0:T(8,128)(2,1)}), bf16[128,6144]{1,0:T(8,128)(2,1)}) %reduce-scatter.2.cloned.1.call-update) | async-done | bytes 1572880 | tf_op jit(solution)/shard_map/reduce_scatter | solution.py:92
  (67 shorter events, 2.5 us)
Async XLA Ops:
  6.5 6.2 %copy-start.1 = (bf16[1024,512]{1,0:T(8,128)(2,1)S(1)}, bf16[1024,512]{1,0:T(8,128)(2,1)}, u32[]{:S(2)}) copy-start(bf16[1024,512]{1,0:T(8,128)(2,1)} %param.8) | copy-start | bytes 3145732
  6.5 166.3 %reduce-scatter.2.cloned.1.call-start = ((), (), s32[]{:S(2)}) async-start(), calls=%async_computation.1 | async-start | bytes 14155776 | tf_op jit(solution)/shard_map/reduce_scatter | solution.py:92
  12.8 18.1 %copy-start.3 = (bf16[2,512,4,128]{3,2,1,0:T(4,128)(2,1)}, bf16[2,512,4,128]{3,2,1,0:T(4,128)(2,1)S(1)}, u32[]{:S(2)}) copy-start(bf16[2,512,4,128]{3,2,1,0:T(4,128)(2,1)S(1)} %reshape.514) | copy-start | bytes 3145732
  17.4 6.7 %collective-permute-start = (bf16[4,136,128]{2,1,0:T(8,128)(2,1)S(1)}, bf16[4,136,128]{2,1,0:T(8,128)(2,1)S(1)}, u32[]{:S(2)}, u32[]{:S(2)}) collective-permute-start(bf16[4,136,128]{2,1,0:T(8,128)(2,1)S(1)} %pad_maximum_fusion), channel_id=1, source_target_pairs={{0,8},{8,16},{16,24},{24,32},{32,40},{40,48},{48,56},{56,64},{64,7... | collective-permute-start | bytes 417800 | tf_op jit(solution)/shard_map/ppermute | solution.py:26
  24.6 6.1 %collective-permute-start.1 = (bf16[4,136,128]{2,1,0:T(8,128)(2,1)S(1)}, bf16[4,136,128]{2,1,0:T(8,128)(2,1)S(1)}, u32[]{:S(2)}, u32[]{:S(2)}) collective-permute-start(bf16[4,136,128]{2,1,0:T(8,128)(2,1)S(1)} %pad_maximum_fusion.1), channel_id=1, source_target_pairs={{0,8},{8,16},{16,24},{24,32},{32,40},{40,48},{48,56},{56,64},{64,7... | collective-permute-start | bytes 417800 | tf_op jit(solution)/shard_map/ppermute | solution.py:26
  30.9 32.7 %copy-start.2 = (bf16[1024,512]{1,0:T(8,128)(2,1)S(1)}, bf16[1024,512]{1,0:T(8,128)(2,1)}, u32[]{:S(2)}) copy-start(bf16[1024,512]{1,0:T(8,128)(2,1)} %param.7) | copy-start | bytes 3145732
  31.4 7.6 %collective-permute-start.2 = (bf16[4,136,128]{2,1,0:T(8,128)(2,1)S(1)}, bf16[4,136,128]{2,1,0:T(8,128)(2,1)S(1)}, u32[]{:S(2)}, u32[]{:S(2)}) collective-permute-start(bf16[4,136,128]{2,1,0:T(8,128)(2,1)S(1)} %pad_maximum_fusion.2), channel_id=1, source_target_pairs={{0,16},{8,24},{16,32},{24,40},{32,48},{40,56},{48,64},{56,72},{64,... | collective-permute-start | bytes 417800 | tf_op jit(solution)/shard_map/ppermute | solution.py:26
  39.8 17.1 %collective-permute-start.3 = (bf16[4,136,128]{2,1,0:T(8,128)(2,1)S(1)}, bf16[4,136,128]{2,1,0:T(8,128)(2,1)S(1)}, u32[]{:S(2)}, u32[]{:S(2)}) collective-permute-start(bf16[4,136,128]{2,1,0:T(8,128)(2,1)S(1)} %pad_maximum_fusion.3), channel_id=1, source_target_pairs={{0,32},{8,40},{16,48},{24,56},{32,64},{40,72},{48,80},{56,88},{64,... | collective-permute-start | bytes 417800 | tf_op jit(solution)/shard_map/ppermute | solution.py:26
  57.5 8.0 %collective-permute-start.4 = (bf16[4,136,128]{2,1,0:T(8,128)(2,1)S(1)}, bf16[4,136,128]{2,1,0:T(8,128)(2,1)S(1)}, u32[]{:S(2)}, u32[]{:S(2)}) collective-permute-start(bf16[4,136,128]{2,1,0:T(8,128)(2,1)S(1)} %pad_maximum_fusion.4), channel_id=1, source_target_pairs={{0,64},{8,72},{16,80},{24,88},{32,96},{40,104},{48,112},{56,120},{... | collective-permute-start | bytes 417800 | tf_op jit(solution)/shard_map/ppermute | solution.py:26
  66.2 12.0 %collective-permute-start.5 = (bf16[4,136,128]{2,1,0:T(8,128)(2,1)S(1)}, bf16[4,136,128]{2,1,0:T(8,128)(2,1)S(1)}, u32[]{:S(2)}, u32[]{:S(2)}) collective-permute-start(bf16[4,136,128]{2,1,0:T(8,128)(2,1)S(1)} %pad_maximum_fusion.5), channel_id=1, source_target_pairs={{0,128},{8,136},{16,144},{24,152},{32,160},{40,168},{48,176},{56,1... | collective-permute-start | bytes 417800 | tf_op jit(solution)/shard_map/ppermute | solution.py:26
  83.4 1.6 copy-start
  83.4 1.6 copy-start.4
Sparse Core Ops, SparseCore 0:
  97.0 75.8 reduce-scatter.1

commit v4 on v3

--- a/solution.py
+++ b/solution.py
@@ -6,6 +6,7 @@
 
 def exclusive_prefix(state, total, axis):
     n = lax.axis_size(axis)
+    me = lax.axis_index(axis)
     heads, rows, cols = state.shape
     pad = 8
 
@@ -22,17 +23,22 @@
         x = x.astype(jnp.float32)
         return x[:, :rows, :], x[:, rows, 0] + x[:, rows + 1, 0]
 
-    def shifted(x, s):
-        return lax.ppermute(x, axis, [(i, i + s) for i in range(n - s)])
+    def join(earlier, later):
+        return (jnp.exp(later[1])[:, None, None] * earlier[0] + later[0], earlier[1] + later[1])
 
-    st, tot = unpack(shifted(pack(state, total), 1))
+    block = (state, total)
+    prefix = (jnp.zeros_like(state), jnp.zeros_like(total))
     s = 1
     while s < n:
-        got_st, got_tot = unpack(shifted(pack(st, tot), s))
-        st = jnp.exp(tot)[:, None, None] * got_st + st
-        tot = got_tot + tot
+        other = unpack(lax.ppermute(pack(*block), axis, [(i, i ^ s) for i in range(n)]))
+        lower = (me & s) != 0
+        new_prefix = join(other, prefix)
+        prefix = tuple(jnp.where(lower, a, b) for a, b in zip(new_prefix, prefix))
+        block = tuple(
+            jnp.where(lower, a, b) for a, b in zip(join(other, block), join(block, other))
+        )
         s *= 2
-    return st
+    return prefix[0]
 
 
 def on_device(queries, keys, values, gates, log_decay, norm_gain, out_weight):

time: 180 us -> 160 us (0.89)
  starting transfers between devices: 40.6 us -> 17.6 us
  waiting for transfers between devices: 86 us -> 90 us
    ppermute x6 -> x5, starting transfers between devices: 40.6 us -> 17.6 us  [exclusive_prefix(): lax.ppermute(pack(*block), axis, [(i, i ^ s) for i in range(n)])]
    ppermute x6 -> x5, waiting for transfers between devices: 10 us -> 12.7 us  [exclusive_prefix(): lax.ppermute(pack(*block), axis, [(i, i ^ s) for i in range(n)])]
  transfers between devices with their start and end apart: 7 -> 6, of which waited for: 6 -> 5; matrix products, arithmetic and copies ran while one was open for 4% -> 5% of each run, Pallas kernels for 0% -> 0%
where the time goes in v4:
time: 160 us; the launch traced here: 159 us
  waiting for transfers between devices  90 us (56%)
  matrix products  22.5 us (14%)
  starting transfers between devices  17.6 us (11%)
  between operations  13.7 us (9%)
  local copies, waits for them, and re-layouts  10.6 us (7%)
  other arithmetic  5.01 us (3%)
    reduce_scatter x1, waiting for transfers between devices, on_device(): lax.psum_scatter(jnp.dot(normed, out_weight, preferred_element_type=jnp.f...  77.3 us
    ppermute x5, starting transfers between devices, exclusive_prefix(): lax.ppermute(pack(*block), axis, [(i, i ^ s) for i in range(n)])  17.6 us
    ppermute x5, waiting for transfers between devices, exclusive_prefix(): lax.ppermute(pack(*block), axis, [(i, i ^ s) for i in range(n)])  12.7 us
    dot_general x1, matrix products, on_device(): jnp.dot(normed, out_weight, preferred_element_type=jnp.float32)  11.9 us
    dot_general x1, matrix products, on_device(): jnp.einsum('bhts,bshd->bthd', weighted, v, preferred_element_type=jnp.flo...  6.43 us
  transfers between devices with their start and end apart: 6, of which 5 were waited for; matrix products, arithmetic and copies ran while one was open for 5% of the time, Pallas kernels for 0%

profile of v4, /device:TPU:1, one launch (start us, length us, event | category | flops | bytes accessed | tf_op | source)
XLA Modules:
  0.0 159.4 jit_solution(1279189207827317986)
XLA Ops:
  6.5 0.8 reshape.503
  7.4 2.4 %reduce-window.6 = f32[2,4,4,128]{3,2,1,0:T(4,128)S(1)} reduce-window(f32[2,4,4,128]{3,2,1,0:T(4,128)S(1)} %copy.97, f32[]{:T(128)} %constant.14.clone.1), window={size=1x1x1x128 pad=0_0x0_0x0_0x127_0}, to_apply=%region_0.0 | reduce-window | flops 520192 | bytes 32772 | tf_op jit(solution)/shard_map/reduce-window
  9.8 0.2 slice_reduce_fusion
  10.0 0.4 reduce-window.9
  10.6 0.1 copy.99
  11.0 0.1 copy.100
  11.1 0.1 copy.82
  11.2 0.1 copy.81
  11.4 1.3 reshape.506
  12.8 0.3 reshape.502
  13.1 0.7 copy.78
  13.8 1.3 fusion.11
  15.1 0.1 fusion.36
  15.4 2.5 %collective-permute-start = (bf16[4,136,128]{2,1,0:T(8,128)(2,1)S(1)}, bf16[4,136,128]{2,1,0:T(8,128)(2,1)S(1)}, u32[]{:S(2)}, u32[]{:S(2)}) collective-permute-start(bf16[4,136,128]{2,1,0:T(8,128)(2,1)S(1)} %pad_maximum_fusion), channel_id=1, source_target_pairs={{0,8},{8,0},{16,24},{24,16},{32,40},{40,32},{48,56},{56,48},{64,72... | collective-permute-start | bytes 417800 | tf_op jit(solution)/shard_map/ppermute | solution.py:33
  18.0 2.4 %collective-permute-done = bf16[4,136,128]{2,1,0:T(8,128)(2,1)S(1)} collective-permute-done((bf16[4,136,128]{2,1,0:T(8,128)(2,1)S(1)}, bf16[4,136,128]{2,1,0:T(8,128)(2,1)S(1)}, u32[]{:S(2)}, u32[]{:S(2)}) %collective-permute-start) | collective-permute-done | bytes 139296 | tf_op jit(solution)/shard_map/ppermute | solution.py:33
  20.4 0.1 exponential_reduce_fusion
  20.5 0.1 copy.83
  20.6 0.1 copy.84
  20.8 0.2 fusion.41
  21.1 3.9 %collective-permute-start.1 = (bf16[4,136,128]{2,1,0:T(8,128)(2,1)S(1)}, bf16[4,136,128]{2,1,0:T(8,128)(2,1)S(1)}, u32[]{:S(2)}, u32[]{:S(2)}) collective-permute-start(bf16[4,136,128]{2,1,0:T(8,128)(2,1)S(1)} %pad_maximum_fusion.1), channel_id=1, source_target_pairs={{0,16},{8,24},{16,0},{24,8},{32,48},{40,56},{48,32},{56,40},{64,80... | collective-permute-start | bytes 417800 | tf_op jit(solution)/shard_map/ppermute | solution.py:33
  25.0 6.1 %collective-permute-done.1 = bf16[4,136,128]{2,1,0:T(8,128)(2,1)S(1)} collective-permute-done((bf16[4,136,128]{2,1,0:T(8,128)(2,1)S(1)}, bf16[4,136,128]{2,1,0:T(8,128)(2,1)S(1)}, u32[]{:S(2)}, u32[]{:S(2)}) %collective-permute-start.1) | collective-permute-done | bytes 139296 | tf_op jit(solution)/shard_map/ppermute | solution.py:33
  31.1 0.1 exponential_reduce_fusion.6
  31.3 0.1 copy.86
  31.4 0.1 copy.87
  31.6 0.1 fusion.37
  31.8 6.6 %collective-permute-start.2 = (bf16[4,136,128]{2,1,0:T(8,128)(2,1)S(1)}, bf16[4,136,128]{2,1,0:T(8,128)(2,1)S(1)}, u32[]{:S(2)}, u32[]{:S(2)}) collective-permute-start(bf16[4,136,128]{2,1,0:T(8,128)(2,1)S(1)} %pad_maximum_fusion.2), channel_id=1, source_target_pairs={{0,32},{8,40},{16,48},{24,56},{32,0},{40,8},{48,16},{56,24},{64,96... | collective-permute-start | bytes 417800 | tf_op jit(solution)/shard_map/ppermute | solution.py:33
  38.4 3.1 %collective-permute-done.2 = bf16[4,136,128]{2,1,0:T(8,128)(2,1)S(1)} collective-permute-done((bf16[4,136,128]{2,1,0:T(8,128)(2,1)S(1)}, bf16[4,136,128]{2,1,0:T(8,128)(2,1)S(1)}, u32[]{:S(2)}, u32[]{:S(2)}) %collective-permute-start.2) | collective-permute-done | bytes 139296 | tf_op jit(solution)/shard_map/ppermute | solution.py:33
  41.5 0.1 exponential_reduce_fusion.4
  41.6 0.1 copy.88
  41.7 0.1 copy.89
  41.9 0.2 fusion.38
  42.2 1.4 collective-permute-start.3
  43.6 1.3 reshape.501
  45.0 1.2 collective-permute-done.3
  46.2 0.1 fusion.29
  46.4 0.1 copy.90
  46.5 0.1 copy.91
  46.7 0.1 select_convert_fusion
  46.9 3.2 %collective-permute-start.4 = (bf16[4,136,128]{2,1,0:T(8,128)(2,1)S(1)}, bf16[4,136,128]{2,1,0:T(8,128)(2,1)S(1)}, u32[]{:S(2)}, u32[]{:S(2)}) collective-permute-start(bf16[4,136,128]{2,1,0:T(8,128)(2,1)S(1)} %pad_maximum_fusion.4), channel_id=1, source_target_pairs={{0,128},{8,136},{16,144},{24,152},{32,160},{40,168},{48,176},{56,1... | collective-permute-start | bytes 417800 | tf_op jit(solution)/shard_map/ppermute | solution.py:33
  50.1 6.4 %fusion = f32[2,4,512,128]{2,3,1,0:T(8,128)} fusion(f32[2,4,512]{2,1,0:T(4,128)S(1)} %reduce_window_sum.24, pred[512,512]{1,0:T(8,128)(4,1)S(1)} %iota_compare_fusion, bf16[2,512,4,128]{1,3,2,0:T(8,128)(2,1)} %copy-done.3, bf16[2,512,4,128]{3,2,1,0:T(4,128)(2,1)} %copy-done.2, bf16[2,512,4,128]{3,2,1,0:T(4,128)(2,1)S(1)} %reshape.501), kind=kOutput, calls=%fused_computation.2 | convolution fusion | flops 1082130432 | bytes 5521408 | tf_op jit(solution)/shard_map/bhts,bshd->bthd/dot_general | solution.py:84
  56.5 0.3 add_bitcast_fusion
  56.8 2.9 %multiply_reduce_fusion = (f32[2,512,4]{1,2,0:T(4,128)S(1)}, f32[2,512,4,128]{1,3,2,0:T(8,128)S(1)}) fusion(bf16[2,512,4,128]{3,2,1,0:T(4,128)(2,1)S(1)} %reshape.501, f32[1,4,128,128]{3,2,1,0:T(8,128)S(1)} %get-tuple-element.20, f32[1,4,128,128]{3,2,1,0:T(8,128)S(1)} %bitcast.107, f32[2,512,4]{1,2,0:T(4,128)S(1)} %get-tuple-element.39, ...), kind=kOutput, calls=%fused_computation.14 | convolution fusion | flops 807530496 | bytes 5799936 | tf_op jit(solution)/shard_map/bthd,bhde->bthe/dot_general | solution.py:89
  59.7 0.2 copy.95
  59.9 1.9 %copy.94 = f32[2,512,4,128]{3,2,1,0:T(4,128)} copy(f32[2,512,4,128]{1,3,2,0:T(8,128)S(1)} %get-tuple-element.47) | data formatting | bytes 4194304 | tf_op jit(solution)/shard_map/add | solution.py:92
  61.8 1.2 mul.237
  63.0 0.4 copy-done
  63.4 11.9 %convolution_convert_fusion = bf16[1024,6144]{1,0:T(8,128)(2,1)} fusion(bf16[512,6144]{1,0:T(8,128)(2,1)} %param.13, f32[128,8,4,128]{3,2,1,0:T(4,128)S(1)} %bitcast.105, f32[128,8,4,128]{3,2,1,0:T(4,128)S(1)} %bitcast.106, bf16[1024,512]{1,0:T(8,128)(2,1)} %param.10, f32[512]{0:T(512)S(1)} %copy-done.4), kind=kOutput, calls=%fused_computation | convolution fusion | flops 6452936704 | bytes 24119296 | tf_op jit(solution)/shard_map/dot_general | solution.py:99
  75.3 77.3 %reduce-scatter.2.cloned.1.call-done = bf16[128,6144]{1,0:T(8,128)(2,1)} async-done(((bf16[1024,6144]{1,0:T(8,128)(2,1)}), bf16[128,6144]{1,0:T(8,128)(2,1)}) %reduce-scatter.2.cloned.1.call-update) | async-done | bytes 1572880 | tf_op jit(solution)/shard_map/reduce_scatter | solution.py:98
  (57 shorter events, 1.8 us)
Async XLA Ops:
  6.5 6.2 %copy-start.1 = (bf16[1024,512]{1,0:T(8,128)(2,1)S(1)}, bf16[1024,512]{1,0:T(8,128)(2,1)}, u32[]{:S(2)}) copy-start(bf16[1024,512]{1,0:T(8,128)(2,1)} %param.8) | copy-start | bytes 3145732
  6.5 146.0 %reduce-scatter.2.cloned.1.call-start = ((), (), s32[]{:S(2)}) async-start(), calls=%async_computation.1 | async-start | bytes 14155776 | tf_op jit(solution)/shard_map/reduce_scatter | solution.py:98
  12.8 29.3 %copy-start.2 = (bf16[2,512,4,128]{3,2,1,0:T(4,128)(2,1)}, bf16[2,512,4,128]{3,2,1,0:T(4,128)(2,1)S(1)}, u32[]{:S(2)}) copy-start(bf16[2,512,4,128]{3,2,1,0:T(4,128)(2,1)S(1)} %reshape.506) | copy-start | bytes 3145732
  13.8 4.3 %copy-start.3 = (bf16[2,512,4,128]{1,3,2,0:T(8,128)(2,1)}, bf16[2,512,4,128]{1,3,2,0:T(8,128)(2,1)S(1)}, u32[]{:S(2)}) copy-start(bf16[2,512,4,128]{1,3,2,0:T(8,128)(2,1)S(1)} %copy.78) | copy-start | bytes 3145732
  15.4 5.0 %collective-permute-start = (bf16[4,136,128]{2,1,0:T(8,128)(2,1)S(1)}, bf16[4,136,128]{2,1,0:T(8,128)(2,1)S(1)}, u32[]{:S(2)}, u32[]{:S(2)}) collective-permute-start(bf16[4,136,128]{2,1,0:T(8,128)(2,1)S(1)} %pad_maximum_fusion), channel_id=1, source_target_pairs={{0,8},{8,0},{16,24},{24,16},{32,40},{40,32},{48,56},{56,48},{64,72... | collective-permute-start | bytes 417800 | tf_op jit(solution)/shard_map/ppermute | solution.py:33
  21.1 10.0 %collective-permute-start.1 = (bf16[4,136,128]{2,1,0:T(8,128)(2,1)S(1)}, bf16[4,136,128]{2,1,0:T(8,128)(2,1)S(1)}, u32[]{:S(2)}, u32[]{:S(2)}) collective-permute-start(bf16[4,136,128]{2,1,0:T(8,128)(2,1)S(1)} %pad_maximum_fusion.1), channel_id=1, source_target_pairs={{0,16},{8,24},{16,0},{24,8},{32,48},{40,56},{48,32},{56,40},{64,80... | collective-permute-start | bytes 417800 | tf_op jit(solution)/shard_map/ppermute | solution.py:33
  31.8 9.7 %collective-permute-start.2 = (bf16[4,136,128]{2,1,0:T(8,128)(2,1)S(1)}, bf16[4,136,128]{2,1,0:T(8,128)(2,1)S(1)}, u32[]{:S(2)}, u32[]{:S(2)}) collective-permute-start(bf16[4,136,128]{2,1,0:T(8,128)(2,1)S(1)} %pad_maximum_fusion.2), channel_id=1, source_target_pairs={{0,32},{8,40},{16,48},{24,56},{32,0},{40,8},{48,16},{56,24},{64,96... | collective-permute-start | bytes 417800 | tf_op jit(solution)/shard_map/ppermute | solution.py:33
  42.2 4.0 %collective-permute-start.3 = (bf16[4,136,128]{2,1,0:T(8,128)(2,1)S(1)}, bf16[4,136,128]{2,1,0:T(8,128)(2,1)S(1)}, u32[]{:S(2)}, u32[]{:S(2)}) collective-permute-start(bf16[4,136,128]{2,1,0:T(8,128)(2,1)S(1)} %pad_maximum_fusion.3), channel_id=1, source_target_pairs={{0,64},{8,72},{16,80},{24,88},{32,96},{40,104},{48,112},{56,120},{... | collective-permute-start | bytes 417800 | tf_op jit(solution)/shard_map/ppermute | solution.py:33
  46.9 9.6 %collective-permute-start.4 = (bf16[4,136,128]{2,1,0:T(8,128)(2,1)S(1)}, bf16[4,136,128]{2,1,0:T(8,128)(2,1)S(1)}, u32[]{:S(2)}, u32[]{:S(2)}) collective-permute-start(bf16[4,136,128]{2,1,0:T(8,128)(2,1)S(1)} %pad_maximum_fusion.4), channel_id=1, source_target_pairs={{0,128},{8,136},{16,144},{24,152},{32,160},{40,168},{48,176},{56,1... | collective-permute-start | bytes 417800 | tf_op jit(solution)/shard_map/ppermute | solution.py:33
  61.8 1.6 copy-start
  61.8 1.6 copy-start.4
Sparse Core Ops, SparseCore 0:
  75.4 77.0 reduce-scatter.1

commit v5 on v4

--- a/solution.py
+++ b/solution.py
@@ -91,16 +91,30 @@
     )
     attn = (inside + carried).reshape(local_rows, head_count, head_width)
 
-    meansq = jnp.mean(attn * attn, axis=-1, keepdims=True)
-    gate = jax.nn.sigmoid(gates.reshape(local_rows, head_count, head_width).astype(jnp.float32))
-    normed = attn * lax.rsqrt(meansq + 1e-06) * norm_gain.reshape(head_count, head_width) * gate
-    normed = normed.astype(jnp.bfloat16).reshape(local_rows, head_count * head_width)
-    return lax.psum_scatter(
-        jnp.dot(normed, out_weight, preferred_element_type=jnp.float32).astype(jnp.bfloat16),
-        "tp",
-        scatter_dimension=0,
-        tiled=True,
-    )
+    tp = lax.axis_size("tp")
+    chunks = 2
+    sub = local_rows // tp // chunks
+    attn = attn.reshape(tp, chunks, sub, head_count, head_width)
+    gate_all = gates.reshape(tp, chunks, sub, head_count, head_width)
+    gain = norm_gain.reshape(head_count, head_width)
+    outs = []
+    for c in range(chunks):
+        part = attn[:, c]
+        meansq = jnp.mean(part * part, axis=-1, keepdims=True)
+        gate = jax.nn.sigmoid(gate_all[:, c].astype(jnp.float32))
+        normed = part * lax.rsqrt(meansq + 1e-06) * gain * gate
+        normed = normed.astype(jnp.bfloat16).reshape(tp * sub, head_count * head_width)
+        outs.append(
+            lax.psum_scatter(
+                jnp.dot(normed, out_weight, preferred_element_type=jnp.float32).astype(
+                    jnp.bfloat16
+                ),
+                "tp",
+                scatter_dimension=0,
+                tiled=True,
+            )
+        )
+    return jnp.concatenate(outs, axis=0)
 
 
 def solution(mesh):

time: 160 us -> 186 us (1.16)
  other arithmetic: 5.01 us -> 16.5 us
  waiting for transfers between devices: 90 us -> 98.6 us
  matrix products: 22.5 us -> 28.8 us
    reduce_scatter x1 -> x2, waiting for transfers between devices: 77.3 us -> 86.4 us  [on_device(): lax.psum_scatter(jnp.dot(normed, out_weight, preferred_element_type=jnp.f...]
    dot_general x1 -> x2, matrix products: 11.9 us -> 17.4 us  [on_device(): jnp.dot(normed, out_weight, preferred_element_type=jnp.float32)]
    concatenate x0 -> x1, other arithmetic: none -> 2.65 us  [on_device(): return jnp.concatenate(outs, axis=0)]
    div x0 -> x1, other arithmetic: none -> 2.44 us  [on_device(): gate = jax.nn.sigmoid(gate_all[:, c].astype(jnp.float32))]
  transfers between devices with their start and end apart: 6 -> 7, of which waited for: 5 -> 6; matrix products, arithmetic and copies ran while one was open for 5% -> 11% of each run, Pallas kernels for 0% -> 0%
where the time goes in v5:
time: 186 us
  waiting for transfers between devices  98.6 us (53%)
  matrix products  28.8 us (15%)
  starting transfers between devices  17 us (9%)
  other arithmetic  16.5 us (9%)
  between operations  13.7 us (7%)
  local copies, waits for them, and re-layouts  11 us (6%)
    reduce_scatter x2, waiting for transfers between devices, on_device(): lax.psum_scatter(jnp.dot(normed, out_weight, preferred_element_type=jnp.f...  86.4 us
    dot_general x2, matrix products, on_device(): jnp.dot(normed, out_weight, preferred_element_type=jnp.float32)  17.4 us
    ppermute x5, starting transfers between devices, exclusive_prefix(): lax.ppermute(pack(*block), axis, [(i, i ^ s) for i in range(n)])  16.9 us
    ppermute x5, waiting for transfers between devices, exclusive_prefix(): lax.ppermute(pack(*block), axis, [(i, i ^ s) for i in range(n)])  12.2 us
    dot_general x1, matrix products, on_device(): jnp.einsum('bhts,bshd->bthd', weighted, v, preferred_element_type=jnp.flo...  5.95 us
  transfers between devices with their start and end apart: 7, of which 6 were waited for; matrix products, arithmetic and copies ran while one was open for 11% of the time, Pallas kernels for 0%

profile of v5, /device:TPU:1, one launch (start us, length us, event | category | flops | bytes accessed | tf_op | source)
XLA Modules:
  0.0 185.6 jit_solution(12095306280025828134)
XLA Ops:
  6.5 0.8 reshape.520
  7.4 2.4 %reduce-window.6 = f32[2,4,4,128]{3,2,1,0:T(4,128)S(1)} reduce-window(f32[2,4,4,128]{3,2,1,0:T(4,128)S(1)} %copy.111, f32[]{:T(128)} %constant.14.clone.1), window={size=1x1x1x128 pad=0_0x0_0x0_0x127_0}, to_apply=%region_0.0 | reduce-window | flops 520192 | bytes 32772 | tf_op jit(solution)/shard_map/reduce-window
  9.8 0.2 slice_reduce_fusion
  10.0 0.4 reduce-window.9
  11.4 1.3 reshape.519
  12.8 1.5 copy.85
  14.2 0.3 reshape.523
  14.5 2.9 %fusion.8 = f32[2,4,128,128]{3,2,1,0:T(8,128)S(1)} fusion(bf16[2,512,4,128]{1,3,2,0:T(8,128)(2,1)} %copy.85, f32[2,512,4]{1,2,0:T(4,128)S(1)} %get-tuple-element.44, bf16[2,512,4,128]{3,2,1,0:T(4,128)(2,1)S(1)} %reshape.523), kind=kOutput, calls=%fused_computation.11 | convolution fusion | flops 806354944 | bytes 2637824 | tf_op jit(solution)/shard_map/bshd,bshe->bhde/dot_general | solution.py:61
  17.7 2.5 %collective-permute-start = (bf16[4,136,128]{2,1,0:T(8,128)(2,1)S(1)}, bf16[4,136,128]{2,1,0:T(8,128)(2,1)S(1)}, u32[]{:S(2)}, u32[]{:S(2)}) collective-permute-start(bf16[4,136,128]{2,1,0:T(8,128)(2,1)S(1)} %pad_maximum_fusion.1), channel_id=1, source_target_pairs={{0,8},{8,0},{16,24},{24,16},{32,40},{40,32},{48,56},{56,48},{64,72... | collective-permute-start | bytes 417800 | tf_op jit(solution)/shard_map/ppermute | solution.py:33
  20.4 2.4 %collective-permute-done = bf16[4,136,128]{2,1,0:T(8,128)(2,1)S(1)} collective-permute-done((bf16[4,136,128]{2,1,0:T(8,128)(2,1)S(1)}, bf16[4,136,128]{2,1,0:T(8,128)(2,1)S(1)}, u32[]{:S(2)}, u32[]{:S(2)}) %collective-permute-start) | collective-permute-done | bytes 139296 | tf_op jit(solution)/shard_map/ppermute | solution.py:33
  22.8 0.1 exponential_reduce_fusion
  23.1 0.2 fusion.42
  23.4 3.9 %collective-permute-start.1 = (bf16[4,136,128]{2,1,0:T(8,128)(2,1)S(1)}, bf16[4,136,128]{2,1,0:T(8,128)(2,1)S(1)}, u32[]{:S(2)}, u32[]{:S(2)}) collective-permute-start(bf16[4,136,128]{2,1,0:T(8,128)(2,1)S(1)} %pad_maximum_fusion.2), channel_id=1, source_target_pairs={{0,16},{8,24},{16,0},{24,8},{32,48},{40,56},{48,32},{56,40},{64,80... | collective-permute-start | bytes 417800 | tf_op jit(solution)/shard_map/ppermute | solution.py:33
  27.4 6.1 %collective-permute-done.1 = bf16[4,136,128]{2,1,0:T(8,128)(2,1)S(1)} collective-permute-done((bf16[4,136,128]{2,1,0:T(8,128)(2,1)S(1)}, bf16[4,136,128]{2,1,0:T(8,128)(2,1)S(1)}, u32[]{:S(2)}, u32[]{:S(2)}) %collective-permute-start.1) | collective-permute-done | bytes 139296 | tf_op jit(solution)/shard_map/ppermute | solution.py:33
  33.5 0.1 exponential_reduce_fusion.6
  33.9 0.1 fusion.38
  34.2 0.7 pad_maximum_fusion.3
  34.8 6.5 %collective-permute-start.2 = (bf16[4,136,128]{2,1,0:T(8,128)(2,1)}, bf16[4,136,128]{2,1,0:T(8,128)(2,1)}, u32[]{:S(2)}, u32[]{:S(2)}) collective-permute-start(bf16[4,136,128]{2,1,0:T(8,128)(2,1)} %pad_maximum_fusion.3), channel_id=1, source_target_pairs={{0,32},{8,40},{16,48},{24,56},{32,0},{40,8},{48,16},{56,24},{64,96... | collective-permute-start | bytes 417800 | tf_op jit(solution)/shard_map/ppermute | solution.py:33
  41.3 0.3 reshape.518
  41.6 3.0 %collective-permute-done.2 = bf16[4,136,128]{2,1,0:T(8,128)(2,1)} collective-permute-done((bf16[4,136,128]{2,1,0:T(8,128)(2,1)}, bf16[4,136,128]{2,1,0:T(8,128)(2,1)}, u32[]{:S(2)}, u32[]{:S(2)}) %collective-permute-start.2) | collective-permute-done | bytes 139296 | tf_op jit(solution)/shard_map/ppermute | solution.py:33
  44.7 0.9 convert_element_type.246
  45.6 0.1 exponential_reduce_fusion.4
  46.1 0.9 fusion.39
  47.0 1.4 collective-permute-start.3
  48.4 6.0 %fusion = f32[2,4,512,128]{3,2,1,0:T(8,128)} fusion(f32[2,4,512]{2,1,0:T(4,128)S(1)} %reduce_window_sum.24, pred[512,512]{1,0:T(8,128)(4,1)S(1)} %iota_compare_fusion, bf16[2,512,4,128]{1,3,2,0:T(8,128)(2,1)} %copy.85, bf16[2,512,4,128]{3,2,1,0:T(4,128)(2,1)} %copy-done.4, bf16[2,512,4,128]{3,2,1,0:T(4,128)(2,1)S(1)} %reshape.518), kind=kOutput, calls=%fused_computation.3 | convolution fusion | flops 1082130432 | bytes 5521408 | tf_op jit(solution)/shard_map/bhts,bshd->bthd/dot_general | solution.py:84
  54.4 1.3 reshape.524
  55.8 0.9 convert_element_type.251
  56.7 0.1 fusion.31
  57.1 1.1 select_convert_fusion
  58.3 0.7 pad_maximum_fusion.5
  59.0 2.6 %collective-permute-start.4 = (bf16[4,136,128]{2,1,0:T(8,128)(2,1)}, bf16[4,136,128]{2,1,0:T(8,128)(2,1)}, u32[]{:S(2)}, u32[]{:S(2)}) collective-permute-start(bf16[4,136,128]{2,1,0:T(8,128)(2,1)} %pad_maximum_fusion.5), channel_id=1, source_target_pairs={{0,128},{8,136},{16,144},{24,152},{32,160},{40,168},{48,176},{56,1... | collective-permute-start | bytes 417800 | tf_op jit(solution)/shard_map/ppermute | solution.py:33
  61.6 2.4 %add_divide_fusion.1 = (f32[8,1,64,4,128]{4,3,2,0,1:T(4,128)}, f32[8,1,64,4,128]{4,3,2,0,1:T(4,128)}) fusion(bf16[8,2,64,4,128]{4,3,2,1,0:T(4,128)(2,1)S(1)} %reshape.524), kind=kLoop, calls=%fused_computation.25 | loop fusion | flops 2097152 | bytes 3145728 | tf_op jit(solution)/shard_map/div | solution.py:104
  64.0 0.7 collective-permute-done.4
  64.7 1.2 add_bitcast_fusion
  65.9 2.6 %fusion.7 = f32[2,512,4,128]{3,1,2,0:T(8,128)S(1)} fusion(f32[2,4,512,128]{3,2,1,0:T(8,128)} %fusion, f32[2,512,4]{1,2,0:T(4,128)S(1)} %get-tuple-element.45, bf16[2,512,4,128]{3,2,1,0:T(4,128)(2,1)S(1)} %reshape.518, f32[1,4,128,128]{3,2,1,0:T(8,128)S(1)} %get-tuple-element.22, f32[1,4,128,128]{3,2,1,0:T(8,128)S(1)} %bitcast.148), kind=kOutput, calls=%fused_computation.10 | convolution fusion | flops 806486016 | bytes 5783552 | tf_op jit(solution)/shard_map/bthd,bhde->bthe/dot_general | solution.py:89
  68.5 0.1 copy.102
  68.7 0.6 multiply_reduce_fusion.1
  69.3 0.1 copy.104
  69.5 0.7 copy.103
  70.2 0.6 mul.263
  70.8 9.2 %convolution_convert_fusion.1 = bf16[512,6144]{1,0:T(8,128)(2,1)} fusion(bf16[512,6144]{1,0:T(8,128)(2,1)} %param.13, f32[64,8,4,128]{3,2,1,0:T(4,128)} %bitcast.147, f32[64,8,4,128]{3,2,1,0:T(4,128)S(1)} %bitcast.150, f32[64,8,4,128]{3,2,1,0:T(4,128)S(1)} %bitcast.152, f32[512]{0:T(512)S(1)} %copy-done.5), kind=kOutput, calls=%fused_computation.1 | convolution fusion | flops 3225419776 | bytes 15730688 | tf_op jit(solution)/shard_map/dot_general | solution.py:109
  80.1 0.1 copy.107
  80.2 0.7 copy.106
  80.9 0.6 mul.270
  81.5 8.1 %convolution_convert_fusion = bf16[512,6144]{1,0:T(8,128)(2,1)} fusion(bf16[512,6144]{1,0:T(8,128)(2,1)} %param.13, f32[64,8,4,128]{3,2,1,0:T(4,128)S(1)} %bitcast.146, f32[64,8,4,128]{3,2,1,0:T(4,128)S(1)} %bitcast.149, f32[64,8,4,128]{3,2,1,0:T(4,128)S(1)} %bitcast.151, f32[512]{0:T(512)S(1)} %copy-done.5), kind=kOutput, calls=%fused_computation | convolution fusion | flops 3225419776 | bytes 15730688 | tf_op jit(solution)/shard_map/dot_general | solution.py:109
  89.7 39.0 %reduce-scatter.3.cloned.1.call-done = bf16[64,6144]{1,0:T(8,128)(2,1)} async-done(((bf16[512,6144]{1,0:T(8,128)(2,1)}), bf16[64,6144]{1,0:T(8,128)(2,1)}) %reduce-scatter.3.cloned.1.call-update) | async-done | bytes 786448 | tf_op jit(solution)/shard_map/reduce_scatter | solution.py:108
  128.7 47.4 %reduce-scatter.5.cloned.1.call-done = bf16[64,6144]{1,0:T(8,128)(2,1)} async-done(((bf16[512,6144]{1,0:T(8,128)(2,1)}), bf16[64,6144]{1,0:T(8,128)(2,1)}) %reduce-scatter.5.cloned.1.call-update) | async-done | bytes 786448 | tf_op jit(solution)/shard_map/reduce_scatter | solution.py:108
  176.1 2.7 %pad_maximum_fusion = bf16[128,6144]{1,0:T(8,128)(2,1)} fusion(bf16[64,6144]{1,0:T(8,128)(2,1)} %reduce-scatter.5.cloned.1.call-done, bf16[64,6144]{1,0:T(8,128)(2,1)} %reduce-scatter.3.cloned.1.call-done), kind=kLoop, calls=%fused_computation.14 | loop fusion | flops 3145728 | bytes 3145728 | tf_op jit(solution)/shard_map/concatenate | solution.py:117
  (71 shorter events, 3.2 us)
Async XLA Ops:
  6.5 7.7 %copy-start.2 = (bf16[1024,512]{1,0:T(8,128)(2,1)S(1)}, bf16[1024,512]{1,0:T(8,128)(2,1)}, u32[]{:S(2)}) copy-start(bf16[1024,512]{1,0:T(8,128)(2,1)} %param.9) | copy-start | bytes 3145732
  6.5 122.1 %reduce-scatter.3.cloned.1.call-start = ((), (), s32[]{:S(2)}) async-start(), calls=%async_computation.2 | async-start | bytes 7077888 | tf_op jit(solution)/shard_map/reduce_scatter | solution.py:108
  14.5 5.9 %copy-start.4 = (bf16[2,512,4,128]{3,2,1,0:T(4,128)(2,1)}, bf16[2,512,4,128]{3,2,1,0:T(4,128)(2,1)S(1)}, u32[]{:S(2)}) copy-start(bf16[2,512,4,128]{3,2,1,0:T(4,128)(2,1)S(1)} %reshape.523) | copy-start | bytes 3145732
  14.5 26.8 %copy-start.3 = (bf16[1024,512]{1,0:T(8,128)(2,1)S(1)}, bf16[1024,512]{1,0:T(8,128)(2,1)}, u32[]{:S(2)}) copy-start(bf16[1024,512]{1,0:T(8,128)(2,1)} %param.7) | copy-start | bytes 3145732
  17.7 5.0 %collective-permute-start = (bf16[4,136,128]{2,1,0:T(8,128)(2,1)S(1)}, bf16[4,136,128]{2,1,0:T(8,128)(2,1)S(1)}, u32[]{:S(2)}, u32[]{:S(2)}) collective-permute-start(bf16[4,136,128]{2,1,0:T(8,128)(2,1)S(1)} %pad_maximum_fusion.1), channel_id=1, source_target_pairs={{0,8},{8,0},{16,24},{24,16},{32,40},{40,32},{48,56},{56,48},{64,72... | collective-permute-start | bytes 417800 | tf_op jit(solution)/shard_map/ppermute | solution.py:33
  23.4 10.0 %collective-permute-start.1 = (bf16[4,136,128]{2,1,0:T(8,128)(2,1)S(1)}, bf16[4,136,128]{2,1,0:T(8,128)(2,1)S(1)}, u32[]{:S(2)}, u32[]{:S(2)}) collective-permute-start(bf16[4,136,128]{2,1,0:T(8,128)(2,1)S(1)} %pad_maximum_fusion.2), channel_id=1, source_target_pairs={{0,16},{8,24},{16,0},{24,8},{32,48},{40,56},{48,32},{56,40},{64,80... | collective-permute-start | bytes 417800 | tf_op jit(solution)/shard_map/ppermute | solution.py:33
  34.8 9.9 %collective-permute-start.2 = (bf16[4,136,128]{2,1,0:T(8,128)(2,1)}, bf16[4,136,128]{2,1,0:T(8,128)(2,1)}, u32[]{:S(2)}, u32[]{:S(2)}) collective-permute-start(bf16[4,136,128]{2,1,0:T(8,128)(2,1)} %pad_maximum_fusion.3), channel_id=1, source_target_pairs={{0,32},{8,40},{16,48},{24,56},{32,0},{40,8},{48,16},{56,24},{64,96... | collective-permute-start | bytes 417800 | tf_op jit(solution)/shard_map/ppermute | solution.py:33
  45.6 8.8 %copy-start = (f32[4,136,128]{2,1,0:T(8,128)}, f32[4,136,128]{2,1,0:T(8,128)S(1)}, u32[]{:S(2)}) copy-start(f32[4,136,128]{2,1,0:T(8,128)S(1)} %convert_element_type.246) | copy-start | bytes 835588
  47.0 8.7 %collective-permute-start.3 = (bf16[4,136,128]{2,1,0:T(8,128)(2,1)S(1)}, bf16[4,136,128]{2,1,0:T(8,128)(2,1)}, u32[]{:S(2)}, u32[]{:S(2)}) collective-permute-start(bf16[4,136,128]{2,1,0:T(8,128)(2,1)S(1)} %pad_maximum_fusion.4), channel_id=1, source_target_pairs={{0,64},{8,72},{16,80},{24,88},{32,96},{40,104},{48,112},{56,120},{... | collective-permute-start | bytes 417800 | tf_op jit(solution)/shard_map/ppermute | solution.py:33
  59.0 5.7 %collective-permute-start.4 = (bf16[4,136,128]{2,1,0:T(8,128)(2,1)}, bf16[4,136,128]{2,1,0:T(8,128)(2,1)}, u32[]{:S(2)}, u32[]{:S(2)}) collective-permute-start(bf16[4,136,128]{2,1,0:T(8,128)(2,1)} %pad_maximum_fusion.5), channel_id=1, source_target_pairs={{0,128},{8,136},{16,144},{24,152},{32,160},{40,168},{48,176},{56,1... | collective-permute-start | bytes 417800 | tf_op jit(solution)/shard_map/ppermute | solution.py:33
  68.7 2.1 %copy-start.5 = (f32[512]{0:T(512)S(1)}, f32[512]{0:T(512)}, u32[]{:S(2)}) copy-start(f32[512]{0:T(512)} %param.12) | copy-start | bytes 6148
  80.0 1.5 copy-start.1
  80.0 96.0 %reduce-scatter.5.cloned.1.call-start = ((), (), s32[]{:S(2)}) async-start(), calls=%async_computation.3 | async-start | bytes 7077888 | tf_op jit(solution)/shard_map/reduce_scatter | solution.py:108
Sparse Core Ops, SparseCore 0:
  80.2 48.4 reduce-scatter.2
  131.2 44.7 reduce-scatter.4

commit v6 on v3

--- a/solution.py
+++ b/solution.py
@@ -4,8 +4,9 @@
 from jax.sharding import PartitionSpec as P
 
 
-def exclusive_prefix(state, total, axis):
+def exclusive_prefix(state, total, axis, group):
     n = lax.axis_size(axis)
+    me = lax.axis_index(axis)
     heads, rows, cols = state.shape
     pad = 8
 
@@ -22,17 +23,38 @@
         x = x.astype(jnp.float32)
         return x[:, :rows, :], x[:, rows, 0] + x[:, rows + 1, 0]
 
-    def shifted(x, s):
-        return lax.ppermute(x, axis, [(i, i + s) for i in range(n - s)])
+    def level(st, tot, stride, count):
+        digit = (me // stride) % count
+        sts, tots = [st], [tot]
+        sent = pack(st, tot)
+        for d in range(1, count):
+            got_st, got_tot = unpack(
+                lax.ppermute(sent, axis, [(i, i ^ (d * stride)) for i in range(n)])
+            )
+            sts.append(got_st)
+            tots.append(got_tot)
+        tots = jnp.stack(tots)
+        pos = jnp.arange(count) ^ digit
+        earlier = pos[:, None] < pos[None, :]
+        is_before = pos < digit
+        mask_b = earlier & is_before[None, :]
+        w_before = jnp.where(
+            is_before[:, None],
+            jnp.exp(jnp.sum(jnp.where(mask_b[:, :, None], tots[None], 0.0), axis=1)),
+            0.0,
+        )
+        w_whole = jnp.exp(jnp.sum(jnp.where(earlier[:, :, None], tots[None], 0.0), axis=1))
+        before = sum(w_before[d][:, None, None] * sts[d] for d in range(count))
+        whole = sum(w_whole[d][:, None, None] * sts[d] for d in range(count))
+        tot_before = jnp.sum(jnp.where(is_before[:, None], tots, 0.0), axis=0)
+        tot_whole = jnp.sum(tots, axis=0)
+        return (before, tot_before), (whole, tot_whole)
 
-    st, tot = unpack(shifted(pack(state, total), 1))
-    s = 1
-    while s < n:
-        got_st, got_tot = unpack(shifted(pack(st, tot), s))
-        st = jnp.exp(tot)[:, None, None] * got_st + st
-        tot = got_tot + tot
-        s *= 2
-    return st
+    (in_st, in_tot), (row_st, row_tot) = level(state, total, 1, group)
+    if group == n:
+        return in_st
+    (out_st, _), _ = level(row_st, row_tot, group, n // group)
+    return jnp.exp(in_tot)[:, None, None] * out_st + in_st
 
 
 def on_device(queries, keys, values, gates, log_decay, norm_gain, out_weight):
@@ -68,7 +90,9 @@
     local_state = run
     own_total = before
 
-    incoming = exclusive_prefix(local_state, own_total, "ctx")
+    ctx_size = lax.axis_size("ctx")
+    group = 8 if ctx_size % 8 == 0 else ctx_size
+    incoming = exclusive_prefix(local_state, own_total, "ctx", group)
 
     lower = jnp.arange(width_blk)[:, None] >= jnp.arange(width_blk)[None, :]
     spread = cum[:, :, :, None] - cum[:, :, None, :]

time: 180 us -> 169 us (0.939)
  starting transfers between devices: 40.6 us -> 20.2 us
  other arithmetic: 5.17 us -> 19.7 us
  waiting for transfers between devices: 86 us -> 82.4 us
  matrix products: 23.7 us -> 20.7 us
    ppermute x6 -> x10, starting transfers between devices: 40.6 us -> 20.2 us  [level(): lax.ppermute(sent, axis, [(i, i ^ d * stride) for i in range(n)])]
    convert_element_type x5 -> x10, other arithmetic: 0.1 us -> 4.74 us  [unpack(): x = x.astype(jnp.float32)]
    ppermute x6 -> x10, waiting for transfers between devices: 10 us -> 7.42 us  [level(): lax.ppermute(sent, axis, [(i, i ^ d * stride) for i in range(n)])]
    lt x0 -> x3, other arithmetic: none -> 2.42 us  [the longest x1 1.42 us: level(): earlier = pos[:, None] < pos[None, :]]
    add x3 -> x10, other arithmetic: 0.35 us -> 2.58 us  [unpack(): return (x[:, :rows, :], x[:, rows, 0] + x[:, rows + 1, 0])]
    unnamed x13 -> x47, local copies, waits for them, and re-layouts: 0.67 us -> 2.65 us
  transfers between devices with their start and end apart: 7 -> 11, of which waited for: 6 -> 4; matrix products, arithmetic and copies ran while one was open for 4% -> 12% of each run, Pallas kernels for 0% -> 0%
where the time goes in v6:
time: 169 us
  waiting for transfers between devices  82.4 us (49%)
  matrix products  20.7 us (12%)
  starting transfers between devices  20.2 us (12%)
  other arithmetic  19.7 us (12%)
  between operations  13.7 us (8%)
  local copies, waits for them, and re-layouts  11.9 us (7%)
    reduce_scatter x1, waiting for transfers between devices, on_device(): lax.psum_scatter(jnp.dot(normed, out_weight, preferred_element_type=jnp.f...  75 us
    ppermute x10, starting transfers between devices, level(): lax.ppermute(sent, axis, [(i, i ^ d * stride) for i in range(n)])  20.2 us
    dot_general x1, matrix products, on_device(): jnp.dot(normed, out_weight, preferred_element_type=jnp.float32)  11.9 us
    ppermute x10, waiting for transfers between devices, level(): lax.ppermute(sent, axis, [(i, i ^ d * stride) for i in range(n)])  7.42 us
    dot_general x1, matrix products, on_device(): jnp.einsum('bhts,bshd->bthd', weighted, v, preferred_element_type=jnp.flo...  6.16 us
    convert_element_type x10, other arithmetic, unpack(): x = x.astype(jnp.float32)  4.74 us
  transfers between devices with their start and end apart: 11, of which 4 were waited for; matrix products, arithmetic and copies ran while one was open for 12% of the time, Pallas kernels for 0%

profile of v6, /device:TPU:1, one launch (start us, length us, event | category | flops | bytes accessed | tf_op | source)
XLA Modules:
  0.0 168.7 jit_solution(8024976933468163645)
XLA Ops:
  6.5 0.8 reshape.850
  7.4 2.4 %reduce-window.6 = f32[2,4,4,128]{3,2,1,0:T(4,128)S(1)} reduce-window(f32[2,4,4,128]{3,2,1,0:T(4,128)S(1)} %copy.119, f32[]{:T(128)} %constant.53.clone.1), window={size=1x1x1x128 pad=0_0x0_0x0_0x127_0}, to_apply=%region_0.0 | reduce-window | flops 520192 | bytes 32772 | tf_op jit(solution)/shard_map/reduce-window
  10.0 0.4 reduce-window.9
  11.1 0.6 bitcast_convert_fusion
  11.9 0.6 exponential_bitcast_fusion
  12.5 1.3 reshape.853
  14.2 0.7 copy.99
  14.9 1.3 fusion.11
  16.3 0.8 copy-done.2
  17.4 6.5 %collective-permute-start.6 = (bf16[4,136,128]{2,1,0:T(8,128)(2,1)S(1)}, bf16[4,136,128]{2,1,0:T(8,128)(2,1)}, u32[]{:S(2)}, u32[]{:S(2)}) collective-permute-start(bf16[4,136,128]{2,1,0:T(8,128)(2,1)S(1)} %pad_maximum_fusion), channel_id=1, source_target_pairs={{0,56},{8,48},{16,40},{24,32},{32,24},{40,16},{48,8},{56,0},{64,12... | collective-permute-start | bytes 417800 | tf_op jit(solution)/shard_map/ppermute | solution.py:32
  23.8 0.5 collective-permute-start.5
  24.4 3.5 %collective-permute-start.4 = (bf16[4,136,128]{2,1,0:T(8,128)(2,1)S(1)}, bf16[4,136,128]{2,1,0:T(8,128)(2,1)}, u32[]{:S(2)}, u32[]{:S(2)}) collective-permute-start(bf16[4,136,128]{2,1,0:T(8,128)(2,1)S(1)} %pad_maximum_fusion), channel_id=1, source_target_pairs={{0,40},{8,32},{16,56},{24,48},{32,8},{40,0},{48,24},{56,16},{64,10... | collective-permute-start | bytes 417800 | tf_op jit(solution)/shard_map/ppermute | solution.py:32
  27.8 1.8 %collective-permute-start.3 = (bf16[4,136,128]{2,1,0:T(8,128)(2,1)S(1)}, bf16[4,136,128]{2,1,0:T(8,128)(2,1)}, u32[]{:S(2)}, u32[]{:S(2)}) collective-permute-start(bf16[4,136,128]{2,1,0:T(8,128)(2,1)S(1)} %pad_maximum_fusion), channel_id=1, source_target_pairs={{0,32},{8,40},{16,48},{24,56},{32,0},{40,8},{48,16},{56,24},{64,96... | collective-permute-start | bytes 417800 | tf_op jit(solution)/shard_map/ppermute | solution.py:32
  29.7 1.6 collective-permute-start.2
  31.3 0.5 broadcast_compare_fusion.2
  31.8 0.6 iota_xor_fusion.1
  32.4 0.5 broadcast_compare_fusion.1
  32.9 0.6 iota_xor_fusion
  33.5 0.8 iota_compare_fusion
  34.9 1.4 broadcast_compare_fusion
  36.3 6.2 %fusion = f32[2,4,512,128]{2,3,1,0:T(8,128)} fusion(f32[2,4,512]{2,1,0:T(4,128)} %copy-done.7, pred[512,512]{1,0:T(8,128)(4,1)} %iota_compare_fusion, bf16[2,512,4,128]{1,3,2,0:T(8,128)(2,1)} %copy-done.6, bf16[2,512,4,128]{3,2,1,0:T(4,128)(2,1)S(1)} %reshape.853, bf16[2,512,4,128]{3,2,1,0:T(4,128)(2,1)S(1)} %reshape.848), kind=kOutput, calls=%fused_computation.2 | convolution fusion | flops 1082130432 | bytes 5521408 | tf_op jit(solution)/shard_map/bhts,bshd->bthd/dot_general | solution.py:102
  42.5 0.6 compare_and_fusion
  43.1 0.9 convert_element_type.135
  44.1 2.6 %collective-permute-start = (bf16[4,136,128]{2,1,0:T(8,128)(2,1)S(1)}, bf16[4,136,128]{2,1,0:T(8,128)(2,1)S(1)}, u32[]{:S(2)}, u32[]{:S(2)}) collective-permute-start(bf16[4,136,128]{2,1,0:T(8,128)(2,1)S(1)} %pad_maximum_fusion), channel_id=1, source_target_pairs={{0,8},{8,0},{16,24},{24,16},{32,40},{40,32},{48,56},{56,48},{64,72... | collective-permute-start | bytes 417800 | tf_op jit(solution)/shard_map/ppermute | solution.py:32
  46.7 0.9 convert_element_type.134
  47.8 0.9 convert_element_type.133
  48.8 0.9 convert_element_type.132
  49.8 0.6 fusion.46
  50.3 0.9 convert_element_type.131
  51.3 0.6 fusion.45
  51.9 3.0 %collective-permute-done.1 = bf16[4,136,128]{2,1,0:T(8,128)(2,1)S(1)} collective-permute-done((bf16[4,136,128]{2,1,0:T(8,128)(2,1)S(1)}, bf16[4,136,128]{2,1,0:T(8,128)(2,1)S(1)}, u32[]{:S(2)}, u32[]{:S(2)}) %collective-permute-start.1) | collective-permute-done | bytes 139296 | tf_op jit(solution)/shard_map/ppermute | solution.py:32
  54.9 0.6 fusion.44
  55.9 0.8 stack.15
  56.7 0.8 select_reduce_fusion
  57.8 0.8 maximum_maximum_fusion.1
  58.9 2.8 %collective-permute-start.9 = (bf16[4,136,128]{2,1,0:T(8,128)(2,1)S(1)}, bf16[4,136,128]{2,1,0:T(8,128)(2,1)S(1)}, u32[]{:S(2)}, u32[]{:S(2)}) collective-permute-start(bf16[4,136,128]{2,1,0:T(8,128)(2,1)S(1)} %pad_maximum_fusion.1), channel_id=1, source_target_pairs={{0,192},{8,200},{16,208},{24,216},{32,224},{40,232},{48,240},{56,2... | collective-permute-start | bytes 417800 | tf_op jit(solution)/shard_map/ppermute | solution.py:32
  61.7 0.5 collective-permute-start.8
  62.1 0.4 collective-permute-start.7
  62.5 0.7 select_reduce_fusion.3
  63.5 3.6 %collective-permute-done.9 = bf16[4,136,128]{2,1,0:T(8,128)(2,1)S(1)} collective-permute-done((bf16[4,136,128]{2,1,0:T(8,128)(2,1)S(1)}, bf16[4,136,128]{2,1,0:T(8,128)(2,1)S(1)}, u32[]{:S(2)}, u32[]{:S(2)}) %collective-permute-start.9) | collective-permute-done | bytes 139296 | tf_op jit(solution)/shard_map/ppermute | solution.py:32
  67.4 0.8 collective-permute-done.7
  68.6 0.4 add_bitcast_fusion
  69.0 0.9 copy-done.1
  69.9 1.4 multiply_reduce_fusion
  71.5 1.9 %copy.116 = f32[2,512,4,128]{3,2,1,0:T(4,128)} copy(f32[2,512,4,128]{1,3,2,0:T(8,128)S(1)} %get-tuple-element.62) | data formatting | bytes 4194304 | tf_op jit(solution)/shard_map/add | solution.py:110
  73.3 1.2 mul.354
  74.9 11.9 %convolution_convert_fusion = bf16[1024,6144]{1,0:T(8,128)(2,1)} fusion(bf16[512,6144]{1,0:T(8,128)(2,1)} %param.13, f32[128,8,4,128]{3,2,1,0:T(4,128)S(1)} %bitcast.144, f32[128,8,4,128]{3,2,1,0:T(4,128)S(1)} %bitcast.145, bf16[1024,512]{1,0:T(8,128)(2,1)} %param.10, f32[512]{0:T(512)S(1)} %copy-done.21), kind=kOutput, calls=%fused_computation | convolution fusion | flops 6452936704 | bytes 24119296 | tf_op jit(solution)/shard_map/dot_general | solution.py:117
  86.9 75.0 %reduce-scatter.2.cloned.1.call-done = bf16[128,6144]{1,0:T(8,128)(2,1)} async-done(((bf16[1024,6144]{1,0:T(8,128)(2,1)}), bf16[128,6144]{1,0:T(8,128)(2,1)}) %reduce-scatter.2.cloned.1.call-update) | async-done | bytes 1572880 | tf_op jit(solution)/shard_map/reduce_scatter | solution.py:116
  (107 shorter events, 5.3 us)
Async XLA Ops:
  6.5 7.3 %copy-start.4 = (bf16[1024,512]{1,0:T(8,128)(2,1)S(1)}, bf16[1024,512]{1,0:T(8,128)(2,1)}, u32[]{:S(2)}) copy-start(bf16[1024,512]{1,0:T(8,128)(2,1)} %param.8) | copy-start | bytes 3145732
  6.5 155.3 %reduce-scatter.2.cloned.1.call-start = ((), (), s32[]{:S(2)}) async-start(), calls=%async_computation.1 | async-start | bytes 14155776 | tf_op jit(solution)/shard_map/reduce_scatter | solution.py:116
  10.5 5.8 %copy-start.7 = (f32[2,4,512]{2,1,0:T(4,128)}, f32[2,4,512]{2,1,0:T(4,128)S(1)}, u32[]{:S(2)}) copy-start(f32[2,4,512]{2,1,0:T(4,128)S(1)} %reduce_window_sum.24) | copy-start | bytes 49156
  10.7 6.5 %copy-start.19 = (bf16[8]{0:T(256)(128)(2,1)}, bf16[8]{0:T(256)(128)(2,1)S(1)}, u32[]{:S(2)}) copy-start(bf16[8]{0:T(256)(128)(2,1)S(1)} %pad.17.clone) | copy-start | bytes 52
  10.8 6.4 %copy-start.20 = (bf16[8]{0:T(256)(128)(2,1)}, bf16[8]{0:T(256)(128)(2,1)S(1)}, u32[]{:S(2)}) copy-start(bf16[8]{0:T(256)(128)(2,1)S(1)} %pad.16.clone) | copy-start | bytes 52
  11.1 5.2 %copy-start.11 = (f32[4]{0:T(128)}, f32[4]{0:T(128)S(1)}, u32[]{:S(2)}) copy-start(f32[4]{0:T(128)S(1)} %broadcast_multiply_fusion) | copy-start | bytes 52
  11.7 22.5 %copy-start.9 = (f32[1,4,1]{1,2,0:T(1,128)}, f32[1,4,1]{1,2,0:T(1,128)S(1)}, u32[]{:S(2)}) copy-start(f32[1,4,1]{1,2,0:T(1,128)S(1)} %get-tuple-element.46) | copy-start | bytes 52
  14.9 19.4 %copy-start.6 = (bf16[2,512,4,128]{1,3,2,0:T(8,128)(2,1)}, bf16[2,512,4,128]{1,3,2,0:T(8,128)(2,1)S(1)}, u32[]{:S(2)}) copy-start(bf16[2,512,4,128]{1,3,2,0:T(8,128)(2,1)S(1)} %copy.99) | copy-start | bytes 3145732
  14.9 19.5 %copy-start.5 = (bf16[1024,512]{1,0:T(8,128)(2,1)S(1)}, bf16[1024,512]{1,0:T(8,128)(2,1)}, u32[]{:S(2)}) copy-start(bf16[1024,512]{1,0:T(8,128)(2,1)} %param.7) | copy-start | bytes 3145732
  16.2 0.8 copy-start.2
  17.4 25.7 %collective-permute-start.6 = (bf16[4,136,128]{2,1,0:T(8,128)(2,1)S(1)}, bf16[4,136,128]{2,1,0:T(8,128)(2,1)}, u32[]{:S(2)}, u32[]{:S(2)}) collective-permute-start(bf16[4,136,128]{2,1,0:T(8,128)(2,1)S(1)} %pad_maximum_fusion), channel_id=1, source_target_pairs={{0,56},{8,48},{16,40},{24,32},{32,24},{40,16},{48,8},{56,0},{64,12... | collective-permute-start | bytes 417800 | tf_op jit(solution)/shard_map/ppermute | solution.py:32
  23.8 20.3 %collective-permute-start.5 = (bf16[4,136,128]{2,1,0:T(8,128)(2,1)S(1)}, bf16[4,136,128]{2,1,0:T(8,128)(2,1)}, u32[]{:S(2)}, u32[]{:S(2)}) collective-permute-start(bf16[4,136,128]{2,1,0:T(8,128)(2,1)S(1)} %pad_maximum_fusion), channel_id=1, source_target_pairs={{0,48},{8,56},{16,32},{24,40},{32,16},{40,24},{48,0},{56,8},{64,11... | collective-permute-start | bytes 417800 | tf_op jit(solution)/shard_map/ppermute | solution.py:32
  24.4 23.4 %collective-permute-start.4 = (bf16[4,136,128]{2,1,0:T(8,128)(2,1)S(1)}, bf16[4,136,128]{2,1,0:T(8,128)(2,1)}, u32[]{:S(2)}, u32[]{:S(2)}) collective-permute-start(bf16[4,136,128]{2,1,0:T(8,128)(2,1)S(1)} %pad_maximum_fusion), channel_id=1, source_target_pairs={{0,40},{8,32},{16,56},{24,48},{32,8},{40,0},{48,24},{56,16},{64,10... | collective-permute-start | bytes 417800 | tf_op jit(solution)/shard_map/ppermute | solution.py:32
  27.8 21.0 %collective-permute-start.3 = (bf16[4,136,128]{2,1,0:T(8,128)(2,1)S(1)}, bf16[4,136,128]{2,1,0:T(8,128)(2,1)}, u32[]{:S(2)}, u32[]{:S(2)}) collective-permute-start(bf16[4,136,128]{2,1,0:T(8,128)(2,1)S(1)} %pad_maximum_fusion), channel_id=1, source_target_pairs={{0,32},{8,40},{16,48},{24,56},{32,0},{40,8},{48,16},{56,24},{64,96... | collective-permute-start | bytes 417800 | tf_op jit(solution)/shard_map/ppermute | solution.py:32
  29.7 20.7 %collective-permute-start.2 = (bf16[4,136,128]{2,1,0:T(8,128)(2,1)S(1)}, bf16[4,136,128]{2,1,0:T(8,128)(2,1)}, u32[]{:S(2)}, u32[]{:S(2)}) collective-permute-start(bf16[4,136,128]{2,1,0:T(8,128)(2,1)S(1)} %pad_maximum_fusion), channel_id=1, source_target_pairs={{0,24},{8,16},{16,8},{24,0},{32,56},{40,48},{48,40},{56,32},{64,88... | collective-permute-start | bytes 417800 | tf_op jit(solution)/shard_map/ppermute | solution.py:32
  34.3 0.6 copy-start.14
  36.3 6.2 %copy-start.15 = (pred[4]{0:T(512)(128)(4,1)S(1)}, pred[4]{0:T(512)(128)(4,1)}, u32[]{:S(2)}) copy-start(pred[4]{0:T(512)(128)(4,1)} %broadcast_compare_fusion.1) | copy-start | bytes 16
  36.3 6.2 %copy-start.18 = (s32[4]{0:T(128)S(1)}, s32[4]{0:T(128)}, u32[]{:S(2)}) copy-start(s32[4]{0:T(128)} %iota_xor_fusion) | copy-start | bytes 52
  42.5 13.1 %copy-start.10 = (f32[1,4,1]{1,2,0:T(1,128)S(1)}, f32[1,4,1]{1,2,0:T(1,128)}, u32[]{:S(2)}) copy-start(f32[1,4,1]{1,2,0:T(1,128)} %copy-done.9) | copy-start | bytes 52
  43.1 11.8 %collective-permute-start.1 = (bf16[4,136,128]{2,1,0:T(8,128)(2,1)S(1)}, bf16[4,136,128]{2,1,0:T(8,128)(2,1)S(1)}, u32[]{:S(2)}, u32[]{:S(2)}) collective-permute-start(bf16[4,136,128]{2,1,0:T(8,128)(2,1)S(1)} %pad_maximum_fusion), channel_id=1, source_target_pairs={{0,16},{8,24},{16,0},{24,8},{32,48},{40,56},{48,32},{56,40},{64,80... | collective-permute-start | bytes 417800 | tf_op jit(solution)/shard_map/ppermute | solution.py:32
  44.1 11.3 %collective-permute-start = (bf16[4,136,128]{2,1,0:T(8,128)(2,1)S(1)}, bf16[4,136,128]{2,1,0:T(8,128)(2,1)S(1)}, u32[]{:S(2)}, u32[]{:S(2)}) collective-permute-start(bf16[4,136,128]{2,1,0:T(8,128)(2,1)S(1)} %pad_maximum_fusion), channel_id=1, source_target_pairs={{0,8},{8,0},{16,24},{24,16},{32,40},{40,32},{48,56},{56,48},{64,72... | collective-permute-start | bytes 417800 | tf_op jit(solution)/shard_map/ppermute | solution.py:32
  55.9 12.6 %copy-start.17 = (pred[4,4]{1,0:T(4,128)(4,1)S(1)}, pred[4,4]{1,0:T(4,128)(4,1)}, u32[]{:S(2)}) copy-start(pred[4,4]{1,0:T(4,128)(4,1)} %compare_and_fusion) | copy-start | bytes 52
  55.9 12.7 %copy-start.16 = (pred[4]{0:T(512)(128)(4,1)S(1)}, pred[4]{0:T(512)(128)(4,1)}, u32[]{:S(2)}) copy-start(pred[4]{0:T(512)(128)(4,1)} %broadcast_compare_fusion.1) | copy-start | bytes 16
  56.6 12.0 %copy-start.3 = (f32[2,4,128,128]{3,2,1,0:T(8,128)S(1)}, f32[2,4,128,128]{3,2,1,0:T(8,128)}, u32[]{:S(2)}) copy-start(f32[2,4,128,128]{3,2,1,0:T(8,128)} %copy-done.2) | copy-start | bytes 1572868
  56.6 12.0 %copy-start.12 = (f32[4]{0:T(128)S(1)}, f32[4]{0:T(128)}, u32[]{:S(2)}) copy-start(f32[4]{0:T(128)} %copy-done.11) | copy-start | bytes 52
  56.6 12.0 %copy-start.13 = (f32[4]{0:T(128)S(1)}, f32[4]{0:T(128)}, u32[]{:S(2)}) copy-start(f32[4]{0:T(128)} %get-tuple-element.60) | copy-start | bytes 52
  58.9 8.3 %collective-permute-start.9 = (bf16[4,136,128]{2,1,0:T(8,128)(2,1)S(1)}, bf16[4,136,128]{2,1,0:T(8,128)(2,1)S(1)}, u32[]{:S(2)}, u32[]{:S(2)}) collective-permute-start(bf16[4,136,128]{2,1,0:T(8,128)(2,1)S(1)} %pad_maximum_fusion.1), channel_id=1, source_target_pairs={{0,192},{8,200},{16,208},{24,216},{32,224},{40,232},{48,240},{56,2... | collective-permute-start | bytes 417800 | tf_op jit(solution)/shard_map/ppermute | solution.py:32
  61.7 5.6 %collective-permute-start.8 = (bf16[4,136,128]{2,1,0:T(8,128)(2,1)S(1)}, bf16[4,136,128]{2,1,0:T(8,128)(2,1)S(1)}, u32[]{:S(2)}, u32[]{:S(2)}) collective-permute-start(bf16[4,136,128]{2,1,0:T(8,128)(2,1)S(1)} %pad_maximum_fusion.1), channel_id=1, source_target_pairs={{0,128},{8,136},{16,144},{24,152},{32,160},{40,168},{48,176},{56,1... | collective-permute-start | bytes 417800 | tf_op jit(solution)/shard_map/ppermute | solution.py:32
  62.1 6.1 %collective-permute-start.7 = (bf16[4,136,128]{2,1,0:T(8,128)(2,1)S(1)}, bf16[4,136,128]{2,1,0:T(8,128)(2,1)S(1)}, u32[]{:S(2)}, u32[]{:S(2)}) collective-permute-start(bf16[4,136,128]{2,1,0:T(8,128)(2,1)S(1)} %pad_maximum_fusion.1), channel_id=1, source_target_pairs={{0,64},{8,72},{16,80},{24,88},{32,96},{40,104},{48,112},{56,120},{... | collective-permute-start | bytes 417800 | tf_op jit(solution)/shard_map/ppermute | solution.py:32
  68.3 1.6 copy-start.1
  68.3 1.6 copy-start.8
  73.3 1.6 copy-start
  73.3 1.6 copy-start.21
Sparse Core Ops, SparseCore 0:
  87.0 74.7 reduce-scatter.1

commit v7 on v4

--- a/solution.py
+++ b/solution.py
@@ -4,7 +4,7 @@
 from jax.sharding import PartitionSpec as P
 
 
-def exclusive_prefix(state, total, axis):
+def exclusive_prefix(state, total, axis, group):
     n = lax.axis_size(axis)
     me = lax.axis_index(axis)
     heads, rows, cols = state.shape
@@ -30,7 +30,8 @@
     prefix = (jnp.zeros_like(state), jnp.zeros_like(total))
     s = 1
     while s < n:
-        other = unpack(lax.ppermute(pack(*block), axis, [(i, i ^ s) for i in range(n)]))
+        flip = 2 * s - 1 if s < group else 2 * s - group
+        other = unpack(lax.ppermute(pack(*block), axis, [(i, i ^ flip) for i in range(n)]))
         lower = (me & s) != 0
         new_prefix = join(other, prefix)
         prefix = tuple(jnp.where(lower, a, b) for a, b in zip(new_prefix, prefix))
@@ -71,10 +72,23 @@
         offsets.append(before)
         run = jnp.exp(last[b])[:, None, None] * run + block_state[b]
         before = before + last[b]
-    local_state = run
-    own_total = before
 
-    incoming = exclusive_prefix(local_state, own_total, "ctx")
+    later = (jnp.arange(local_rows)[:, None] > jnp.arange(local_rows)[None, :]).astype(jnp.float32)
+    suffix = jnp.dot(log_decay, later, precision=hp)
+    key_tail = keys.reshape(local_rows, head_count, head_width).astype(jnp.float32) * jnp.exp(
+        suffix
+    ).T[:, :, None]
+    local_state = jnp.einsum(
+        "shd,she->hde",
+        key_tail,
+        values.reshape(local_rows, head_count, head_width).astype(jnp.float32),
+        precision=hp,
+    )
+    own_total = jnp.sum(log_decay, axis=1)
+    ctx_size = lax.axis_size("ctx")
+    group = 8 if ctx_size % 8 == 0 else ctx_size
+
+    incoming = exclusive_prefix(local_state, own_total, "ctx", group)
 
     lower = jnp.arange(width_blk)[:, None] >= jnp.arange(width_blk)[None, :]
     spread = cum[:, :, :, None] - cum[:, :, None, :]

time: 160 us -> 164 us (1.025)
  other arithmetic: 5.01 us -> 10.3 us
  starting transfers between devices: 17.6 us -> 13.3 us
  local copies, waits for them, and re-layouts: 10.6 us -> 14.6 us
  waiting for transfers between devices: 90 us -> 87.8 us
  matrix products: 22.5 us -> 24.2 us
    ppermute x5, starting transfers between devices: 17.6 us -> 13.3 us  [exclusive_prefix(): lax.ppermute(pack(*block), axis, [(i, i ^ flip) for i in range(n)])]
    slice x0 -> x1, matrix products: none -> 2.21 us  [on_device(): run = jnp.exp(last[b])[:, None, None] * run + block_state[b]]
  transfers between devices with their start and end apart: 6 -> 6, of which waited for: 5 -> 4; matrix products, arithmetic and copies ran while one was open for 5% -> 10% of each run, Pallas kernels for 0% -> 0%
where the time goes in v7:
time: 164 us
  waiting for transfers between devices  87.8 us (54%)
  matrix products  24.2 us (15%)
  local copies, waits for them, and re-layouts  14.6 us (9%)
  between operations  13.7 us (8%)
  starting transfers between devices  13.3 us (8%)
  other arithmetic  10.3 us (6%)
    reduce_scatter x1, waiting for transfers between devices, on_device(): lax.psum_scatter(jnp.dot(normed, out_weight, preferred_element_type=jnp.f...  76.3 us
    ppermute x5, starting transfers between devices, exclusive_prefix(): lax.ppermute(pack(*block), axis, [(i, i ^ flip) for i in range(n)])  13.3 us
    dot_general x1, matrix products, on_device(): jnp.dot(normed, out_weight, preferred_element_type=jnp.float32)  11.9 us
    ppermute x5, waiting for transfers between devices, exclusive_prefix(): lax.ppermute(pack(*block), axis, [(i, i ^ flip) for i in range(n)])  11.5 us
    dot_general x1, matrix products, on_device(): jnp.einsum('bhts,bshd->bthd', weighted, v, preferred_element_type=jnp.flo...  6.1 us
  transfers between devices with their start and end apart: 6, of which 4 were waited for; matrix products, arithmetic and copies ran while one was open for 10% of the time, Pallas kernels for 0%

profile of v7, /device:TPU:1, one launch (start us, length us, event | category | flops | bytes accessed | tf_op | source)
XLA Modules:
  0.0 164.0 jit_solution(614926865896127436)
XLA Ops:
  6.5 0.8 reduce_sum.22
  7.4 0.5 fusion.58
  7.9 1.4 fusion.29
  9.4 0.1 copy.82
  9.8 1.5 copy.102
  11.3 1.2 fusion.59
  12.7 2.5 %collective-permute-start = (bf16[4,136,128]{2,1,0:T(8,128)(2,1)S(1)}, bf16[4,136,128]{2,1,0:T(8,128)(2,1)}, u32[]{:S(2)}, u32[]{:S(2)}) collective-permute-start(bf16[4,136,128]{2,1,0:T(8,128)(2,1)S(1)} %pad_maximum_fusion), channel_id=1, source_target_pairs={{0,8},{8,0},{16,24},{24,16},{32,40},{40,32},{48,56},{56,48},{64,72... | collective-permute-start | bytes 417800 | tf_op jit(solution)/shard_map/ppermute | solution.py:34
  15.2 0.7 reshape.427
  16.0 2.4 %reduce-window.6 = f32[2,4,4,128]{3,2,1,0:T(4,128)S(1)} reduce-window(f32[2,4,4,128]{3,2,1,0:T(4,128)S(1)} %copy.101, f32[]{:T(128)} %constant.14.clone.1), window={size=1x1x1x128 pad=0_0x0_0x0_0x127_0}, to_apply=%region_0.0 | reduce-window | flops 520192 | bytes 32772 | tf_op jit(solution)/shard_map/reduce-window
  18.4 0.2 slice_reduce_fusion
  18.6 0.4 reduce-window.9
  19.0 1.1 reshape.430
  20.2 0.3 reshape.426
  20.5 0.6 reduce_window_sum.24
  21.2 1.3 reshape.425
  22.5 1.5 copy.93
  24.1 0.9 convert_element_type.232
  25.0 0.7 exponential_reduce_fusion
  25.7 0.7 fusion.57
  26.5 0.1 copy.84
  26.6 0.8 maximum_maximum_fusion.1
  27.4 0.7 fusion.53
  28.2 2.8 %collective-permute-start.1 = (bf16[4,136,128]{2,1,0:T(8,128)(2,1)S(1)}, bf16[4,136,128]{2,1,0:T(8,128)(2,1)S(1)}, u32[]{:S(2)}, u32[]{:S(2)}) collective-permute-start(bf16[4,136,128]{2,1,0:T(8,128)(2,1)S(1)} %pad_maximum_fusion.1), channel_id=1, source_target_pairs={{0,24},{8,16},{16,8},{24,0},{32,56},{40,48},{48,40},{56,32},{64,88... | collective-permute-start | bytes 417800 | tf_op jit(solution)/shard_map/ppermute | solution.py:34
  31.1 6.1 %fusion = f32[2,4,512,128]{2,3,1,0:T(8,128)} fusion(f32[2,4,512]{2,1,0:T(4,128)} %reduce_window_sum.24, pred[512,512]{1,0:T(8,128)(4,1)S(1)} %iota_compare_fusion.4, bf16[2,512,4,128]{1,3,2,0:T(8,128)(2,1)} %copy.93, bf16[2,512,4,128]{3,2,1,0:T(4,128)(2,1)S(1)} %copy-done.4, bf16[2,512,4,128]{3,2,1,0:T(4,128)(2,1)S(1)} %reshape.425), kind=kOutput, calls=%fused_computation.2 | convolution fusion | flops 1082130432 | bytes 5521408 | tf_op jit(solution)/shard_map/bhts,bshd->bthd/dot_general | solution.py:98
  37.2 0.8 slice.95
  38.1 0.1 exponential_reduce_fusion.6
  38.5 0.9 fusion.56
  39.5 3.6 %collective-permute-start.2 = (bf16[4,136,128]{2,1,0:T(8,128)(2,1)S(1)}, bf16[4,136,128]{2,1,0:T(8,128)(2,1)S(1)}, u32[]{:S(2)}, u32[]{:S(2)}) collective-permute-start(bf16[4,136,128]{2,1,0:T(8,128)(2,1)S(1)} %pad_maximum_fusion.2), channel_id=1, source_target_pairs={{0,56},{8,48},{16,40},{24,32},{32,24},{40,16},{48,8},{56,0},{64,12... | collective-permute-start | bytes 417800 | tf_op jit(solution)/shard_map/ppermute | solution.py:34
  43.1 0.8 slice_exponential_fusion
  44.0 5.9 %collective-permute-done.2 = bf16[4,136,128]{2,1,0:T(8,128)(2,1)S(1)} collective-permute-done((bf16[4,136,128]{2,1,0:T(8,128)(2,1)S(1)}, bf16[4,136,128]{2,1,0:T(8,128)(2,1)S(1)}, u32[]{:S(2)}, u32[]{:S(2)}) %collective-permute-start.2) | collective-permute-done | bytes 139296 | tf_op jit(solution)/shard_map/ppermute | solution.py:34
  50.0 0.1 exponential_reduce_fusion.4
  50.2 0.1 copy.89
  50.4 0.1 fusion.54
  50.6 1.4 collective-permute-start.3
  52.1 3.1 %collective-permute-done.3 = bf16[4,136,128]{2,1,0:T(8,128)(2,1)S(1)} collective-permute-done((bf16[4,136,128]{2,1,0:T(8,128)(2,1)S(1)}, bf16[4,136,128]{2,1,0:T(8,128)(2,1)S(1)}, u32[]{:S(2)}, u32[]{:S(2)}) %collective-permute-start.3) | collective-permute-done | bytes 139296 | tf_op jit(solution)/shard_map/ppermute | solution.py:34
  55.2 0.1 fusion.46
  55.6 0.2 select_convert_fusion
  56.0 3.0 %collective-permute-start.4 = (bf16[4,136,128]{2,1,0:T(8,128)(2,1)S(1)}, bf16[4,136,128]{2,1,0:T(8,128)(2,1)S(1)}, u32[]{:S(2)}, u32[]{:S(2)}) collective-permute-start(bf16[4,136,128]{2,1,0:T(8,128)(2,1)S(1)} %pad_maximum_fusion.4), channel_id=1, source_target_pairs={{0,192},{8,200},{16,208},{24,216},{32,224},{40,232},{48,240},{56,2... | collective-permute-start | bytes 417800 | tf_op jit(solution)/shard_map/ppermute | solution.py:34
  58.9 2.4 %collective-permute-done.4 = bf16[4,136,128]{2,1,0:T(8,128)(2,1)S(1)} collective-permute-done((bf16[4,136,128]{2,1,0:T(8,128)(2,1)S(1)}, bf16[4,136,128]{2,1,0:T(8,128)(2,1)S(1)}, u32[]{:S(2)}, u32[]{:S(2)}) %collective-permute-start.4) | collective-permute-done | bytes 139296 | tf_op jit(solution)/shard_map/ppermute | solution.py:34
  61.4 0.2 add_select_fusion
  61.6 2.2 %fusion.26 = f32[1,4,128,128]{3,2,1,0:T(8,128)S(1)} fusion(bf16[2,512,4,128]{1,3,2,0:T(8,128)(2,1)} %copy.93, f32[2,512,4]{1,2,0:T(4,128)S(1)} %get-tuple-element.30, bf16[2,512,4,128]{3,2,1,0:T(4,128)(2,1)} %reshape.430, f32[4,128,128]{2,1,0:T(8,128)S(1)} %add_select_fusion, f32[4]{0:T(128)S(1)} %bitcast.99, f32[4]{0:T(128)S(1)} %broadcast_multiply_fusion), kind=kOutput, calls=%fused_computation.25 | convolution fusion | flops 403898368 | bytes 2637856 | tf_op jit(solution)/shard_map/slice | solution.py:73
  63.8 1.4 multiply_reduce_fusion
  65.2 0.2 copy.99
  65.4 1.9 %copy.98 = f32[2,512,4,128]{3,2,1,0:T(4,128)} copy(f32[2,512,4,128]{1,3,2,0:T(8,128)S(1)} %get-tuple-element.41) | data formatting | bytes 4194304 | tf_op jit(solution)/shard_map/add | solution.py:106
  67.3 1.2 mul.237
  68.5 0.4 copy-done.2
  68.9 11.9 %convolution_convert_fusion = bf16[1024,6144]{1,0:T(8,128)(2,1)} fusion(bf16[512,6144]{1,0:T(8,128)(2,1)} %param.13, f32[128,8,4,128]{3,2,1,0:T(4,128)S(1)} %bitcast.91, f32[128,8,4,128]{3,2,1,0:T(4,128)S(1)} %bitcast.92, bf16[1024,512]{1,0:T(8,128)(2,1)} %param.10, f32[512]{0:T(512)S(1)} %copy-done.18), kind=kOutput, calls=%fused_computation | convolution fusion | flops 6452936704 | bytes 24119296 | tf_op jit(solution)/shard_map/dot_general | solution.py:113
  80.8 76.3 %reduce-scatter.2.cloned.1.call-done = bf16[128,6144]{1,0:T(8,128)(2,1)} async-done(((bf16[1024,6144]{1,0:T(8,128)(2,1)}), bf16[128,6144]{1,0:T(8,128)(2,1)}) %reduce-scatter.2.cloned.1.call-update) | async-done | bytes 1572880 | tf_op jit(solution)/shard_map/reduce_scatter | solution.py:112
  (86 shorter events, 2.4 us)
Async XLA Ops:
  6.5 150.6 %reduce-scatter.2.cloned.1.call-start = ((), (), s32[]{:S(2)}) async-start(), calls=%async_computation.1 | async-start | bytes 14155776 | tf_op jit(solution)/shard_map/reduce_scatter | solution.py:112
  7.4 13.1 %copy-start.12 = (f32[4]{0:T(128)}, f32[4]{0:T(128)S(1)}, u32[]{:S(2)}) copy-start(f32[4]{0:T(128)S(1)} %reduce_sum.22) | copy-start | bytes 52
  7.9 3.3 %copy-start = (bf16[1024,512]{1,0:T(8,128)(2,1)S(1)}, bf16[1024,512]{1,0:T(8,128)(2,1)}, u32[]{:S(2)}) copy-start(bf16[1024,512]{1,0:T(8,128)(2,1)} %param.9) | copy-start | bytes 3145732
  9.6 2.9 %copy-start.6 = (bf16[8]{0:T(256)(128)(2,1)}, bf16[8]{0:T(256)(128)(2,1)S(1)}, u32[]{:S(2)}) copy-start(bf16[8]{0:T(256)(128)(2,1)S(1)} %pad.31.clone) | copy-start | bytes 52
  9.6 2.8 %copy-start.9 = (bf16[8]{0:T(256)(128)(2,1)}, bf16[8]{0:T(256)(128)(2,1)S(1)}, u32[]{:S(2)}) copy-start(bf16[8]{0:T(256)(128)(2,1)S(1)} %pad.30.clone) | copy-start | bytes 52
  12.5 7.7 %copy-start.1 = (bf16[1024,512]{1,0:T(8,128)(2,1)S(1)}, bf16[1024,512]{1,0:T(8,128)(2,1)}, u32[]{:S(2)}) copy-start(bf16[1024,512]{1,0:T(8,128)(2,1)} %param.8) | copy-start | bytes 3145732
  12.7 11.4 %collective-permute-start = (bf16[4,136,128]{2,1,0:T(8,128)(2,1)S(1)}, bf16[4,136,128]{2,1,0:T(8,128)(2,1)}, u32[]{:S(2)}, u32[]{:S(2)}) collective-permute-start(bf16[4,136,128]{2,1,0:T(8,128)(2,1)S(1)} %pad_maximum_fusion), channel_id=1, source_target_pairs={{0,8},{8,0},{16,24},{24,16},{32,40},{40,32},{48,56},{56,48},{64,72... | collective-permute-start | bytes 417800 | tf_op jit(solution)/shard_map/ppermute | solution.py:34
  22.5 8.6 %copy-start.4 = (bf16[2,512,4,128]{3,2,1,0:T(4,128)(2,1)S(1)}, bf16[2,512,4,128]{3,2,1,0:T(4,128)(2,1)}, u32[]{:S(2)}) copy-start(bf16[2,512,4,128]{3,2,1,0:T(4,128)(2,1)} %reshape.430) | copy-start | bytes 3145732
  25.7 2.5 %copy-start.16 = (f32[4]{0:T(128)}, f32[4]{0:T(128)S(1)}, u32[]{:S(2)}) copy-start(f32[4]{0:T(128)S(1)} %get-tuple-element.15) | copy-start | bytes 52
  26.4 1.0 copy-start.13
  28.2 10.0 %copy-start.14 = (f32[4,1]{0,1:T(1,128)S(1)}, f32[4,1]{0,1:T(1,128)}, u32[]{:S(2)}) copy-start(f32[4,1]{0,1:T(1,128)} %copy-done.13) | copy-start | bytes 52
  28.2 10.2 %copy-start.7 = (bf16[8]{0:T(256)(128)(2,1)S(1)}, bf16[8]{0:T(256)(128)(2,1)}, u32[]{:S(2)}) copy-start(bf16[8]{0:T(256)(128)(2,1)} %copy-done.6) | copy-start | bytes 52
  28.2 10.2 %copy-start.10 = (bf16[8]{0:T(256)(128)(2,1)S(1)}, bf16[8]{0:T(256)(128)(2,1)}, u32[]{:S(2)}) copy-start(bf16[8]{0:T(256)(128)(2,1)} %copy-done.9) | copy-start | bytes 52
  28.2 9.8 %collective-permute-start.1 = (bf16[4,136,128]{2,1,0:T(8,128)(2,1)S(1)}, bf16[4,136,128]{2,1,0:T(8,128)(2,1)S(1)}, u32[]{:S(2)}, u32[]{:S(2)}) collective-permute-start(bf16[4,136,128]{2,1,0:T(8,128)(2,1)S(1)} %pad_maximum_fusion.1), channel_id=1, source_target_pairs={{0,24},{8,16},{16,8},{24,0},{32,56},{40,48},{48,40},{56,32},{64,88... | collective-permute-start | bytes 417800 | tf_op jit(solution)/shard_map/ppermute | solution.py:34
  37.2 12.9 %copy-start.15 = (f32[4,1]{0,1:T(1,128)S(1)}, f32[4,1]{0,1:T(1,128)}, u32[]{:S(2)}) copy-start(f32[4,1]{0,1:T(1,128)} %copy-done.13) | copy-start | bytes 52
  37.2 13.2 %copy-start.8 = (bf16[8]{0:T(256)(128)(2,1)S(1)}, bf16[8]{0:T(256)(128)(2,1)}, u32[]{:S(2)}) copy-start(bf16[8]{0:T(256)(128)(2,1)} %copy-done.6) | copy-start | bytes 52
  37.2 13.2 %copy-start.11 = (bf16[8]{0:T(256)(128)(2,1)S(1)}, bf16[8]{0:T(256)(128)(2,1)}, u32[]{:S(2)}) copy-start(bf16[8]{0:T(256)(128)(2,1)} %copy-done.9) | copy-start | bytes 52
  37.2 14.8 %copy-start.5 = (f32[2,4,512]{2,1,0:T(4,128)S(1)}, f32[2,4,512]{2,1,0:T(4,128)}, u32[]{:S(2)}) copy-start(f32[2,4,512]{2,1,0:T(4,128)} %reduce_window_sum.24) | copy-start | bytes 49156
  38.5 22.9 %copy-start.17 = (f32[4]{0:T(128)S(1)}, f32[4]{0:T(128)}, u32[]{:S(2)}) copy-start(f32[4]{0:T(128)} %get-tuple-element.12) | copy-start | bytes 52
  39.5 10.5 %collective-permute-start.2 = (bf16[4,136,128]{2,1,0:T(8,128)(2,1)S(1)}, bf16[4,136,128]{2,1,0:T(8,128)(2,1)S(1)}, u32[]{:S(2)}, u32[]{:S(2)}) collective-permute-start(bf16[4,136,128]{2,1,0:T(8,128)(2,1)S(1)} %pad_maximum_fusion.2), channel_id=1, source_target_pairs={{0,56},{8,48},{16,40},{24,32},{32,24},{40,16},{48,8},{56,0},{64,12... | collective-permute-start | bytes 417800 | tf_op jit(solution)/shard_map/ppermute | solution.py:34
  50.6 4.6 %collective-permute-start.3 = (bf16[4,136,128]{2,1,0:T(8,128)(2,1)S(1)}, bf16[4,136,128]{2,1,0:T(8,128)(2,1)S(1)}, u32[]{:S(2)}, u32[]{:S(2)}) collective-permute-start(bf16[4,136,128]{2,1,0:T(8,128)(2,1)S(1)} %pad_maximum_fusion.3), channel_id=1, source_target_pairs={{0,64},{8,72},{16,80},{24,88},{32,96},{40,104},{48,112},{56,120},{... | collective-permute-start | bytes 417800 | tf_op jit(solution)/shard_map/ppermute | solution.py:34
  56.0 5.4 %collective-permute-start.4 = (bf16[4,136,128]{2,1,0:T(8,128)(2,1)S(1)}, bf16[4,136,128]{2,1,0:T(8,128)(2,1)S(1)}, u32[]{:S(2)}, u32[]{:S(2)}) collective-permute-start(bf16[4,136,128]{2,1,0:T(8,128)(2,1)S(1)} %pad_maximum_fusion.4), channel_id=1, source_target_pairs={{0,192},{8,200},{16,208},{24,216},{32,224},{40,232},{48,240},{56,2... | collective-permute-start | bytes 417800 | tf_op jit(solution)/shard_map/ppermute | solution.py:34
  61.4 2.4 %copy-start.3 = (f32[2,4,512,128]{2,3,1,0:T(8,128)S(1)}, f32[2,4,512,128]{2,3,1,0:T(8,128)}, u32[]{:S(2)}) copy-start(f32[2,4,512,128]{2,3,1,0:T(8,128)} %fusion) | copy-start | bytes 6291460
  67.3 1.6 copy-start.2
  67.3 1.6 copy-start.18
Sparse Core Ops, SparseCore 0:
  80.9 76.1 reduce-scatter.1

commit v8 on v4

--- a/solution.py
+++ b/solution.py
@@ -4,7 +4,7 @@
 from jax.sharding import PartitionSpec as P
 
 
-def exclusive_prefix(state, total, axis):
+def exclusive_prefix(state, total, axis, group):
     n = lax.axis_size(axis)
     me = lax.axis_index(axis)
     heads, rows, cols = state.shape
@@ -30,7 +30,8 @@
     prefix = (jnp.zeros_like(state), jnp.zeros_like(total))
     s = 1
     while s < n:
-        other = unpack(lax.ppermute(pack(*block), axis, [(i, i ^ s) for i in range(n)]))
+        flip = 2 * s - 1 if s < group else 2 * s - group
+        other = unpack(lax.ppermute(pack(*block), axis, [(i, i ^ flip) for i in range(n)]))
         lower = (me & s) != 0
         new_prefix = join(other, prefix)
         prefix = tuple(jnp.where(lower, a, b) for a, b in zip(new_prefix, prefix))
@@ -74,7 +75,9 @@
     local_state = run
     own_total = before
 
-    incoming = exclusive_prefix(local_state, own_total, "ctx")
+    ctx_size = lax.axis_size("ctx")
+    group = 8 if ctx_size % 8 == 0 else ctx_size
+    incoming = exclusive_prefix(local_state, own_total, "ctx", group)
 
     lower = jnp.arange(width_blk)[:, None] >= jnp.arange(width_blk)[None, :]
     spread = cum[:, :, :, None] - cum[:, :, None, :]

time: 160 us -> 156 us (0.975)
  waiting for transfers between devices: 90 us -> 87.1 us
    ppermute x5, waiting for transfers between devices: 12.7 us -> 8.7 us  [exclusive_prefix(): lax.ppermute(pack(*block), axis, [(i, i ^ flip) for i in range(n)])]
where the time goes in v8:
time: 156 us; the launch traced here: 155 us
  waiting for transfers between devices  87.1 us (56%)
  matrix products  22.5 us (14%)
  starting transfers between devices  16.4 us (11%)
  between operations  13.7 us (9%)
  local copies, waits for them, and re-layouts  10.6 us (7%)
  other arithmetic  5.01 us (3%)
    reduce_scatter x1, waiting for transfers between devices, on_device(): lax.psum_scatter(jnp.dot(normed, out_weight, preferred_element_type=jnp.f...  78.4 us
    ppermute x5, starting transfers between devices, exclusive_prefix(): lax.ppermute(pack(*block), axis, [(i, i ^ flip) for i in range(n)])  16.4 us
    dot_general x1, matrix products, on_device(): jnp.dot(normed, out_weight, preferred_element_type=jnp.float32)  11.9 us
    ppermute x5, waiting for transfers between devices, exclusive_prefix(): lax.ppermute(pack(*block), axis, [(i, i ^ flip) for i in range(n)])  8.7 us
    dot_general x1, matrix products, on_device(): jnp.einsum('bhts,bshd->bthd', weighted, v, preferred_element_type=jnp.flo...  6.43 us
  transfers between devices with their start and end apart: 6, of which 5 were waited for; matrix products, arithmetic and copies ran while one was open for 5% of the time, Pallas kernels for 0%

profile of v8, /device:TPU:1, one launch (start us, length us, event | category | flops | bytes accessed | tf_op | source)
XLA Modules:
  0.0 155.3 jit_solution(11452684841669211587)
XLA Ops:
  6.5 0.8 reshape.503
  7.4 2.4 %reduce-window.6 = f32[2,4,4,128]{3,2,1,0:T(4,128)S(1)} reduce-window(f32[2,4,4,128]{3,2,1,0:T(4,128)S(1)} %copy.97, f32[]{:T(128)} %constant.14.clone.1), window={size=1x1x1x128 pad=0_0x0_0x0_0x127_0}, to_apply=%region_0.0 | reduce-window | flops 520192 | bytes 32772 | tf_op jit(solution)/shard_map/reduce-window
  9.8 0.2 slice_reduce_fusion
  10.0 0.4 reduce-window.9
  10.6 0.1 copy.99
  11.0 0.1 copy.100
  11.1 0.1 copy.82
  11.2 0.1 copy.81
  11.4 1.3 reshape.506
  12.8 0.3 reshape.502
  13.1 0.7 copy.78
  13.8 1.3 fusion.11
  15.1 0.1 fusion.36
  15.4 2.5 %collective-permute-start = (bf16[4,136,128]{2,1,0:T(8,128)(2,1)S(1)}, bf16[4,136,128]{2,1,0:T(8,128)(2,1)S(1)}, u32[]{:S(2)}, u32[]{:S(2)}) collective-permute-start(bf16[4,136,128]{2,1,0:T(8,128)(2,1)S(1)} %pad_maximum_fusion), channel_id=1, source_target_pairs={{0,8},{8,0},{16,24},{24,16},{32,40},{40,32},{48,56},{56,48},{64,72... | collective-permute-start | bytes 417800 | tf_op jit(solution)/shard_map/ppermute | solution.py:34
  18.0 2.4 %collective-permute-done = bf16[4,136,128]{2,1,0:T(8,128)(2,1)S(1)} collective-permute-done((bf16[4,136,128]{2,1,0:T(8,128)(2,1)S(1)}, bf16[4,136,128]{2,1,0:T(8,128)(2,1)S(1)}, u32[]{:S(2)}, u32[]{:S(2)}) %collective-permute-start) | collective-permute-done | bytes 139296 | tf_op jit(solution)/shard_map/ppermute | solution.py:34
  20.4 0.1 exponential_reduce_fusion
  20.5 0.1 copy.83
  20.6 0.1 copy.84
  20.8 0.2 fusion.41
  21.1 4.9 %collective-permute-start.1 = (bf16[4,136,128]{2,1,0:T(8,128)(2,1)S(1)}, bf16[4,136,128]{2,1,0:T(8,128)(2,1)S(1)}, u32[]{:S(2)}, u32[]{:S(2)}) collective-permute-start(bf16[4,136,128]{2,1,0:T(8,128)(2,1)S(1)} %pad_maximum_fusion.1), channel_id=1, source_target_pairs={{0,24},{8,16},{16,8},{24,0},{32,56},{40,48},{48,40},{56,32},{64,88... | collective-permute-start | bytes 417800 | tf_op jit(solution)/shard_map/ppermute | solution.py:34
  26.0 2.5 %collective-permute-done.1 = bf16[4,136,128]{2,1,0:T(8,128)(2,1)S(1)} collective-permute-done((bf16[4,136,128]{2,1,0:T(8,128)(2,1)S(1)}, bf16[4,136,128]{2,1,0:T(8,128)(2,1)S(1)}, u32[]{:S(2)}, u32[]{:S(2)}) %collective-permute-start.1) | collective-permute-done | bytes 139296 | tf_op jit(solution)/shard_map/ppermute | solution.py:34
  28.6 0.1 exponential_reduce_fusion.6
  28.7 0.1 copy.86
  28.8 0.1 copy.87
  29.0 0.1 fusion.37
  29.2 4.6 %collective-permute-start.2 = (bf16[4,136,128]{2,1,0:T(8,128)(2,1)S(1)}, bf16[4,136,128]{2,1,0:T(8,128)(2,1)S(1)}, u32[]{:S(2)}, u32[]{:S(2)}) collective-permute-start(bf16[4,136,128]{2,1,0:T(8,128)(2,1)S(1)} %pad_maximum_fusion.2), channel_id=1, source_target_pairs={{0,56},{8,48},{16,40},{24,32},{32,24},{40,16},{48,8},{56,0},{64,12... | collective-permute-start | bytes 417800 | tf_op jit(solution)/shard_map/ppermute | solution.py:34
  33.8 2.4 %collective-permute-done.2 = bf16[4,136,128]{2,1,0:T(8,128)(2,1)S(1)} collective-permute-done((bf16[4,136,128]{2,1,0:T(8,128)(2,1)S(1)}, bf16[4,136,128]{2,1,0:T(8,128)(2,1)S(1)}, u32[]{:S(2)}, u32[]{:S(2)}) %collective-permute-start.2) | collective-permute-done | bytes 139296 | tf_op jit(solution)/shard_map/ppermute | solution.py:34
  36.3 0.1 exponential_reduce_fusion.4
  36.4 0.1 copy.88
  36.5 0.1 copy.89
  36.7 0.2 fusion.38
  37.0 1.4 collective-permute-start.3
  38.4 1.3 reshape.501
  39.8 1.4 collective-permute-done.3
  41.2 0.1 fusion.29
  41.4 0.1 copy.90
  41.5 0.1 copy.91
  41.7 0.1 select_convert_fusion
  41.9 3.0 %collective-permute-start.4 = (bf16[4,136,128]{2,1,0:T(8,128)(2,1)S(1)}, bf16[4,136,128]{2,1,0:T(8,128)(2,1)S(1)}, u32[]{:S(2)}, u32[]{:S(2)}) collective-permute-start(bf16[4,136,128]{2,1,0:T(8,128)(2,1)S(1)} %pad_maximum_fusion.4), channel_id=1, source_target_pairs={{0,192},{8,200},{16,208},{24,216},{32,224},{40,232},{48,240},{56,2... | collective-permute-start | bytes 417800 | tf_op jit(solution)/shard_map/ppermute | solution.py:34
  44.9 6.4 %fusion = f32[2,4,512,128]{2,3,1,0:T(8,128)} fusion(f32[2,4,512]{2,1,0:T(4,128)S(1)} %reduce_window_sum.24, pred[512,512]{1,0:T(8,128)(4,1)S(1)} %iota_compare_fusion, bf16[2,512,4,128]{1,3,2,0:T(8,128)(2,1)} %copy-done.3, bf16[2,512,4,128]{3,2,1,0:T(4,128)(2,1)} %copy-done.2, bf16[2,512,4,128]{3,2,1,0:T(4,128)(2,1)S(1)} %reshape.501), kind=kOutput, calls=%fused_computation.2 | convolution fusion | flops 1082130432 | bytes 5521408 | tf_op jit(solution)/shard_map/bhts,bshd->bthd/dot_general | solution.py:87
  51.3 0.3 add_bitcast_fusion
  51.6 2.9 %multiply_reduce_fusion = (f32[2,512,4]{1,2,0:T(4,128)S(1)}, f32[2,512,4,128]{1,3,2,0:T(8,128)S(1)}) fusion(bf16[2,512,4,128]{3,2,1,0:T(4,128)(2,1)S(1)} %reshape.501, f32[1,4,128,128]{3,2,1,0:T(8,128)S(1)} %get-tuple-element.20, f32[1,4,128,128]{3,2,1,0:T(8,128)S(1)} %bitcast.107, f32[2,512,4]{1,2,0:T(4,128)S(1)} %get-tuple-element.39, ...), kind=kOutput, calls=%fused_computation.14 | convolution fusion | flops 807530496 | bytes 5799936 | tf_op jit(solution)/shard_map/bthd,bhde->bthe/dot_general | solution.py:92
  54.5 0.2 copy.95
  54.7 1.9 %copy.94 = f32[2,512,4,128]{3,2,1,0:T(4,128)} copy(f32[2,512,4,128]{1,3,2,0:T(8,128)S(1)} %get-tuple-element.47) | data formatting | bytes 4194304 | tf_op jit(solution)/shard_map/add | solution.py:95
  56.6 1.2 mul.237
  57.8 0.4 copy-done
  58.1 11.9 %convolution_convert_fusion = bf16[1024,6144]{1,0:T(8,128)(2,1)} fusion(bf16[512,6144]{1,0:T(8,128)(2,1)} %param.13, f32[128,8,4,128]{3,2,1,0:T(4,128)S(1)} %bitcast.105, f32[128,8,4,128]{3,2,1,0:T(4,128)S(1)} %bitcast.106, bf16[1024,512]{1,0:T(8,128)(2,1)} %param.10, f32[512]{0:T(512)S(1)} %copy-done.4), kind=kOutput, calls=%fused_computation | convolution fusion | flops 6452936704 | bytes 24119296 | tf_op jit(solution)/shard_map/dot_general | solution.py:102
  70.1 78.4 %reduce-scatter.2.cloned.1.call-done = bf16[128,6144]{1,0:T(8,128)(2,1)} async-done(((bf16[1024,6144]{1,0:T(8,128)(2,1)}), bf16[128,6144]{1,0:T(8,128)(2,1)}) %reduce-scatter.2.cloned.1.call-update) | async-done | bytes 1572880 | tf_op jit(solution)/shard_map/reduce_scatter | solution.py:101
  (57 shorter events, 1.8 us)
Async XLA Ops:
  6.5 6.2 %copy-start.1 = (bf16[1024,512]{1,0:T(8,128)(2,1)S(1)}, bf16[1024,512]{1,0:T(8,128)(2,1)}, u32[]{:S(2)}) copy-start(bf16[1024,512]{1,0:T(8,128)(2,1)} %param.8) | copy-start | bytes 3145732
  6.5 141.9 %reduce-scatter.2.cloned.1.call-start = ((), (), s32[]{:S(2)}) async-start(), calls=%async_computation.1 | async-start | bytes 14155776 | tf_op jit(solution)/shard_map/reduce_scatter | solution.py:101
  12.8 24.1 %copy-start.2 = (bf16[2,512,4,128]{3,2,1,0:T(4,128)(2,1)}, bf16[2,512,4,128]{3,2,1,0:T(4,128)(2,1)S(1)}, u32[]{:S(2)}) copy-start(bf16[2,512,4,128]{3,2,1,0:T(4,128)(2,1)S(1)} %reshape.506) | copy-start | bytes 3145732
  13.8 4.3 %copy-start.3 = (bf16[2,512,4,128]{1,3,2,0:T(8,128)(2,1)}, bf16[2,512,4,128]{1,3,2,0:T(8,128)(2,1)S(1)}, u32[]{:S(2)}) copy-start(bf16[2,512,4,128]{1,3,2,0:T(8,128)(2,1)S(1)} %copy.78) | copy-start | bytes 3145732
  15.4 5.0 %collective-permute-start = (bf16[4,136,128]{2,1,0:T(8,128)(2,1)S(1)}, bf16[4,136,128]{2,1,0:T(8,128)(2,1)S(1)}, u32[]{:S(2)}, u32[]{:S(2)}) collective-permute-start(bf16[4,136,128]{2,1,0:T(8,128)(2,1)S(1)} %pad_maximum_fusion), channel_id=1, source_target_pairs={{0,8},{8,0},{16,24},{24,16},{32,40},{40,32},{48,56},{56,48},{64,72... | collective-permute-start | bytes 417800 | tf_op jit(solution)/shard_map/ppermute | solution.py:34
  21.1 7.5 %collective-permute-start.1 = (bf16[4,136,128]{2,1,0:T(8,128)(2,1)S(1)}, bf16[4,136,128]{2,1,0:T(8,128)(2,1)S(1)}, u32[]{:S(2)}, u32[]{:S(2)}) collective-permute-start(bf16[4,136,128]{2,1,0:T(8,128)(2,1)S(1)} %pad_maximum_fusion.1), channel_id=1, source_target_pairs={{0,24},{8,16},{16,8},{24,0},{32,56},{40,48},{48,40},{56,32},{64,88... | collective-permute-start | bytes 417800 | tf_op jit(solution)/shard_map/ppermute | solution.py:34
  29.2 7.0 %collective-permute-start.2 = (bf16[4,136,128]{2,1,0:T(8,128)(2,1)S(1)}, bf16[4,136,128]{2,1,0:T(8,128)(2,1)S(1)}, u32[]{:S(2)}, u32[]{:S(2)}) collective-permute-start(bf16[4,136,128]{2,1,0:T(8,128)(2,1)S(1)} %pad_maximum_fusion.2), channel_id=1, source_target_pairs={{0,56},{8,48},{16,40},{24,32},{32,24},{40,16},{48,8},{56,0},{64,12... | collective-permute-start | bytes 417800 | tf_op jit(solution)/shard_map/ppermute | solution.py:34
  37.0 4.2 %collective-permute-start.3 = (bf16[4,136,128]{2,1,0:T(8,128)(2,1)S(1)}, bf16[4,136,128]{2,1,0:T(8,128)(2,1)S(1)}, u32[]{:S(2)}, u32[]{:S(2)}) collective-permute-start(bf16[4,136,128]{2,1,0:T(8,128)(2,1)S(1)} %pad_maximum_fusion.3), channel_id=1, source_target_pairs={{0,64},{8,72},{16,80},{24,88},{32,96},{40,104},{48,112},{56,120},{... | collective-permute-start | bytes 417800 | tf_op jit(solution)/shard_map/ppermute | solution.py:34
  41.9 9.4 %collective-permute-start.4 = (bf16[4,136,128]{2,1,0:T(8,128)(2,1)S(1)}, bf16[4,136,128]{2,1,0:T(8,128)(2,1)S(1)}, u32[]{:S(2)}, u32[]{:S(2)}) collective-permute-start(bf16[4,136,128]{2,1,0:T(8,128)(2,1)S(1)} %pad_maximum_fusion.4), channel_id=1, source_target_pairs={{0,192},{8,200},{16,208},{24,216},{32,224},{40,232},{48,240},{56,2... | collective-permute-start | bytes 417800 | tf_op jit(solution)/shard_map/ppermute | solution.py:34
  56.6 1.6 %copy-start = (f32[2,512,4,128]{3,2,1,0:T(4,128)S(1)}, f32[2,512,4,128]{3,2,1,0:T(4,128)}, u32[]{:S(2)}) copy-start(f32[2,512,4,128]{3,2,1,0:T(4,128)} %copy.94) | copy-start | bytes 6291460
  56.6 1.6 %copy-start.4 = (f32[512]{0:T(512)S(1)}, f32[512]{0:T(512)}, u32[]{:S(2)}) copy-start(f32[512]{0:T(512)} %param.12) | copy-start | bytes 6148
Sparse Core Ops, SparseCore 0:
  70.2 78.2 reduce-scatter.1

commit v9 on v8

--- a/solution.py
+++ b/solution.py
@@ -84,25 +84,32 @@
     factor = jnp.exp(jnp.where(lower[None, None], spread, -jnp.inf))
     scores = jnp.einsum("bthd,bshd->bhts", q, k, preferred_element_type=jnp.float32)
     weighted = (scores * factor).astype(jnp.bfloat16)
-    inside = jnp.einsum("bhts,bshd->bthd", weighted, v, preferred_element_type=jnp.float32)
+    inside = jnp.einsum("bhts,bshd->bhtd", weighted, v, preferred_element_type=jnp.float32)
 
     carry_all = jnp.stack(
         [carries[b] + jnp.exp(offsets[b])[:, None, None] * incoming for b in range(blocks)]
     )
-    carried = jnp.exp(cum).transpose(0, 2, 1)[:, :, :, None] * jnp.einsum(
-        "bthd,bhde->bthe", q.astype(jnp.float32), carry_all, precision=hp
+    carried = jnp.exp(cum)[:, :, :, None] * jnp.einsum(
+        "bthd,bhde->bhte", q.astype(jnp.float32), carry_all, precision=hp
     )
-    attn = (inside + carried).reshape(local_rows, head_count, head_width)
+    attn = inside + carried
 
     meansq = jnp.mean(attn * attn, axis=-1, keepdims=True)
-    gate = jax.nn.sigmoid(gates.reshape(local_rows, head_count, head_width).astype(jnp.float32))
-    normed = attn * lax.rsqrt(meansq + 1e-06) * norm_gain.reshape(head_count, head_width) * gate
-    normed = normed.astype(jnp.bfloat16).reshape(local_rows, head_count * head_width)
+    gate = jax.nn.sigmoid(
+        gates.reshape(blocks, width_blk, head_count, head_width)
+        .transpose(0, 2, 1, 3)
+        .astype(jnp.float32)
+    )
+    normed = attn * lax.rsqrt(meansq + 1e-06) * norm_gain.reshape(head_count, 1, head_width) * gate
+    normed = normed.astype(jnp.bfloat16)
+    projected = jnp.einsum(
+        "bhte,hen->btn",
+        normed,
+        out_weight.reshape(head_count, head_width, out_weight.shape[1]),
+        preferred_element_type=jnp.float32,
+    ).reshape(local_rows, out_weight.shape[1])
     return lax.psum_scatter(
-        jnp.dot(normed, out_weight, preferred_element_type=jnp.float32).astype(jnp.bfloat16),
-        "tp",
-        scatter_dimension=0,
-        tiled=True,
+        projected.astype(jnp.bfloat16), "tp", scatter_dimension=0, tiled=True
     )
 
 

time: 156 us -> 162 us (1.038)
  other arithmetic: 5.01 us -> 12.2 us
  waiting for transfers between devices: 87.1 us -> 88.8 us
    convert_element_type x0 -> x1, other arithmetic: none -> 2.81 us  [on_device(): normed = normed.astype(jnp.bfloat16)]
    dot_general x3, matrix products: 21.2 us -> 19.1 us  [the longest x1 12 us: on_device(): jnp.einsum('bhte,hen->btn', normed, out_weight.reshape(head_count, head_w...]
    add x1 -> x0, local copies, waits for them, and re-layouts: 1.87 us -> none  [on_device(): attn = (inside + carried).reshape(local_rows, head_count, head_width)]
    div x0 -> x1, local copies, waits for them, and re-layouts: none -> 1.79 us  [on_device(): jax.nn.sigmoid(gates.reshape(blocks, width_blk, head_count, head_width).t...]
    div x0 -> x1, other arithmetic: none -> 1.77 us  [on_device(): jax.nn.sigmoid(gates.reshape(blocks, width_blk, head_count, head_width).t...]
  transfers between devices with their start and end apart: 6 -> 6, of which waited for: 5 -> 5; matrix products, arithmetic and copies ran while one was open for 5% -> 4% of each run, Pallas kernels for 0% -> 0%
where the time goes in v9:
time: 162 us
  waiting for transfers between devices  88.8 us (55%)
  matrix products  21.6 us (13%)
  starting transfers between devices  16.1 us (10%)
  between operations  13.7 us (8%)
  other arithmetic  12.2 us (8%)
  local copies, waits for them, and re-layouts  9.62 us (6%)
    reduce_scatter x1, waiting for transfers between devices, on_device(): lax.psum_scatter(projected.astype(jnp.bfloat16), 'tp', scatter_dimension=...  78.6 us
    ppermute x5, starting transfers between devices, exclusive_prefix(): lax.ppermute(pack(*block), axis, [(i, i ^ flip) for i in range(n)])  16.1 us
    dot_general x1, matrix products, on_device(): jnp.einsum('bhte,hen->btn', normed, out_weight.reshape(head_count, head_w...  12 us
    ppermute x5, waiting for transfers between devices, exclusive_prefix(): lax.ppermute(pack(*block), axis, [(i, i ^ flip) for i in range(n)])  10.1 us
    dot_general x1, matrix products, on_device(): jnp.einsum('bhts,bshd->bhtd', weighted, v, preferred_element_type=jnp.flo...  6.13 us
  transfers between devices with their start and end apart: 6, of which 5 were waited for; matrix products, arithmetic and copies ran while one was open for 4% of the time, Pallas kernels for 0%

profile of v9, /device:TPU:1, one launch (start us, length us, event | category | flops | bytes accessed | tf_op | source)
XLA Modules:
  0.0 162.0 jit_solution(16905958669092645734)
XLA Ops:
  6.5 0.8 reshape.500
  7.4 2.4 %reduce-window.6 = f32[2,4,4,128]{3,2,1,0:T(4,128)S(1)} reduce-window(f32[2,4,4,128]{3,2,1,0:T(4,128)S(1)} %copy.56, f32[]{:T(128)} %constant.14.clone.1), window={size=1x1x1x128 pad=0_0x0_0x0_0x127_0}, to_apply=%region_0.0 | reduce-window | flops 520192 | bytes 32772 | tf_op jit(solution)/shard_map/reduce-window
  9.8 0.2 slice_reduce_fusion
  10.0 0.4 reduce-window.9
  11.0 0.1 copy.59
  11.1 0.1 copy.38
  11.2 0.1 copy.37
  11.4 1.3 reshape.503
  12.8 0.3 reshape.499
  13.1 1.5 copy.34
  14.5 2.5 %fusion.13 = f32[2,4,128,128]{3,2,1,0:T(8,128)S(1)} fusion(bf16[2,512,4,128]{1,3,2,0:T(8,128)(2,1)} %copy.34, f32[2,512,4]{1,2,0:T(4,128)S(1)} %get-tuple-element.37, bf16[2,512,4,128]{3,2,1,0:T(4,128)(2,1)S(1)} %reshape.503), kind=kOutput, calls=%fused_computation.18 | convolution fusion | flops 806354944 | bytes 2637824 | tf_op jit(solution)/shard_map/bshd,bshe->bhde/dot_general | solution.py:62
  17.1 0.1 fusion.35
  17.4 2.5 %collective-permute-start = (bf16[4,136,128]{2,1,0:T(8,128)(2,1)S(1)}, bf16[4,136,128]{2,1,0:T(8,128)(2,1)S(1)}, u32[]{:S(2)}, u32[]{:S(2)}) collective-permute-start(bf16[4,136,128]{2,1,0:T(8,128)(2,1)S(1)} %pad_maximum_fusion), channel_id=1, source_target_pairs={{0,8},{8,0},{16,24},{24,16},{32,40},{40,32},{48,56},{56,48},{64,72... | collective-permute-start | bytes 417800 | tf_op jit(solution)/shard_map/ppermute | solution.py:34
  20.0 2.4 %collective-permute-done = bf16[4,136,128]{2,1,0:T(8,128)(2,1)S(1)} collective-permute-done((bf16[4,136,128]{2,1,0:T(8,128)(2,1)S(1)}, bf16[4,136,128]{2,1,0:T(8,128)(2,1)S(1)}, u32[]{:S(2)}, u32[]{:S(2)}) %collective-permute-start) | collective-permute-done | bytes 139296 | tf_op jit(solution)/shard_map/ppermute | solution.py:34
  22.4 0.1 exponential_reduce_fusion
  22.5 0.1 copy.39
  22.6 0.1 copy.40
  22.8 0.2 fusion.40
  23.1 4.9 %collective-permute-start.1 = (bf16[4,136,128]{2,1,0:T(8,128)(2,1)S(1)}, bf16[4,136,128]{2,1,0:T(8,128)(2,1)S(1)}, u32[]{:S(2)}, u32[]{:S(2)}) collective-permute-start(bf16[4,136,128]{2,1,0:T(8,128)(2,1)S(1)} %pad_maximum_fusion.1), channel_id=1, source_target_pairs={{0,24},{8,16},{16,8},{24,0},{32,56},{40,48},{48,40},{56,32},{64,88... | collective-permute-start | bytes 417800 | tf_op jit(solution)/shard_map/ppermute | solution.py:34
  28.0 2.5 %collective-permute-done.1 = bf16[4,136,128]{2,1,0:T(8,128)(2,1)S(1)} collective-permute-done((bf16[4,136,128]{2,1,0:T(8,128)(2,1)S(1)}, bf16[4,136,128]{2,1,0:T(8,128)(2,1)S(1)}, u32[]{:S(2)}, u32[]{:S(2)}) %collective-permute-start.1) | collective-permute-done | bytes 139296 | tf_op jit(solution)/shard_map/ppermute | solution.py:34
  30.6 0.1 exponential_reduce_fusion.6
  30.7 0.1 copy.42
  30.8 0.1 copy.43
  31.0 0.1 fusion.36
  31.2 4.6 %collective-permute-start.2 = (bf16[4,136,128]{2,1,0:T(8,128)(2,1)S(1)}, bf16[4,136,128]{2,1,0:T(8,128)(2,1)S(1)}, u32[]{:S(2)}, u32[]{:S(2)}) collective-permute-start(bf16[4,136,128]{2,1,0:T(8,128)(2,1)S(1)} %pad_maximum_fusion.2), channel_id=1, source_target_pairs={{0,56},{8,48},{16,40},{24,32},{32,24},{40,16},{48,8},{56,0},{64,12... | collective-permute-start | bytes 417800 | tf_op jit(solution)/shard_map/ppermute | solution.py:34
  35.8 2.4 %collective-permute-done.2 = bf16[4,136,128]{2,1,0:T(8,128)(2,1)S(1)} collective-permute-done((bf16[4,136,128]{2,1,0:T(8,128)(2,1)S(1)}, bf16[4,136,128]{2,1,0:T(8,128)(2,1)S(1)}, u32[]{:S(2)}, u32[]{:S(2)}) %collective-permute-start.2) | collective-permute-done | bytes 139296 | tf_op jit(solution)/shard_map/ppermute | solution.py:34
  38.3 0.1 exponential_reduce_fusion.4
  38.4 0.1 copy.44
  38.6 0.1 copy.45
  38.7 0.2 fusion.37
  39.0 1.4 collective-permute-start.3
  40.4 2.8 %collective-permute-done.3 = bf16[4,136,128]{2,1,0:T(8,128)(2,1)S(1)} collective-permute-done((bf16[4,136,128]{2,1,0:T(8,128)(2,1)S(1)}, bf16[4,136,128]{2,1,0:T(8,128)(2,1)S(1)}, u32[]{:S(2)}, u32[]{:S(2)}) %collective-permute-start.3) | collective-permute-done | bytes 139296 | tf_op jit(solution)/shard_map/ppermute | solution.py:34
  43.2 0.1 fusion.29
  43.4 0.1 copy.46
  43.5 0.1 copy.47
  43.7 0.1 select_convert_fusion
  43.9 0.7 pad_maximum_fusion.4
  44.5 2.7 %collective-permute-start.4 = (bf16[4,136,128]{2,1,0:T(8,128)(2,1)}, bf16[4,136,128]{2,1,0:T(8,128)(2,1)}, u32[]{:S(2)}, u32[]{:S(2)}) collective-permute-start(bf16[4,136,128]{2,1,0:T(8,128)(2,1)} %pad_maximum_fusion.4), channel_id=1, source_target_pairs={{0,192},{8,200},{16,208},{24,216},{32,224},{40,232},{48,240},{56,2... | collective-permute-start | bytes 417800 | tf_op jit(solution)/shard_map/ppermute | solution.py:34
  47.3 1.8 %add_divide_fusion = f32[1024,512]{1,0:T(8,128)S(1)} fusion(bf16[1024,512]{1,0:T(8,128)(2,1)} %param.10), kind=kLoop, calls=%fused_computation.17 | loop fusion | flops 2097152 | bytes 3145728 | tf_op jit(solution)/shard_map/div | solution.py:98
  49.1 1.3 reshape.498
  50.4 1.8 %reshape.508 = f32[2,512,4,128]{3,2,1,0:T(4,128)} reshape(f32[1024,512]{1,0:T(8,128)S(1)} %add_divide_fusion) | data formatting | bytes 4194304 | tf_op jit(solution)/shard_map/div | solution.py:98
  52.2 0.8 iota_compare_fusion
  53.0 1.5 add_bitcast_fusion
  54.5 1.0 fusion.19
  55.5 6.1 %fusion.9 = (f32[2,4,512]{2,1,0:T(4,128)S(1)}, f32[2,4,512,128]{3,2,1,0:T(8,128)}) fusion(f32[2,4,128,512]{2,3,1,0:T(8,128)S(1)} %fusion.19, f32[2,4,512]{2,1,0:T(4,128)S(1)} %get-tuple-element.38, bf16[2,512,4,128]{3,2,1,0:T(4,128)(2,1)} %copy-done.5, f32[2,4,512]{2,1,0:T(4,128)S(1)} %reduce_window_sum.27, pred[512,512]{1,0:T(8,128)(4,1)S(1)} %copy-done.6, ...), kind=kOutput, calls=%fused_computation.12 | convolution fusion | flops 1084223488 | bytes 7651328 | tf_op jit(solution)/shard_map/bhts,bshd->bhtd/dot_general | solution.py:87
  61.7 2.8 %fusion.7 = bf16[2,512,128,4]{2,1,3,0:T(8,128)(2,1)S(1)} fusion(f32[2,4,128,512]{2,3,1,0:T(8,128)S(1)} %fusion.19, f32[2,4,512,128]{3,2,1,0:T(8,128)} %get-tuple-element.48, f32[2,512,4,128]{3,2,1,0:T(4,128)} %reshape.508, f32[128,4]{0,1:T(4,128)S(1)} %bitcast.121, f32[2,512,4]{1,2,0:T(4,128)S(1)} %rsqrt_bitcast_fusion, f32[2,512,4]{1,2,0:T(4,128)S(1)} %get-tuple-element.36), kind=kLoop, calls=%fused_computation.9 | loop fusion | flops 3145728 | bytes 7374848 | tf_op jit(solution)/shard_map/convert_element_type | solution.py:104
  64.6 12.0 %bitcast_convert_fusion = bf16[1024,6144]{1,0:T(8,128)(2,1)} fusion(bf16[1024,128,4]{1,0,2:T(8,128)(2,1)S(1)} %bitcast.116, bf16[4,128,6144]{2,1,0:T(8,128)(2,1)} %bitcast.122), kind=kOutput, calls=%fused_computation | convolution fusion | flops 6448742400 | bytes 19922944 | tf_op jit(solution)/shard_map/bhte,hen->btn/dot_general | solution.py:105
  76.5 78.6 %reduce-scatter.2.cloned.1.call-done = bf16[128,6144]{1,0:T(8,128)(2,1)} async-done(((bf16[1024,6144]{1,0:T(8,128)(2,1)}), bf16[128,6144]{1,0:T(8,128)(2,1)}) %reduce-scatter.2.cloned.1.call-update) | async-done | bytes 1572880 | tf_op jit(solution)/shard_map/reduce_scatter | solution.py:111
  (64 shorter events, 1.9 us)
Async XLA Ops:
  6.5 6.2 %copy-start.4 = (bf16[1024,512]{1,0:T(8,128)(2,1)S(1)}, bf16[1024,512]{1,0:T(8,128)(2,1)}, u32[]{:S(2)}) copy-start(bf16[1024,512]{1,0:T(8,128)(2,1)} %param.8) | copy-start | bytes 3145732
  6.5 148.6 %reduce-scatter.2.cloned.1.call-start = ((), (), s32[]{:S(2)}) async-start(), calls=%async_computation.1 | async-start | bytes 14155776 | tf_op jit(solution)/shard_map/reduce_scatter | solution.py:111
  12.8 1.8 %copy-start.5 = (bf16[2,512,4,128]{3,2,1,0:T(4,128)(2,1)}, bf16[2,512,4,128]{3,2,1,0:T(4,128)(2,1)S(1)}, u32[]{:S(2)}) copy-start(bf16[2,512,4,128]{3,2,1,0:T(4,128)(2,1)S(1)} %reshape.503) | copy-start | bytes 3145732
  17.1 10.9 %copy-start = (f32[2,4,128,128]{3,2,1,0:T(8,128)}, f32[2,4,128,128]{3,2,1,0:T(8,128)S(1)}, u32[]{:S(2)}) copy-start(f32[2,4,128,128]{3,2,1,0:T(8,128)S(1)} %fusion.13) | copy-start | bytes 1572868
  17.4 5.0 %collective-permute-start = (bf16[4,136,128]{2,1,0:T(8,128)(2,1)S(1)}, bf16[4,136,128]{2,1,0:T(8,128)(2,1)S(1)}, u32[]{:S(2)}, u32[]{:S(2)}) collective-permute-start(bf16[4,136,128]{2,1,0:T(8,128)(2,1)S(1)} %pad_maximum_fusion), channel_id=1, source_target_pairs={{0,8},{8,0},{16,24},{24,16},{32,40},{40,32},{48,56},{56,48},{64,72... | collective-permute-start | bytes 417800 | tf_op jit(solution)/shard_map/ppermute | solution.py:34
  22.4 5.6 %copy-start.2 = (f32[4,136,128]{2,1,0:T(8,128)}, f32[4,136,128]{2,1,0:T(8,128)S(1)}, u32[]{:S(2)}) copy-start(f32[4,136,128]{2,1,0:T(8,128)S(1)} %convert_element_type.225) | copy-start | bytes 835588
  23.1 7.5 %collective-permute-start.1 = (bf16[4,136,128]{2,1,0:T(8,128)(2,1)S(1)}, bf16[4,136,128]{2,1,0:T(8,128)(2,1)S(1)}, u32[]{:S(2)}, u32[]{:S(2)}) collective-permute-start(bf16[4,136,128]{2,1,0:T(8,128)(2,1)S(1)} %pad_maximum_fusion.1), channel_id=1, source_target_pairs={{0,24},{8,16},{16,8},{24,0},{32,56},{40,48},{48,40},{56,32},{64,88... | collective-permute-start | bytes 417800 | tf_op jit(solution)/shard_map/ppermute | solution.py:34
  31.2 7.0 %collective-permute-start.2 = (bf16[4,136,128]{2,1,0:T(8,128)(2,1)S(1)}, bf16[4,136,128]{2,1,0:T(8,128)(2,1)S(1)}, u32[]{:S(2)}, u32[]{:S(2)}) collective-permute-start(bf16[4,136,128]{2,1,0:T(8,128)(2,1)S(1)} %pad_maximum_fusion.2), channel_id=1, source_target_pairs={{0,56},{8,48},{16,40},{24,32},{32,24},{40,16},{48,8},{56,0},{64,12... | collective-permute-start | bytes 417800 | tf_op jit(solution)/shard_map/ppermute | solution.py:34
  38.3 2.1 %copy-start.3 = (f32[4,136,128]{2,1,0:T(8,128)}, f32[4,136,128]{2,1,0:T(8,128)S(1)}, u32[]{:S(2)}) copy-start(f32[4,136,128]{2,1,0:T(8,128)S(1)} %convert_element_type.235) | copy-start | bytes 835588
  39.0 4.2 %collective-permute-start.3 = (bf16[4,136,128]{2,1,0:T(8,128)(2,1)S(1)}, bf16[4,136,128]{2,1,0:T(8,128)(2,1)S(1)}, u32[]{:S(2)}, u32[]{:S(2)}) collective-permute-start(bf16[4,136,128]{2,1,0:T(8,128)(2,1)S(1)} %pad_maximum_fusion.3), channel_id=1, source_target_pairs={{0,64},{8,72},{16,80},{24,88},{32,96},{40,104},{48,112},{56,120},{... | collective-permute-start | bytes 417800 | tf_op jit(solution)/shard_map/ppermute | solution.py:34
  43.2 5.8 %copy-start.1 = (f32[4,136,128]{2,1,0:T(8,128)}, f32[4,136,128]{2,1,0:T(8,128)S(1)}, u32[]{:S(2)}) copy-start(f32[4,136,128]{2,1,0:T(8,128)S(1)} %convert_element_type.240) | copy-start | bytes 835588
  44.5 8.5 %collective-permute-start.4 = (bf16[4,136,128]{2,1,0:T(8,128)(2,1)}, bf16[4,136,128]{2,1,0:T(8,128)(2,1)}, u32[]{:S(2)}, u32[]{:S(2)}) collective-permute-start(bf16[4,136,128]{2,1,0:T(8,128)(2,1)} %pad_maximum_fusion.4), channel_id=1, source_target_pairs={{0,192},{8,200},{16,208},{24,216},{32,224},{40,232},{48,240},{56,2... | collective-permute-start | bytes 417800 | tf_op jit(solution)/shard_map/ppermute | solution.py:34
  54.5 1.0 copy-start.6
  55.5 6.2 %copy-start.7 = (f32[512]{0:T(512)S(1)}, f32[512]{0:T(512)}, u32[]{:S(2)}) copy-start(f32[512]{0:T(512)} %param.12) | copy-start | bytes 6148
Sparse Core Ops, SparseCore 0:
  76.7 78.4 reduce-scatter.1

commit v10 on v8

--- a/solution.py
+++ b/solution.py
@@ -54,7 +54,8 @@
     k = keys.reshape(blocks, width_blk, head_count, head_width)
     v = values.reshape(blocks, width_blk, head_count, head_width)
     decay = log_decay.reshape(head_count, blocks, width_blk).transpose(1, 0, 2)
-    cum = jnp.cumsum(decay, axis=2)
+    upto = (jnp.arange(width_blk)[:, None] <= jnp.arange(width_blk)[None, :]).astype(jnp.float32)
+    cum = jnp.einsum("bhu,ut->bht", decay, upto, precision=hp)
     last = cum[:, :, -1]
 
     tail = jnp.exp(last[:, :, None] - cum)

time: 156 us -> 153 us (0.981)
  other arithmetic: 5.01 us -> 2.36 us
    another operation x3 -> x0, other arithmetic: 2.88 us -> none
where the time goes in v10:
time: 153 us; the launch traced here: 152 us
  waiting for transfers between devices  87.2 us (57%)
  matrix products  22.7 us (15%)
  starting transfers between devices  16.4 us (11%)
  between operations  13.6 us (9%)
  local copies, waits for them, and re-layouts  9.96 us (7%)
  other arithmetic  2.36 us (2%)
    reduce_scatter x1, waiting for transfers between devices, on_device(): lax.psum_scatter(jnp.dot(normed, out_weight, preferred_element_type=jnp.f...  78.4 us
    ppermute x5, starting transfers between devices, exclusive_prefix(): lax.ppermute(pack(*block), axis, [(i, i ^ flip) for i in range(n)])  16.4 us
    dot_general x1, matrix products, on_device(): jnp.dot(normed, out_weight, preferred_element_type=jnp.float32)  11.9 us
    ppermute x5, waiting for transfers between devices, exclusive_prefix(): lax.ppermute(pack(*block), axis, [(i, i ^ flip) for i in range(n)])  8.79 us
    dot_general x1, matrix products, on_device(): jnp.einsum('bhts,bshd->bthd', weighted, v, preferred_element_type=jnp.flo...  6.42 us
  transfers between devices with their start and end apart: 6, of which 5 were waited for; matrix products, arithmetic and copies ran while one was open for 5% of the time, Pallas kernels for 0%

profile of v10, /device:TPU:1, one launch (start us, length us, event | category | flops | bytes accessed | tf_op | source)
XLA Modules:
  0.0 152.4 jit_solution(16560376532859627259)
XLA Ops:
  6.5 0.7 copy-done
  7.3 0.3 fusion.19
  7.5 0.2 slice_reduce_fusion
  7.7 0.2 exponential_reduce_fusion.12
  8.1 0.1 copy.70
  8.2 0.1 copy.69
  8.4 1.3 reshape.472
  9.8 0.3 reshape.470
  10.1 0.7 copy.67
  10.8 1.3 fusion.11
  12.1 0.1 fusion.39
  12.4 2.5 %collective-permute-start = (bf16[4,136,128]{2,1,0:T(8,128)(2,1)S(1)}, bf16[4,136,128]{2,1,0:T(8,128)(2,1)S(1)}, u32[]{:S(2)}, u32[]{:S(2)}) collective-permute-start(bf16[4,136,128]{2,1,0:T(8,128)(2,1)S(1)} %pad_maximum_fusion), channel_id=1, source_target_pairs={{0,8},{8,0},{16,24},{24,16},{32,40},{40,32},{48,56},{56,48},{64,72... | collective-permute-start | bytes 417800 | tf_op jit(solution)/shard_map/ppermute | solution.py:34
  14.9 2.4 %collective-permute-done = bf16[4,136,128]{2,1,0:T(8,128)(2,1)S(1)} collective-permute-done((bf16[4,136,128]{2,1,0:T(8,128)(2,1)S(1)}, bf16[4,136,128]{2,1,0:T(8,128)(2,1)S(1)}, u32[]{:S(2)}, u32[]{:S(2)}) %collective-permute-start) | collective-permute-done | bytes 139296 | tf_op jit(solution)/shard_map/ppermute | solution.py:34
  17.4 0.1 exponential_reduce_fusion
  17.5 0.1 copy.71
  17.7 0.1 copy.72
  17.8 0.1 maximum_maximum_fusion.1
  17.9 0.2 fusion.43
  18.1 4.9 %collective-permute-start.1 = (bf16[4,136,128]{2,1,0:T(8,128)(2,1)S(1)}, bf16[4,136,128]{2,1,0:T(8,128)(2,1)S(1)}, u32[]{:S(2)}, u32[]{:S(2)}) collective-permute-start(bf16[4,136,128]{2,1,0:T(8,128)(2,1)S(1)} %pad_maximum_fusion.1), channel_id=1, source_target_pairs={{0,24},{8,16},{16,8},{24,0},{32,56},{40,48},{48,40},{56,32},{64,88... | collective-permute-start | bytes 417800 | tf_op jit(solution)/shard_map/ppermute | solution.py:34
  23.0 2.5 %collective-permute-done.1 = bf16[4,136,128]{2,1,0:T(8,128)(2,1)S(1)} collective-permute-done((bf16[4,136,128]{2,1,0:T(8,128)(2,1)S(1)}, bf16[4,136,128]{2,1,0:T(8,128)(2,1)S(1)}, u32[]{:S(2)}, u32[]{:S(2)}) %collective-permute-start.1) | collective-permute-done | bytes 139296 | tf_op jit(solution)/shard_map/ppermute | solution.py:34
  25.6 0.1 exponential_reduce_fusion.6
  25.7 0.1 copy.74
  25.8 0.1 copy.75
  25.9 0.1 maximum_maximum_fusion.2
  26.0 0.1 fusion.40
  26.3 4.6 %collective-permute-start.2 = (bf16[4,136,128]{2,1,0:T(8,128)(2,1)S(1)}, bf16[4,136,128]{2,1,0:T(8,128)(2,1)S(1)}, u32[]{:S(2)}, u32[]{:S(2)}) collective-permute-start(bf16[4,136,128]{2,1,0:T(8,128)(2,1)S(1)} %pad_maximum_fusion.2), channel_id=1, source_target_pairs={{0,56},{8,48},{16,40},{24,32},{32,24},{40,16},{48,8},{56,0},{64,12... | collective-permute-start | bytes 417800 | tf_op jit(solution)/shard_map/ppermute | solution.py:34
  30.8 2.4 %collective-permute-done.2 = bf16[4,136,128]{2,1,0:T(8,128)(2,1)S(1)} collective-permute-done((bf16[4,136,128]{2,1,0:T(8,128)(2,1)S(1)}, bf16[4,136,128]{2,1,0:T(8,128)(2,1)S(1)}, u32[]{:S(2)}, u32[]{:S(2)}) %collective-permute-start.2) | collective-permute-done | bytes 139296 | tf_op jit(solution)/shard_map/ppermute | solution.py:34
  33.3 0.1 exponential_reduce_fusion.4
  33.4 0.1 copy.76
  33.6 0.1 copy.77
  33.7 0.2 fusion.41
  34.0 1.4 collective-permute-start.3
  35.4 1.3 reshape.469
  36.9 1.4 collective-permute-done.3
  38.2 0.1 fusion.32
  38.4 0.1 copy.78
  38.5 0.1 copy.79
  38.7 0.1 select_convert_fusion
  38.9 3.0 %collective-permute-start.4 = (bf16[4,136,128]{2,1,0:T(8,128)(2,1)S(1)}, bf16[4,136,128]{2,1,0:T(8,128)(2,1)S(1)}, u32[]{:S(2)}, u32[]{:S(2)}) collective-permute-start(bf16[4,136,128]{2,1,0:T(8,128)(2,1)S(1)} %pad_maximum_fusion.4), channel_id=1, source_target_pairs={{0,192},{8,200},{16,208},{24,216},{32,224},{40,232},{48,240},{56,2... | collective-permute-start | bytes 417800 | tf_op jit(solution)/shard_map/ppermute | solution.py:34
  41.9 6.4 %fusion = f32[2,4,512,128]{2,3,1,0:T(8,128)} fusion(f32[2,4,512]{2,1,0:T(4,128)S(1)} %bitcast.101, pred[512,512]{1,0:T(8,128)(4,1)S(1)} %iota_compare_fusion.1, bf16[2,512,4,128]{1,3,2,0:T(8,128)(2,1)} %copy-done.4, bf16[2,512,4,128]{3,2,1,0:T(4,128)(2,1)} %copy-done.3, bf16[2,512,4,128]{3,2,1,0:T(4,128)(2,1)S(1)} %reshape.469), kind=kOutput, calls=%fused_computation.2 | convolution fusion | flops 1082130432 | bytes 5521408 | tf_op jit(solution)/shard_map/bhts,bshd->bthd/dot_general | solution.py:88
  48.3 0.3 add_bitcast_fusion
  48.6 2.9 %multiply_reduce_fusion = (f32[2,512,4]{1,2,0:T(4,128)S(1)}, f32[2,512,4,128]{1,3,2,0:T(8,128)S(1)}) fusion(bf16[2,512,4,128]{3,2,1,0:T(4,128)(2,1)S(1)} %reshape.469, f32[1,4,128,128]{3,2,1,0:T(8,128)S(1)} %get-tuple-element.24, f32[1,4,128,128]{3,2,1,0:T(8,128)S(1)} %bitcast.97, f32[2,512,4]{1,2,0:T(4,128)S(1)} %get-tuple-element.42, ...), kind=kOutput, calls=%fused_computation.14 | convolution fusion | flops 807530496 | bytes 5799936 | tf_op jit(solution)/shard_map/bthd,bhde->bthe/dot_general | solution.py:93
  51.5 0.2 copy.83
  51.7 1.9 %copy.82 = f32[2,512,4,128]{3,2,1,0:T(4,128)} copy(f32[2,512,4,128]{1,3,2,0:T(8,128)S(1)} %get-tuple-element.48) | data formatting | bytes 4194304 | tf_op jit(solution)/shard_map/add | solution.py:96
  53.6 1.2 mul.237
  54.8 0.4 copy-done.1
  55.2 11.9 %convolution_convert_fusion = bf16[1024,6144]{1,0:T(8,128)(2,1)} fusion(bf16[512,6144]{1,0:T(8,128)(2,1)} %param.13, f32[128,8,4,128]{3,2,1,0:T(4,128)S(1)} %bitcast.95, f32[128,8,4,128]{3,2,1,0:T(4,128)S(1)} %bitcast.96, bf16[1024,512]{1,0:T(8,128)(2,1)} %param.10, f32[512]{0:T(512)S(1)} %copy-done.5), kind=kOutput, calls=%fused_computation | convolution fusion | flops 6452936704 | bytes 24119296 | tf_op jit(solution)/shard_map/dot_general | solution.py:103
  67.1 78.4 %reduce-scatter.2.cloned.1.call-done = bf16[128,6144]{1,0:T(8,128)(2,1)} async-done(((bf16[1024,6144]{1,0:T(8,128)(2,1)}), bf16[128,6144]{1,0:T(8,128)(2,1)}) %reduce-scatter.2.cloned.1.call-update) | async-done | bytes 1572880 | tf_op jit(solution)/shard_map/reduce_scatter | solution.py:102
  (47 shorter events, 1.2 us)
Async XLA Ops:
  6.5 0.7 copy-start
  6.5 3.2 %copy-start.2 = (bf16[1024,512]{1,0:T(8,128)(2,1)S(1)}, bf16[1024,512]{1,0:T(8,128)(2,1)}, u32[]{:S(2)}) copy-start(bf16[1024,512]{1,0:T(8,128)(2,1)} %param.8) | copy-start | bytes 3145732
  6.5 139.0 %reduce-scatter.2.cloned.1.call-start = ((), (), s32[]{:S(2)}) async-start(), calls=%async_computation.1 | async-start | bytes 14155776 | tf_op jit(solution)/shard_map/reduce_scatter | solution.py:102
  9.8 24.1 %copy-start.3 = (bf16[2,512,4,128]{3,2,1,0:T(4,128)(2,1)}, bf16[2,512,4,128]{3,2,1,0:T(4,128)(2,1)S(1)}, u32[]{:S(2)}) copy-start(bf16[2,512,4,128]{3,2,1,0:T(4,128)(2,1)S(1)} %reshape.472) | copy-start | bytes 3145732
  10.8 4.2 %copy-start.4 = (bf16[2,512,4,128]{1,3,2,0:T(8,128)(2,1)}, bf16[2,512,4,128]{1,3,2,0:T(8,128)(2,1)S(1)}, u32[]{:S(2)}) copy-start(bf16[2,512,4,128]{1,3,2,0:T(8,128)(2,1)S(1)} %copy.67) | copy-start | bytes 3145732
  12.4 5.0 %collective-permute-start = (bf16[4,136,128]{2,1,0:T(8,128)(2,1)S(1)}, bf16[4,136,128]{2,1,0:T(8,128)(2,1)S(1)}, u32[]{:S(2)}, u32[]{:S(2)}) collective-permute-start(bf16[4,136,128]{2,1,0:T(8,128)(2,1)S(1)} %pad_maximum_fusion), channel_id=1, source_target_pairs={{0,8},{8,0},{16,24},{24,16},{32,40},{40,32},{48,56},{56,48},{64,72... | collective-permute-start | bytes 417800 | tf_op jit(solution)/shard_map/ppermute | solution.py:34
  18.1 7.5 %collective-permute-start.1 = (bf16[4,136,128]{2,1,0:T(8,128)(2,1)S(1)}, bf16[4,136,128]{2,1,0:T(8,128)(2,1)S(1)}, u32[]{:S(2)}, u32[]{:S(2)}) collective-permute-start(bf16[4,136,128]{2,1,0:T(8,128)(2,1)S(1)} %pad_maximum_fusion.1), channel_id=1, source_target_pairs={{0,24},{8,16},{16,8},{24,0},{32,56},{40,48},{48,40},{56,32},{64,88... | collective-permute-start | bytes 417800 | tf_op jit(solution)/shard_map/ppermute | solution.py:34
  26.3 7.0 %collective-permute-start.2 = (bf16[4,136,128]{2,1,0:T(8,128)(2,1)S(1)}, bf16[4,136,128]{2,1,0:T(8,128)(2,1)S(1)}, u32[]{:S(2)}, u32[]{:S(2)}) collective-permute-start(bf16[4,136,128]{2,1,0:T(8,128)(2,1)S(1)} %pad_maximum_fusion.2), channel_id=1, source_target_pairs={{0,56},{8,48},{16,40},{24,32},{32,24},{40,16},{48,8},{56,0},{64,12... | collective-permute-start | bytes 417800 | tf_op jit(solution)/shard_map/ppermute | solution.py:34
  34.0 4.2 %collective-permute-start.3 = (bf16[4,136,128]{2,1,0:T(8,128)(2,1)S(1)}, bf16[4,136,128]{2,1,0:T(8,128)(2,1)S(1)}, u32[]{:S(2)}, u32[]{:S(2)}) collective-permute-start(bf16[4,136,128]{2,1,0:T(8,128)(2,1)S(1)} %pad_maximum_fusion.3), channel_id=1, source_target_pairs={{0,64},{8,72},{16,80},{24,88},{32,96},{40,104},{48,112},{56,120},{... | collective-permute-start | bytes 417800 | tf_op jit(solution)/shard_map/ppermute | solution.py:34
  38.9 9.4 %collective-permute-start.4 = (bf16[4,136,128]{2,1,0:T(8,128)(2,1)S(1)}, bf16[4,136,128]{2,1,0:T(8,128)(2,1)S(1)}, u32[]{:S(2)}, u32[]{:S(2)}) collective-permute-start(bf16[4,136,128]{2,1,0:T(8,128)(2,1)S(1)} %pad_maximum_fusion.4), channel_id=1, source_target_pairs={{0,192},{8,200},{16,208},{24,216},{32,224},{40,232},{48,240},{56,2... | collective-permute-start | bytes 417800 | tf_op jit(solution)/shard_map/ppermute | solution.py:34
  53.6 1.6 %copy-start.1 = (f32[2,512,4,128]{3,2,1,0:T(4,128)S(1)}, f32[2,512,4,128]{3,2,1,0:T(4,128)}, u32[]{:S(2)}) copy-start(f32[2,512,4,128]{3,2,1,0:T(4,128)} %copy.82) | copy-start | bytes 6291460
  53.6 1.6 %copy-start.5 = (f32[512]{0:T(512)S(1)}, f32[512]{0:T(512)}, u32[]{:S(2)}) copy-start(f32[512]{0:T(512)} %param.12) | copy-start | bytes 6148
Sparse Core Ops, SparseCore 0:
  67.2 78.2 reduce-scatter.1

commit v11 on v10

--- a/solution.py
+++ b/solution.py
@@ -42,6 +42,17 @@
     return prefix[0]
 
 
+def split_dot(spec, a, b, lhs_wide):
+    wide, narrow = (a, b) if lhs_wide else (b, a)
+    hi = wide.astype(jnp.bfloat16)
+    lo = (wide - hi.astype(jnp.float32)).astype(jnp.bfloat16)
+    out = 0.0
+    for part in (hi, lo):
+        x, y = (part, narrow) if lhs_wide else (narrow, part)
+        out = out + jnp.einsum(spec, x, y, preferred_element_type=jnp.float32)
+    return out
+
+
 def on_device(queries, keys, values, gates, log_decay, norm_gain, out_weight):
     local_rows = queries.shape[0]
     head_count = log_decay.shape[0]
@@ -60,9 +71,7 @@
 
     tail = jnp.exp(last[:, :, None] - cum)
     key_decayed = k.astype(jnp.float32) * tail.transpose(0, 2, 1)[:, :, :, None]
-    block_state = jnp.einsum(
-        "bshd,bshe->bhde", key_decayed, v.astype(jnp.float32), precision=hp
-    )
+    block_state = split_dot("bshd,bshe->bhde", key_decayed, v, lhs_wide=True)
 
     carries = []
     run = jnp.zeros((head_count, head_width, head_width), jnp.float32)
@@ -90,9 +99,7 @@
     carry_all = jnp.stack(
         [carries[b] + jnp.exp(offsets[b])[:, None, None] * incoming for b in range(blocks)]
     )
-    carried = jnp.exp(cum).transpose(0, 2, 1)[:, :, :, None] * jnp.einsum(
-        "bthd,bhde->bthe", q.astype(jnp.float32), carry_all, precision=hp
-    )
+    carried = jnp.exp(cum).transpose(0, 2, 1)[:, :, :, None] * split_dot("bthd,bhde->bthe", q, carry_all, lhs_wide=False)
     attn = (inside + carried).reshape(local_rows, head_count, head_width)
 
     meansq = jnp.mean(attn * attn, axis=-1, keepdims=True)

time: 153 us -> 161 us (1.052)
  waiting for transfers between devices: 87.2 us -> 92.9 us
  matrix products: 22.7 us -> 24.6 us
    reduce_scatter x1, waiting for transfers between devices: 78.4 us -> 81.6 us  [on_device(): lax.psum_scatter(jnp.dot(normed, out_weight, preferred_element_type=jnp.f...]
    ppermute x5, waiting for transfers between devices: 8.79 us -> 11.3 us  [exclusive_prefix(): lax.ppermute(pack(*block), axis, [(i, i ^ flip) for i in range(n)])]
    dot_general x2 -> x4, matrix products: 4.17 us -> 4.55 us  [split_dot(): out = out + jnp.einsum(spec, x, y, preferred_element_type=jnp.float32)]
  transfers between devices with their start and end apart: 6 -> 6, of which waited for: 5 -> 6; matrix products, arithmetic and copies ran while one was open for 5% -> 1% of each run, Pallas kernels for 0% -> 0%
where the time goes in v11:
time: 161 us
  waiting for transfers between devices  92.9 us (58%)
  matrix products  24.6 us (15%)
  starting transfers between devices  16.4 us (10%)
  between operations  13.7 us (9%)
  local copies, waits for them, and re-layouts  10.7 us (7%)
  other arithmetic  2.36 us (1%)
    reduce_scatter x1, waiting for transfers between devices, on_device(): lax.psum_scatter(jnp.dot(normed, out_weight, preferred_element_type=jnp.f...  81.6 us
    ppermute x5, starting transfers between devices, exclusive_prefix(): lax.ppermute(pack(*block), axis, [(i, i ^ flip) for i in range(n)])  16.4 us
    dot_general x1, matrix products, on_device(): jnp.dot(normed, out_weight, preferred_element_type=jnp.float32)  12.5 us
    ppermute x5, waiting for transfers between devices, exclusive_prefix(): lax.ppermute(pack(*block), axis, [(i, i ^ flip) for i in range(n)])  11.3 us
    dot_general x1, matrix products, on_device(): jnp.einsum('bhts,bshd->bthd', weighted, v, preferred_element_type=jnp.flo...  7.29 us
    dot_general x4, matrix products, split_dot(): out = out + jnp.einsum(spec, x, y, preferred_element_type=jnp.float32)  4.55 us
  transfers between devices with their start and end apart: 6, of which 6 were waited for; matrix products, arithmetic and copies ran while one was open for 1% of the time, Pallas kernels for 0%

profile of v11, /device:TPU:1, one launch (start us, length us, event | category | flops | bytes accessed | tf_op | source)
XLA Modules:
  0.0 160.6 jit_solution(3307431155863539818)
XLA Ops:
  6.5 0.7 copy-done
  7.3 0.3 fusion.20
  7.5 0.2 slice_reduce_fusion
  7.7 0.2 exponential_reduce_fusion.12
  8.1 0.1 copy.80
  8.2 0.1 copy.79
  8.4 1.3 reshape.472
  9.8 0.3 reshape.470
  10.1 0.7 copy.76
  10.8 1.0 copy-done.3
  11.8 0.5 fusion.12
  12.2 1.8 %convolution_add_fusion = f32[2,4,128,128]{3,2,1,0:T(8,128)S(1)} fusion(f32[2,4,128,128]{3,2,1,0:T(8,128)S(1)} %fusion.12, bf16[2,512,4,128]{1,3,2,0:T(8,128)(2,1)} %copy-done.3, f32[2,512,4]{1,2,0:T(4,128)S(1)} %get-tuple-element.40, bf16[2,512,4,128]{3,2,1,0:T(4,128)(2,1)S(1)} %reshape.472), kind=kOutput, calls=%fused_computation.19 | convolution fusion | flops 137494528 | bytes 3162112 | tf_op jit(solution)/shard_map/bshd,bshe->bhde/dot_general | solution.py:52
  14.0 0.1 fusion.44
  14.3 2.5 %collective-permute-start = (bf16[4,136,128]{2,1,0:T(8,128)(2,1)S(1)}, bf16[4,136,128]{2,1,0:T(8,128)(2,1)S(1)}, u32[]{:S(2)}, u32[]{:S(2)}) collective-permute-start(bf16[4,136,128]{2,1,0:T(8,128)(2,1)S(1)} %pad_maximum_fusion.1), channel_id=1, source_target_pairs={{0,8},{8,0},{16,24},{24,16},{32,40},{40,32},{48,56},{56,48},{64,72... | collective-permute-start | bytes 417800 | tf_op jit(solution)/shard_map/ppermute | solution.py:34
  16.8 2.4 %collective-permute-done = bf16[4,136,128]{2,1,0:T(8,128)(2,1)S(1)} collective-permute-done((bf16[4,136,128]{2,1,0:T(8,128)(2,1)S(1)}, bf16[4,136,128]{2,1,0:T(8,128)(2,1)S(1)}, u32[]{:S(2)}, u32[]{:S(2)}) %collective-permute-start) | collective-permute-done | bytes 139296 | tf_op jit(solution)/shard_map/ppermute | solution.py:34
  19.3 0.1 exponential_reduce_fusion
  19.4 0.1 copy.81
  19.5 0.1 copy.82
  19.7 0.2 fusion.48
  20.0 4.9 %collective-permute-start.1 = (bf16[4,136,128]{2,1,0:T(8,128)(2,1)S(1)}, bf16[4,136,128]{2,1,0:T(8,128)(2,1)S(1)}, u32[]{:S(2)}, u32[]{:S(2)}) collective-permute-start(bf16[4,136,128]{2,1,0:T(8,128)(2,1)S(1)} %pad_maximum_fusion.2), channel_id=1, source_target_pairs={{0,24},{8,16},{16,8},{24,0},{32,56},{40,48},{48,40},{56,32},{64,88... | collective-permute-start | bytes 417800 | tf_op jit(solution)/shard_map/ppermute | solution.py:34
  24.9 2.5 %collective-permute-done.1 = bf16[4,136,128]{2,1,0:T(8,128)(2,1)S(1)} collective-permute-done((bf16[4,136,128]{2,1,0:T(8,128)(2,1)S(1)}, bf16[4,136,128]{2,1,0:T(8,128)(2,1)S(1)}, u32[]{:S(2)}, u32[]{:S(2)}) %collective-permute-start.1) | collective-permute-done | bytes 139296 | tf_op jit(solution)/shard_map/ppermute | solution.py:34
  27.5 0.1 exponential_reduce_fusion.6
  27.6 0.1 copy.84
  27.9 0.1 fusion.45
  28.1 4.6 %collective-permute-start.2 = (bf16[4,136,128]{2,1,0:T(8,128)(2,1)S(1)}, bf16[4,136,128]{2,1,0:T(8,128)(2,1)S(1)}, u32[]{:S(2)}, u32[]{:S(2)}) collective-permute-start(bf16[4,136,128]{2,1,0:T(8,128)(2,1)S(1)} %pad_maximum_fusion.3), channel_id=1, source_target_pairs={{0,56},{8,48},{16,40},{24,32},{32,24},{40,16},{48,8},{56,0},{64,12... | collective-permute-start | bytes 417800 | tf_op jit(solution)/shard_map/ppermute | solution.py:34
  32.7 2.4 %collective-permute-done.2 = bf16[4,136,128]{2,1,0:T(8,128)(2,1)S(1)} collective-permute-done((bf16[4,136,128]{2,1,0:T(8,128)(2,1)S(1)}, bf16[4,136,128]{2,1,0:T(8,128)(2,1)S(1)}, u32[]{:S(2)}, u32[]{:S(2)}) %collective-permute-start.2) | collective-permute-done | bytes 139296 | tf_op jit(solution)/shard_map/ppermute | solution.py:34
  35.2 0.1 exponential_reduce_fusion.4
  35.3 0.1 copy.86
  35.4 0.1 copy.87
  35.6 0.2 fusion.46
  35.9 1.4 collective-permute-start.3
  37.3 2.8 %collective-permute-done.3 = bf16[4,136,128]{2,1,0:T(8,128)(2,1)S(1)} collective-permute-done((bf16[4,136,128]{2,1,0:T(8,128)(2,1)S(1)}, bf16[4,136,128]{2,1,0:T(8,128)(2,1)S(1)}, u32[]{:S(2)}, u32[]{:S(2)}) %collective-permute-start.3) | collective-permute-done | bytes 139296 | tf_op jit(solution)/shard_map/ppermute | solution.py:34
  40.1 0.1 fusion.36
  40.3 0.1 copy.88
  40.4 0.1 copy.89
  40.5 0.1 select_convert_fusion
  40.8 3.0 %collective-permute-start.4 = (bf16[4,136,128]{2,1,0:T(8,128)(2,1)S(1)}, bf16[4,136,128]{2,1,0:T(8,128)(2,1)S(1)}, u32[]{:S(2)}, u32[]{:S(2)}) collective-permute-start(bf16[4,136,128]{2,1,0:T(8,128)(2,1)S(1)} %pad_maximum_fusion.5), channel_id=1, source_target_pairs={{0,192},{8,200},{16,208},{24,216},{32,224},{40,232},{48,240},{56,2... | collective-permute-start | bytes 417800 | tf_op jit(solution)/shard_map/ppermute | solution.py:34
  43.7 1.3 reshape.469
  45.2 1.0 collective-permute-done.4
  46.2 0.3 add_bitcast_fusion
  46.4 0.5 fusion.25
  47.0 1.8 %fusion.27 = f32[2,4,128,512]{3,2,1,0:T(8,128)} fusion(bf16[2,512,4,128]{3,2,1,0:T(4,128)(2,1)S(1)} %reshape.469, f32[1,4,128,128]{3,2,1,0:T(8,128)S(1)} %get-tuple-element.24, f32[1,4,128,128]{3,2,1,0:T(8,128)S(1)} %bitcast.96), kind=kOutput, calls=%fused_computation.33 | convolution fusion | flops 134348800 | bytes 3670016 | tf_op jit(solution)/shard_map/bthd,bhde->bthe/dot_general | solution.py:52
  48.8 7.3 %multiply_reduce_fusion = (f32[2,512,4]{1,2,0:T(4,128)S(1)}, f32[2,512,4,128]{1,3,2,0:T(8,128)}) fusion(f32[2,4,128,512]{3,2,1,0:T(8,128)} %fusion.27, f32[2,4,128,512]{3,2,1,0:T(8,128)S(1)} %fusion.25, f32[2,512,4]{1,2,0:T(4,128)S(1)} %get-tuple-element.39, bf16[2,512,4,128]{3,2,1,0:T(4,128)(2,1)} %copy-done.2, f32[2,4,512]{2,1,0:T(4,128)S(1)} %bitcast.102, ...), kind=kOutput, calls=%fused_computation.14 | convolution fusion | flops 1084747776 | bytes 9748480 | tf_op jit(solution)/shard_map/bhts,bshd->bthd/dot_general | solution.py:97
  56.1 0.2 copy.95
  56.3 2.0 %copy.94 = f32[2,512,4,128]{3,2,1,0:T(4,128)S(1)} copy(f32[2,512,4,128]{1,3,2,0:T(8,128)} %get-tuple-element.48) | data formatting | bytes 4194304 | tf_op jit(solution)/shard_map/add | solution.py:103
  58.4 1.2 mul.237
  59.7 12.5 %convolution_convert_fusion = bf16[1024,6144]{1,0:T(8,128)(2,1)} fusion(bf16[512,6144]{1,0:T(8,128)(2,1)} %param.13, f32[128,8,4,128]{3,2,1,0:T(4,128)S(1)} %bitcast.97, f32[128,8,4,128]{3,2,1,0:T(4,128)S(1)} %bitcast.98, bf16[1024,512]{1,0:T(8,128)(2,1)S(1)} %copy-done.4, f32[512]{0:T(512)S(1)} %copy-done.5), kind=kOutput, calls=%fused_computation | convolution fusion | flops 6452936704 | bytes 24119296 | tf_op jit(solution)/shard_map/dot_general | solution.py:110
  72.2 81.6 %reduce-scatter.2.cloned.1.call-done = bf16[128,6144]{1,0:T(8,128)(2,1)} async-done(((bf16[1024,6144]{1,0:T(8,128)(2,1)}), bf16[128,6144]{1,0:T(8,128)(2,1)}) %reduce-scatter.2.cloned.1.call-update) | async-done | bytes 1572880 | tf_op jit(solution)/shard_map/reduce_scatter | solution.py:109
  (49 shorter events, 1.5 us)
Async XLA Ops:
  6.5 0.7 copy-start
  6.5 3.2 %copy-start.1 = (bf16[1024,512]{1,0:T(8,128)(2,1)S(1)}, bf16[1024,512]{1,0:T(8,128)(2,1)}, u32[]{:S(2)}) copy-start(bf16[1024,512]{1,0:T(8,128)(2,1)} %param.8) | copy-start | bytes 3145732
  6.5 147.2 %reduce-scatter.2.cloned.1.call-start = ((), (), s32[]{:S(2)}) async-start(), calls=%async_computation.1 | async-start | bytes 14155776 | tf_op jit(solution)/shard_map/reduce_scatter | solution.py:109
  9.8 7.0 %copy-start.2 = (bf16[2,512,4,128]{3,2,1,0:T(4,128)(2,1)}, bf16[2,512,4,128]{3,2,1,0:T(4,128)(2,1)S(1)}, u32[]{:S(2)}) copy-start(bf16[2,512,4,128]{3,2,1,0:T(4,128)(2,1)S(1)} %reshape.472) | copy-start | bytes 3145732
  10.8 1.0 copy-start.3
  14.3 5.0 %collective-permute-start = (bf16[4,136,128]{2,1,0:T(8,128)(2,1)S(1)}, bf16[4,136,128]{2,1,0:T(8,128)(2,1)S(1)}, u32[]{:S(2)}, u32[]{:S(2)}) collective-permute-start(bf16[4,136,128]{2,1,0:T(8,128)(2,1)S(1)} %pad_maximum_fusion.1), channel_id=1, source_target_pairs={{0,8},{8,0},{16,24},{24,16},{32,40},{40,32},{48,56},{56,48},{64,72... | collective-permute-start | bytes 417800 | tf_op jit(solution)/shard_map/ppermute | solution.py:34
  20.0 7.5 %collective-permute-start.1 = (bf16[4,136,128]{2,1,0:T(8,128)(2,1)S(1)}, bf16[4,136,128]{2,1,0:T(8,128)(2,1)S(1)}, u32[]{:S(2)}, u32[]{:S(2)}) collective-permute-start(bf16[4,136,128]{2,1,0:T(8,128)(2,1)S(1)} %pad_maximum_fusion.2), channel_id=1, source_target_pairs={{0,24},{8,16},{16,8},{24,0},{32,56},{40,48},{48,40},{56,32},{64,88... | collective-permute-start | bytes 417800 | tf_op jit(solution)/shard_map/ppermute | solution.py:34
  28.1 7.0 %collective-permute-start.2 = (bf16[4,136,128]{2,1,0:T(8,128)(2,1)S(1)}, bf16[4,136,128]{2,1,0:T(8,128)(2,1)S(1)}, u32[]{:S(2)}, u32[]{:S(2)}) collective-permute-start(bf16[4,136,128]{2,1,0:T(8,128)(2,1)S(1)} %pad_maximum_fusion.3), channel_id=1, source_target_pairs={{0,56},{8,48},{16,40},{24,32},{32,24},{40,16},{48,8},{56,0},{64,12... | collective-permute-start | bytes 417800 | tf_op jit(solution)/shard_map/ppermute | solution.py:34
  35.9 4.2 %collective-permute-start.3 = (bf16[4,136,128]{2,1,0:T(8,128)(2,1)S(1)}, bf16[4,136,128]{2,1,0:T(8,128)(2,1)S(1)}, u32[]{:S(2)}, u32[]{:S(2)}) collective-permute-start(bf16[4,136,128]{2,1,0:T(8,128)(2,1)S(1)} %pad_maximum_fusion.4), channel_id=1, source_target_pairs={{0,64},{8,72},{16,80},{24,88},{32,96},{40,104},{48,112},{56,120},{... | collective-permute-start | bytes 417800 | tf_op jit(solution)/shard_map/ppermute | solution.py:34
  40.8 5.4 %collective-permute-start.4 = (bf16[4,136,128]{2,1,0:T(8,128)(2,1)S(1)}, bf16[4,136,128]{2,1,0:T(8,128)(2,1)S(1)}, u32[]{:S(2)}, u32[]{:S(2)}) collective-permute-start(bf16[4,136,128]{2,1,0:T(8,128)(2,1)S(1)} %pad_maximum_fusion.5), channel_id=1, source_target_pairs={{0,192},{8,200},{16,208},{24,216},{32,224},{40,232},{48,240},{56,2... | collective-permute-start | bytes 417800 | tf_op jit(solution)/shard_map/ppermute | solution.py:34
  58.4 1.3 copy-start.4
  58.4 1.3 copy-start.5
Sparse Core Ops, SparseCore 0:
  72.3 81.4 reduce-scatter.1

commit v12 on v10

--- a/solution.py
+++ b/solution.py
@@ -61,7 +61,7 @@
     tail = jnp.exp(last[:, :, None] - cum)
     key_decayed = k.astype(jnp.float32) * tail.transpose(0, 2, 1)[:, :, :, None]
     block_state = jnp.einsum(
-        "bshd,bshe->bhde", key_decayed, v.astype(jnp.float32), precision=hp
+        "bshd,bshe->bhde", key_decayed, v.astype(jnp.float32), precision=lax.Precision.HIGH
     )
 
     carries = []
@@ -91,7 +91,7 @@
         [carries[b] + jnp.exp(offsets[b])[:, None, None] * incoming for b in range(blocks)]
     )
     carried = jnp.exp(cum).transpose(0, 2, 1)[:, :, :, None] * jnp.einsum(
-        "bthd,bhde->bthe", q.astype(jnp.float32), carry_all, precision=hp
+        "bthd,bhde->bthe", q.astype(jnp.float32), carry_all, precision=lax.Precision.HIGH
     )
     attn = (inside + carried).reshape(local_rows, head_count, head_width)
 

time: 153 us -> 152 us (level)
  no operation moved by 1% of the time
where the time goes in v12:
time: 152 us
  waiting for transfers between devices  87.2 us (57%)
  matrix products  22 us (14%)
  starting transfers between devices  16.4 us (11%)
  between operations  13.6 us (9%)
  local copies, waits for them, and re-layouts  9.96 us (7%)
  other arithmetic  2.36 us (2%)
    reduce_scatter x1, waiting for transfers between devices, on_device(): lax.psum_scatter(jnp.dot(normed, out_weight, preferred_element_type=jnp.f...  78.4 us
    ppermute x5, starting transfers between devices, exclusive_prefix(): lax.ppermute(pack(*block), axis, [(i, i ^ flip) for i in range(n)])  16.4 us
    dot_general x1, matrix products, on_device(): jnp.dot(normed, out_weight, preferred_element_type=jnp.float32)  11.9 us
    ppermute x5, waiting for transfers between devices, exclusive_prefix(): lax.ppermute(pack(*block), axis, [(i, i ^ flip) for i in range(n)])  8.8 us
    dot_general x1, matrix products, on_device(): jnp.einsum('bhts,bshd->bthd', weighted, v, preferred_element_type=jnp.flo...  6.42 us
  transfers between devices with their start and end apart: 6, of which 5 were waited for; matrix products, arithmetic and copies ran while one was open for 5% of the time, Pallas kernels for 0%

profile of v12, /device:TPU:1, one launch (start us, length us, event | category | flops | bytes accessed | tf_op | source)
XLA Modules:
  0.0 151.6 jit_solution(12180690127208763397)
XLA Ops:
  6.5 0.7 copy-done
  7.3 0.3 fusion.19
  7.5 0.2 slice_reduce_fusion
  7.7 0.2 exponential_reduce_fusion.12
  8.1 0.1 copy.70
  8.2 0.1 copy.69
  8.4 1.3 reshape.472
  9.8 0.3 reshape.470
  10.1 0.7 copy.67
  10.8 0.8 fusion.11
  11.6 0.1 fusion.39
  11.9 2.5 %collective-permute-start = (bf16[4,136,128]{2,1,0:T(8,128)(2,1)S(1)}, bf16[4,136,128]{2,1,0:T(8,128)(2,1)S(1)}, u32[]{:S(2)}, u32[]{:S(2)}) collective-permute-start(bf16[4,136,128]{2,1,0:T(8,128)(2,1)S(1)} %pad_maximum_fusion), channel_id=1, source_target_pairs={{0,8},{8,0},{16,24},{24,16},{32,40},{40,32},{48,56},{56,48},{64,72... | collective-permute-start | bytes 417800 | tf_op jit(solution)/shard_map/ppermute | solution.py:34
  14.5 2.4 %collective-permute-done = bf16[4,136,128]{2,1,0:T(8,128)(2,1)S(1)} collective-permute-done((bf16[4,136,128]{2,1,0:T(8,128)(2,1)S(1)}, bf16[4,136,128]{2,1,0:T(8,128)(2,1)S(1)}, u32[]{:S(2)}, u32[]{:S(2)}) %collective-permute-start) | collective-permute-done | bytes 139296 | tf_op jit(solution)/shard_map/ppermute | solution.py:34
  16.9 0.1 exponential_reduce_fusion
  17.1 0.1 copy.71
  17.2 0.1 copy.72
  17.3 0.1 maximum_maximum_fusion.1
  17.4 0.2 fusion.43
  17.6 4.9 %collective-permute-start.1 = (bf16[4,136,128]{2,1,0:T(8,128)(2,1)S(1)}, bf16[4,136,128]{2,1,0:T(8,128)(2,1)S(1)}, u32[]{:S(2)}, u32[]{:S(2)}) collective-permute-start(bf16[4,136,128]{2,1,0:T(8,128)(2,1)S(1)} %pad_maximum_fusion.1), channel_id=1, source_target_pairs={{0,24},{8,16},{16,8},{24,0},{32,56},{40,48},{48,40},{56,32},{64,88... | collective-permute-start | bytes 417800 | tf_op jit(solution)/shard_map/ppermute | solution.py:34
  22.5 2.5 %collective-permute-done.1 = bf16[4,136,128]{2,1,0:T(8,128)(2,1)S(1)} collective-permute-done((bf16[4,136,128]{2,1,0:T(8,128)(2,1)S(1)}, bf16[4,136,128]{2,1,0:T(8,128)(2,1)S(1)}, u32[]{:S(2)}, u32[]{:S(2)}) %collective-permute-start.1) | collective-permute-done | bytes 139296 | tf_op jit(solution)/shard_map/ppermute | solution.py:34
  25.1 0.1 exponential_reduce_fusion.6
  25.2 0.1 copy.74
  25.4 0.1 copy.75
  25.5 0.1 fusion.40
  25.8 4.6 %collective-permute-start.2 = (bf16[4,136,128]{2,1,0:T(8,128)(2,1)S(1)}, bf16[4,136,128]{2,1,0:T(8,128)(2,1)S(1)}, u32[]{:S(2)}, u32[]{:S(2)}) collective-permute-start(bf16[4,136,128]{2,1,0:T(8,128)(2,1)S(1)} %pad_maximum_fusion.2), channel_id=1, source_target_pairs={{0,56},{8,48},{16,40},{24,32},{32,24},{40,16},{48,8},{56,0},{64,12... | collective-permute-start | bytes 417800 | tf_op jit(solution)/shard_map/ppermute | solution.py:34
  30.3 2.4 %collective-permute-done.2 = bf16[4,136,128]{2,1,0:T(8,128)(2,1)S(1)} collective-permute-done((bf16[4,136,128]{2,1,0:T(8,128)(2,1)S(1)}, bf16[4,136,128]{2,1,0:T(8,128)(2,1)S(1)}, u32[]{:S(2)}, u32[]{:S(2)}) %collective-permute-start.2) | collective-permute-done | bytes 139296 | tf_op jit(solution)/shard_map/ppermute | solution.py:34
  32.8 0.1 exponential_reduce_fusion.4
  33.0 0.1 copy.76
  33.1 0.1 copy.77
  33.3 0.2 fusion.41
  33.5 1.4 collective-permute-start.3
  34.9 1.3 reshape.469
  36.4 1.4 collective-permute-done.3
  37.8 0.1 fusion.32
  37.9 0.1 copy.78
  38.0 0.1 copy.79
  38.1 0.1 maximum_maximum_fusion.4
  38.2 0.1 select_convert_fusion
  38.4 3.0 %collective-permute-start.4 = (bf16[4,136,128]{2,1,0:T(8,128)(2,1)S(1)}, bf16[4,136,128]{2,1,0:T(8,128)(2,1)S(1)}, u32[]{:S(2)}, u32[]{:S(2)}) collective-permute-start(bf16[4,136,128]{2,1,0:T(8,128)(2,1)S(1)} %pad_maximum_fusion.4), channel_id=1, source_target_pairs={{0,192},{8,200},{16,208},{24,216},{32,224},{40,232},{48,240},{56,2... | collective-permute-start | bytes 417800 | tf_op jit(solution)/shard_map/ppermute | solution.py:34
  41.4 6.4 %fusion = f32[2,4,512,128]{2,3,1,0:T(8,128)} fusion(f32[2,4,512]{2,1,0:T(4,128)S(1)} %bitcast.101, pred[512,512]{1,0:T(8,128)(4,1)S(1)} %iota_compare_fusion.1, bf16[2,512,4,128]{1,3,2,0:T(8,128)(2,1)} %copy-done.4, bf16[2,512,4,128]{3,2,1,0:T(4,128)(2,1)} %copy-done.3, bf16[2,512,4,128]{3,2,1,0:T(4,128)(2,1)S(1)} %reshape.469), kind=kOutput, calls=%fused_computation.2 | convolution fusion | flops 1082130432 | bytes 5521408 | tf_op jit(solution)/shard_map/bhts,bshd->bthd/dot_general | solution.py:88
  47.8 0.3 add_bitcast_fusion
  48.1 2.6 %multiply_reduce_fusion = (f32[2,512,4]{1,2,0:T(4,128)S(1)}, f32[2,512,4,128]{1,3,2,0:T(8,128)S(1)}) fusion(bf16[2,512,4,128]{3,2,1,0:T(4,128)(2,1)S(1)} %reshape.469, f32[1,4,128,128]{3,2,1,0:T(8,128)S(1)} %get-tuple-element.24, f32[1,4,128,128]{3,2,1,0:T(8,128)S(1)} %bitcast.97, f32[2,512,4]{1,2,0:T(4,128)S(1)} %get-tuple-element.42, ...), kind=kOutput, calls=%fused_computation.14 | convolution fusion | flops 404877312 | bytes 5799936 | tf_op jit(solution)/shard_map/bthd,bhde->bthe/dot_general | solution.py:93
  50.7 0.2 copy.83
  51.0 1.9 %copy.82 = f32[2,512,4,128]{3,2,1,0:T(4,128)} copy(f32[2,512,4,128]{1,3,2,0:T(8,128)S(1)} %get-tuple-element.48) | data formatting | bytes 4194304 | tf_op jit(solution)/shard_map/add | solution.py:96
  52.8 1.2 mul.237
  54.1 0.4 copy-done.1
  54.4 11.9 %convolution_convert_fusion = bf16[1024,6144]{1,0:T(8,128)(2,1)} fusion(bf16[512,6144]{1,0:T(8,128)(2,1)} %param.13, f32[128,8,4,128]{3,2,1,0:T(4,128)S(1)} %bitcast.95, f32[128,8,4,128]{3,2,1,0:T(4,128)S(1)} %bitcast.96, bf16[1024,512]{1,0:T(8,128)(2,1)} %param.10, f32[512]{0:T(512)S(1)} %copy-done.5), kind=kOutput, calls=%fused_computation | convolution fusion | flops 6452936704 | bytes 24119296 | tf_op jit(solution)/shard_map/dot_general | solution.py:103
  66.3 78.4 %reduce-scatter.2.cloned.1.call-done = bf16[128,6144]{1,0:T(8,128)(2,1)} async-done(((bf16[1024,6144]{1,0:T(8,128)(2,1)}), bf16[128,6144]{1,0:T(8,128)(2,1)}) %reduce-scatter.2.cloned.1.call-update) | async-done | bytes 1572880 | tf_op jit(solution)/shard_map/reduce_scatter | solution.py:102
  (47 shorter events, 1.2 us)
Async XLA Ops:
  6.5 0.7 copy-start
  6.5 3.2 %copy-start.2 = (bf16[1024,512]{1,0:T(8,128)(2,1)S(1)}, bf16[1024,512]{1,0:T(8,128)(2,1)}, u32[]{:S(2)}) copy-start(bf16[1024,512]{1,0:T(8,128)(2,1)} %param.8) | copy-start | bytes 3145732
  6.5 138.2 %reduce-scatter.2.cloned.1.call-start = ((), (), s32[]{:S(2)}) async-start(), calls=%async_computation.1 | async-start | bytes 14155776 | tf_op jit(solution)/shard_map/reduce_scatter | solution.py:102
  9.8 23.7 %copy-start.3 = (bf16[2,512,4,128]{3,2,1,0:T(4,128)(2,1)}, bf16[2,512,4,128]{3,2,1,0:T(4,128)(2,1)S(1)}, u32[]{:S(2)}) copy-start(bf16[2,512,4,128]{3,2,1,0:T(4,128)(2,1)S(1)} %reshape.472) | copy-start | bytes 3145732
  10.8 3.7 %copy-start.4 = (bf16[2,512,4,128]{1,3,2,0:T(8,128)(2,1)}, bf16[2,512,4,128]{1,3,2,0:T(8,128)(2,1)S(1)}, u32[]{:S(2)}) copy-start(bf16[2,512,4,128]{1,3,2,0:T(8,128)(2,1)S(1)} %copy.67) | copy-start | bytes 3145732
  11.9 5.0 %collective-permute-start = (bf16[4,136,128]{2,1,0:T(8,128)(2,1)S(1)}, bf16[4,136,128]{2,1,0:T(8,128)(2,1)S(1)}, u32[]{:S(2)}, u32[]{:S(2)}) collective-permute-start(bf16[4,136,128]{2,1,0:T(8,128)(2,1)S(1)} %pad_maximum_fusion), channel_id=1, source_target_pairs={{0,8},{8,0},{16,24},{24,16},{32,40},{40,32},{48,56},{56,48},{64,72... | collective-permute-start | bytes 417800 | tf_op jit(solution)/shard_map/ppermute | solution.py:34
  17.6 7.4 %collective-permute-start.1 = (bf16[4,136,128]{2,1,0:T(8,128)(2,1)S(1)}, bf16[4,136,128]{2,1,0:T(8,128)(2,1)S(1)}, u32[]{:S(2)}, u32[]{:S(2)}) collective-permute-start(bf16[4,136,128]{2,1,0:T(8,128)(2,1)S(1)} %pad_maximum_fusion.1), channel_id=1, source_target_pairs={{0,24},{8,16},{16,8},{24,0},{32,56},{40,48},{48,40},{56,32},{64,88... | collective-permute-start | bytes 417800 | tf_op jit(solution)/shard_map/ppermute | solution.py:34
  25.8 7.0 %collective-permute-start.2 = (bf16[4,136,128]{2,1,0:T(8,128)(2,1)S(1)}, bf16[4,136,128]{2,1,0:T(8,128)(2,1)S(1)}, u32[]{:S(2)}, u32[]{:S(2)}) collective-permute-start(bf16[4,136,128]{2,1,0:T(8,128)(2,1)S(1)} %pad_maximum_fusion.2), channel_id=1, source_target_pairs={{0,56},{8,48},{16,40},{24,32},{32,24},{40,16},{48,8},{56,0},{64,12... | collective-permute-start | bytes 417800 | tf_op jit(solution)/shard_map/ppermute | solution.py:34
  33.5 4.2 %collective-permute-start.3 = (bf16[4,136,128]{2,1,0:T(8,128)(2,1)S(1)}, bf16[4,136,128]{2,1,0:T(8,128)(2,1)S(1)}, u32[]{:S(2)}, u32[]{:S(2)}) collective-permute-start(bf16[4,136,128]{2,1,0:T(8,128)(2,1)S(1)} %pad_maximum_fusion.3), channel_id=1, source_target_pairs={{0,64},{8,72},{16,80},{24,88},{32,96},{40,104},{48,112},{56,120},{... | collective-permute-start | bytes 417800 | tf_op jit(solution)/shard_map/ppermute | solution.py:34
  38.4 9.4 %collective-permute-start.4 = (bf16[4,136,128]{2,1,0:T(8,128)(2,1)S(1)}, bf16[4,136,128]{2,1,0:T(8,128)(2,1)S(1)}, u32[]{:S(2)}, u32[]{:S(2)}) collective-permute-start(bf16[4,136,128]{2,1,0:T(8,128)(2,1)S(1)} %pad_maximum_fusion.4), channel_id=1, source_target_pairs={{0,192},{8,200},{16,208},{24,216},{32,224},{40,232},{48,240},{56,2... | collective-permute-start | bytes 417800 | tf_op jit(solution)/shard_map/ppermute | solution.py:34
  52.8 1.6 %copy-start.1 = (f32[2,512,4,128]{3,2,1,0:T(4,128)S(1)}, f32[2,512,4,128]{3,2,1,0:T(4,128)}, u32[]{:S(2)}) copy-start(f32[2,512,4,128]{3,2,1,0:T(4,128)} %copy.82) | copy-start | bytes 6291460
  52.8 1.6 %copy-start.5 = (f32[512]{0:T(512)S(1)}, f32[512]{0:T(512)}, u32[]{:S(2)}) copy-start(f32[512]{0:T(512)} %param.12) | copy-start | bytes 6148
Sparse Core Ops, SparseCore 0:
  66.5 78.2 reduce-scatter.1

commit v13 on v12

--- a/solution.py
+++ b/solution.py
@@ -54,8 +54,13 @@
     k = keys.reshape(blocks, width_blk, head_count, head_width)
     v = values.reshape(blocks, width_blk, head_count, head_width)
     decay = log_decay.reshape(head_count, blocks, width_blk).transpose(1, 0, 2)
-    upto = (jnp.arange(width_blk)[:, None] <= jnp.arange(width_blk)[None, :]).astype(jnp.float32)
-    cum = jnp.einsum("bhu,ut->bht", decay, upto, precision=hp)
+    upto = (jnp.arange(width_blk)[:, None] <= jnp.arange(width_blk)[None, :]).astype(jnp.bfloat16)
+    cum = 0.0
+    rest = decay
+    for _ in range(3):
+        part = rest.astype(jnp.bfloat16)
+        rest = rest - part.astype(jnp.float32)
+        cum = cum + jnp.einsum("bhu,ut->bht", part, upto, preferred_element_type=jnp.float32)
     last = cum[:, :, -1]
 
     tail = jnp.exp(last[:, :, None] - cum)

time: 152 us -> 154 us (1.013)
  matrix products: 22 us -> 24.7 us
    dot_general x1 -> x3, matrix products: 0.26 us -> 2.88 us  [on_device(): jnp.einsum('bhu,ut->bht', part, upto, preferred_element_type=jnp.float32)]
where the time goes in v13:
time: 154 us
  waiting for transfers between devices  87.2 us (57%)
  matrix products  24.7 us (16%)
  starting transfers between devices  16.4 us (11%)
  between operations  13.7 us (9%)
  local copies, waits for them, and re-layouts  9.22 us (6%)
  other arithmetic  2.36 us (2%)
    reduce_scatter x1, waiting for transfers between devices, on_device(): lax.psum_scatter(jnp.dot(normed, out_weight, preferred_element_type=jnp.f...  78.4 us
    ppermute x5, starting transfers between devices, exclusive_prefix(): lax.ppermute(pack(*block), axis, [(i, i ^ flip) for i in range(n)])  16.4 us
    dot_general x1, matrix products, on_device(): jnp.dot(normed, out_weight, preferred_element_type=jnp.float32)  11.9 us
    ppermute x5, waiting for transfers between devices, exclusive_prefix(): lax.ppermute(pack(*block), axis, [(i, i ^ flip) for i in range(n)])  8.8 us
    dot_general x1, matrix products, on_device(): jnp.einsum('bhts,bshd->bthd', weighted, v, preferred_element_type=jnp.flo...  6.46 us
  transfers between devices with their start and end apart: 6, of which 5 were waited for; matrix products, arithmetic and copies ran while one was open for 5% of the time, Pallas kernels for 0%

profile of v13, /device:TPU:1, one launch (start us, length us, event | category | flops | bytes accessed | tf_op | source)
XLA Modules:
  0.0 153.5 jit_solution(6048290877315015032)
XLA Ops:
  6.5 1.0 fusion.21
  7.5 0.9 fusion.23
  8.4 1.0 fusion.35
  9.4 0.2 slice_reduce_fusion
  9.6 0.2 exponential_reduce_fusion.12
  10.0 0.1 copy.70
  10.1 0.1 copy.69
  10.2 1.3 reshape.472
  11.6 0.3 reshape.470
  11.9 0.7 copy.67
  12.6 0.1 subtract_exponential_fusion
  12.7 0.8 fusion.11
  13.5 0.1 fusion.48
  13.8 2.5 %collective-permute-start = (bf16[4,136,128]{2,1,0:T(8,128)(2,1)S(1)}, bf16[4,136,128]{2,1,0:T(8,128)(2,1)S(1)}, u32[]{:S(2)}, u32[]{:S(2)}) collective-permute-start(bf16[4,136,128]{2,1,0:T(8,128)(2,1)S(1)} %pad_maximum_fusion), channel_id=1, source_target_pairs={{0,8},{8,0},{16,24},{24,16},{32,40},{40,32},{48,56},{56,48},{64,72... | collective-permute-start | bytes 417800 | tf_op jit(solution)/shard_map/ppermute | solution.py:34
  16.3 2.4 %collective-permute-done = bf16[4,136,128]{2,1,0:T(8,128)(2,1)S(1)} collective-permute-done((bf16[4,136,128]{2,1,0:T(8,128)(2,1)S(1)}, bf16[4,136,128]{2,1,0:T(8,128)(2,1)S(1)}, u32[]{:S(2)}, u32[]{:S(2)}) %collective-permute-start) | collective-permute-done | bytes 139296 | tf_op jit(solution)/shard_map/ppermute | solution.py:34
  18.8 0.1 exponential_reduce_fusion
  19.0 0.1 copy.71
  19.1 0.1 copy.72
  19.3 0.2 fusion.52
  19.5 4.9 %collective-permute-start.1 = (bf16[4,136,128]{2,1,0:T(8,128)(2,1)S(1)}, bf16[4,136,128]{2,1,0:T(8,128)(2,1)S(1)}, u32[]{:S(2)}, u32[]{:S(2)}) collective-permute-start(bf16[4,136,128]{2,1,0:T(8,128)(2,1)S(1)} %pad_maximum_fusion.1), channel_id=1, source_target_pairs={{0,24},{8,16},{16,8},{24,0},{32,56},{40,48},{48,40},{56,32},{64,88... | collective-permute-start | bytes 417800 | tf_op jit(solution)/shard_map/ppermute | solution.py:34
  24.4 2.5 %collective-permute-done.1 = bf16[4,136,128]{2,1,0:T(8,128)(2,1)S(1)} collective-permute-done((bf16[4,136,128]{2,1,0:T(8,128)(2,1)S(1)}, bf16[4,136,128]{2,1,0:T(8,128)(2,1)S(1)}, u32[]{:S(2)}, u32[]{:S(2)}) %collective-permute-start.1) | collective-permute-done | bytes 139296 | tf_op jit(solution)/shard_map/ppermute | solution.py:34
  27.0 0.1 exponential_reduce_fusion.6
  27.1 0.1 copy.74
  27.2 0.1 copy.75
  27.4 0.1 fusion.49
  27.7 4.6 %collective-permute-start.2 = (bf16[4,136,128]{2,1,0:T(8,128)(2,1)S(1)}, bf16[4,136,128]{2,1,0:T(8,128)(2,1)S(1)}, u32[]{:S(2)}, u32[]{:S(2)}) collective-permute-start(bf16[4,136,128]{2,1,0:T(8,128)(2,1)S(1)} %pad_maximum_fusion.2), channel_id=1, source_target_pairs={{0,56},{8,48},{16,40},{24,32},{32,24},{40,16},{48,8},{56,0},{64,12... | collective-permute-start | bytes 417800 | tf_op jit(solution)/shard_map/ppermute | solution.py:34
  32.2 2.4 %collective-permute-done.2 = bf16[4,136,128]{2,1,0:T(8,128)(2,1)S(1)} collective-permute-done((bf16[4,136,128]{2,1,0:T(8,128)(2,1)S(1)}, bf16[4,136,128]{2,1,0:T(8,128)(2,1)S(1)}, u32[]{:S(2)}, u32[]{:S(2)}) %collective-permute-start.2) | collective-permute-done | bytes 139296 | tf_op jit(solution)/shard_map/ppermute | solution.py:34
  34.7 0.1 exponential_reduce_fusion.4
  34.9 0.1 copy.76
  35.0 0.1 copy.77
  35.2 0.2 fusion.50
  35.4 1.4 collective-permute-start.3
  36.8 1.3 reshape.469
  38.3 1.4 collective-permute-done.3
  39.6 0.1 fusion.40
  39.8 0.1 copy.78
  39.9 0.1 copy.79
  40.1 0.1 select_convert_fusion
  40.3 3.0 %collective-permute-start.4 = (bf16[4,136,128]{2,1,0:T(8,128)(2,1)S(1)}, bf16[4,136,128]{2,1,0:T(8,128)(2,1)S(1)}, u32[]{:S(2)}, u32[]{:S(2)}) collective-permute-start(bf16[4,136,128]{2,1,0:T(8,128)(2,1)S(1)} %pad_maximum_fusion.4), channel_id=1, source_target_pairs={{0,192},{8,200},{16,208},{24,216},{32,224},{40,232},{48,240},{56,2... | collective-permute-start | bytes 417800 | tf_op jit(solution)/shard_map/ppermute | solution.py:34
  43.3 6.5 %fusion = f32[2,4,512,128]{2,3,1,0:T(8,128)} fusion(f32[2,4,512]{2,1,0:T(4,128)S(1)} %get-tuple-element.47, pred[512,512]{1,0:T(8,128)(4,1)S(1)} %iota_compare_fusion.1, bf16[2,512,4,128]{1,3,2,0:T(8,128)(2,1)} %copy-done.3, bf16[2,512,4,128]{3,2,1,0:T(4,128)(2,1)} %copy-done.2, bf16[2,512,4,128]{3,2,1,0:T(4,128)(2,1)S(1)} %reshape.469), kind=kOutput, calls=%fused_computation.2 | convolution fusion | flops 1082130432 | bytes 5521408 | tf_op jit(solution)/shard_map/bhts,bshd->bthd/dot_general | solution.py:93
  49.8 0.3 add_bitcast_fusion
  50.0 2.6 %multiply_reduce_fusion = (f32[2,512,4]{1,2,0:T(4,128)S(1)}, f32[2,512,4,128]{1,3,2,0:T(8,128)S(1)}) fusion(bf16[2,512,4,128]{3,2,1,0:T(4,128)(2,1)S(1)} %reshape.469, f32[1,4,128,128]{3,2,1,0:T(8,128)S(1)} %get-tuple-element.24, f32[1,4,128,128]{3,2,1,0:T(8,128)S(1)} %bitcast.118, f32[2,512,4]{1,2,0:T(4,128)S(1)} %get-tuple-element.40, ...), kind=kOutput, calls=%fused_computation.14 | convolution fusion | flops 404877312 | bytes 5799936 | tf_op jit(solution)/shard_map/bthd,bhde->bthe/dot_general | solution.py:98
  52.6 0.2 copy.83
  52.9 1.9 %copy.82 = f32[2,512,4,128]{3,2,1,0:T(4,128)} copy(f32[2,512,4,128]{1,3,2,0:T(8,128)S(1)} %get-tuple-element.50) | data formatting | bytes 4194304 | tf_op jit(solution)/shard_map/add | solution.py:101
  54.8 1.2 mul.237
  56.0 0.4 copy-done
  56.3 11.9 %convolution_convert_fusion = bf16[1024,6144]{1,0:T(8,128)(2,1)} fusion(bf16[512,6144]{1,0:T(8,128)(2,1)} %param.13, f32[128,8,4,128]{3,2,1,0:T(4,128)S(1)} %bitcast.116, f32[128,8,4,128]{3,2,1,0:T(4,128)S(1)} %bitcast.117, bf16[1024,512]{1,0:T(8,128)(2,1)} %param.10, f32[512]{0:T(512)S(1)} %copy-done.4), kind=kOutput, calls=%fused_computation | convolution fusion | flops 6452936704 | bytes 24119296 | tf_op jit(solution)/shard_map/dot_general | solution.py:108
  68.3 78.4 %reduce-scatter.2.cloned.1.call-done = bf16[128,6144]{1,0:T(8,128)(2,1)} async-done(((bf16[1024,6144]{1,0:T(8,128)(2,1)}), bf16[128,6144]{1,0:T(8,128)(2,1)}) %reduce-scatter.2.cloned.1.call-update) | async-done | bytes 1572880 | tf_op jit(solution)/shard_map/reduce_scatter | solution.py:107
  (47 shorter events, 1.3 us)
Async XLA Ops:
  6.5 5.1 %copy-start.1 = (bf16[1024,512]{1,0:T(8,128)(2,1)S(1)}, bf16[1024,512]{1,0:T(8,128)(2,1)}, u32[]{:S(2)}) copy-start(bf16[1024,512]{1,0:T(8,128)(2,1)} %param.8) | copy-start | bytes 3145732
  6.5 140.1 %reduce-scatter.2.cloned.1.call-start = ((), (), s32[]{:S(2)}) async-start(), calls=%async_computation.1 | async-start | bytes 14155776 | tf_op jit(solution)/shard_map/reduce_scatter | solution.py:107
  11.6 23.7 %copy-start.2 = (bf16[2,512,4,128]{3,2,1,0:T(4,128)(2,1)}, bf16[2,512,4,128]{3,2,1,0:T(4,128)(2,1)S(1)}, u32[]{:S(2)}) copy-start(bf16[2,512,4,128]{3,2,1,0:T(4,128)(2,1)S(1)} %reshape.472) | copy-start | bytes 3145732
  12.6 3.8 %copy-start.3 = (bf16[2,512,4,128]{1,3,2,0:T(8,128)(2,1)}, bf16[2,512,4,128]{1,3,2,0:T(8,128)(2,1)S(1)}, u32[]{:S(2)}) copy-start(bf16[2,512,4,128]{1,3,2,0:T(8,128)(2,1)S(1)} %copy.67) | copy-start | bytes 3145732
  13.8 5.0 %collective-permute-start = (bf16[4,136,128]{2,1,0:T(8,128)(2,1)S(1)}, bf16[4,136,128]{2,1,0:T(8,128)(2,1)S(1)}, u32[]{:S(2)}, u32[]{:S(2)}) collective-permute-start(bf16[4,136,128]{2,1,0:T(8,128)(2,1)S(1)} %pad_maximum_fusion), channel_id=1, source_target_pairs={{0,8},{8,0},{16,24},{24,16},{32,40},{40,32},{48,56},{56,48},{64,72... | collective-permute-start | bytes 417800 | tf_op jit(solution)/shard_map/ppermute | solution.py:34
  19.5 7.4 %collective-permute-start.1 = (bf16[4,136,128]{2,1,0:T(8,128)(2,1)S(1)}, bf16[4,136,128]{2,1,0:T(8,128)(2,1)S(1)}, u32[]{:S(2)}, u32[]{:S(2)}) collective-permute-start(bf16[4,136,128]{2,1,0:T(8,128)(2,1)S(1)} %pad_maximum_fusion.1), channel_id=1, source_target_pairs={{0,24},{8,16},{16,8},{24,0},{32,56},{40,48},{48,40},{56,32},{64,88... | collective-permute-start | bytes 417800 | tf_op jit(solution)/shard_map/ppermute | solution.py:34
  27.7 7.0 %collective-permute-start.2 = (bf16[4,136,128]{2,1,0:T(8,128)(2,1)S(1)}, bf16[4,136,128]{2,1,0:T(8,128)(2,1)S(1)}, u32[]{:S(2)}, u32[]{:S(2)}) collective-permute-start(bf16[4,136,128]{2,1,0:T(8,128)(2,1)S(1)} %pad_maximum_fusion.2), channel_id=1, source_target_pairs={{0,56},{8,48},{16,40},{24,32},{32,24},{40,16},{48,8},{56,0},{64,12... | collective-permute-start | bytes 417800 | tf_op jit(solution)/shard_map/ppermute | solution.py:34
  35.4 4.2 %collective-permute-start.3 = (bf16[4,136,128]{2,1,0:T(8,128)(2,1)S(1)}, bf16[4,136,128]{2,1,0:T(8,128)(2,1)S(1)}, u32[]{:S(2)}, u32[]{:S(2)}) collective-permute-start(bf16[4,136,128]{2,1,0:T(8,128)(2,1)S(1)} %pad_maximum_fusion.3), channel_id=1, source_target_pairs={{0,64},{8,72},{16,80},{24,88},{32,96},{40,104},{48,112},{56,120},{... | collective-permute-start | bytes 417800 | tf_op jit(solution)/shard_map/ppermute | solution.py:34
  40.3 9.5 %collective-permute-start.4 = (bf16[4,136,128]{2,1,0:T(8,128)(2,1)S(1)}, bf16[4,136,128]{2,1,0:T(8,128)(2,1)S(1)}, u32[]{:S(2)}, u32[]{:S(2)}) collective-permute-start(bf16[4,136,128]{2,1,0:T(8,128)(2,1)S(1)} %pad_maximum_fusion.4), channel_id=1, source_target_pairs={{0,192},{8,200},{16,208},{24,216},{32,224},{40,232},{48,240},{56,2... | collective-permute-start | bytes 417800 | tf_op jit(solution)/shard_map/ppermute | solution.py:34
  54.7 1.6 %copy-start = (f32[2,512,4,128]{3,2,1,0:T(4,128)S(1)}, f32[2,512,4,128]{3,2,1,0:T(4,128)}, u32[]{:S(2)}) copy-start(f32[2,512,4,128]{3,2,1,0:T(4,128)} %copy.82) | copy-start | bytes 6291460
  54.7 1.6 %copy-start.4 = (f32[512]{0:T(512)S(1)}, f32[512]{0:T(512)}, u32[]{:S(2)}) copy-start(f32[512]{0:T(512)} %param.12) | copy-start | bytes 6148
Sparse Core Ops, SparseCore 0:
  68.4 78.2 reduce-scatter.1
